TPU v7x, 128 devices: a whole 4x4x4 slice. The times are simulated.
128 devices in a mesh: dom: 64 (over z, y, x), col: 2 (over core).
Axes of the slice: x: 4, y: 4, z: 4, core: 2. Of those that a mesh axis runs over, the one named last changes fastest.
Arguments:
- features: bfloat16 [196608, 1024], P('dom', 'col'), may hold values from -6 to 6
- block_type: int32 [1536], P('dom'), may hold values from 0 to 2
- rel_weight: bfloat16 [16, 1024, 1024], P(None, None, 'col'), may hold values from -0.1875 to 0.1875
- self_weight: bfloat16 [3, 1024, 1024], P(None, None, 'col'), may hold values from -0.1875 to 0.1875
- source_relation: int32 [64, 64, 2], P('dom'), may hold values from 0 to 15
- source_block: int32 [64, 64, 2], P('dom'), may hold values from 0 to 23
- target_relation: int32 [64, 64, 2], P('dom'), may hold values from 0 to 15, as said below
- target_block: int32 [64, 64, 2], P('dom'), may hold values from 0 to 23
- live: int32 [64, 64, 2], P('dom'), may hold values from 0 to 1, as said below
- tiles: int32 [64, 64, 2, 128, 128], P('dom'), may hold values 0 or 1
Outputs:
- updated: bfloat16 [196608, 1024], P('dom', 'col')
Inputs may be any that keep to these rules, and one draw needn't show every extreme that they name: For each destination q and source p, live[q, p, k] is 1 exactly for k below a count of 0 to 2; in every draw some destinations receive 2 live slots from every source. target_relation[q, p, k] equals source_relation[p, q, k].
All inputs are finite; a program needn't handle non-finite values. No bound on the sum of `tiles` on one device may be relied on, other than what follows from the above.
Results may differ from a plain program's by a relative error of at most 0.0034.
Values may be sent and summed in bfloat16 or wider, within the bound.
No kernel may reach another device: no remote copies, remote signals or barrier semaphores. Data moves between devices by JAX's collectives and lax.ppermute only.
A program may use at most 320 MiB of HBM per device.

v0:
```python
import jax
import jax.numpy as jnp
from jax import lax
from jax.sharding import PartitionSpec as P


def on_device(
    features,
    block_type,
    rel_weight,
    self_weight,
    source_relation,
    source_block,
    target_relation,
    target_block,
    live,
    tiles,
):
    blk_count = block_type.shape[0]
    rows_total = features.shape[0]
    col_width = features.shape[1]
    block_rows = rows_total // blk_count
    relations = rel_weight.shape[0]
    partitions = lax.axis_size("dom")
    capacity = live.shape[2]
    slots = live.shape[1] * capacity
    full_rows = lax.all_gather(features, "col", axis=1, tiled=True)
    full_blocks = full_rows.reshape(blk_count, block_rows, full_rows.shape[1])
    adjacency_int = (
        tiles.reshape(slots, block_rows, block_rows) * live.reshape(slots)[:, None, None]
    )
    adjacency = adjacency_int.astype(jnp.bfloat16)
    row_sums = jnp.sum(adjacency_int, axis=2).astype(jnp.float32)
    keys = target_relation.reshape(slots) * blk_count + target_block.reshape(slots)
    table = (keys[:, None] == jnp.arange(relations * blk_count)[None, :]).astype(jnp.float32)
    degree = jnp.dot(table.T, row_sums, precision=lax.Precision.HIGHEST)
    inverse = 1.0 / jnp.maximum(degree, 1.0)
    scale = jnp.dot(table, inverse, precision=lax.Precision.HIGHEST)

    def self_one(pair):
        return jnp.dot(pair[0], self_weight[pair[1]], preferred_element_type=jnp.float32)

    selfs = lax.map(self_one, (full_blocks, block_type), batch_size=8)
    picked = features.reshape(blk_count, block_rows, col_width)[source_block.reshape(slots)]
    arrived = lax.all_to_all(
        picked.reshape(partitions, capacity, block_rows, col_width),
        "dom",
        split_axis=0,
        concat_axis=0,
        tiled=True,
    )
    widened = lax.all_gather(
        arrived.reshape(slots, block_rows, col_width), "col", axis=2, tiled=True
    )

    def project_arrived(pair):
        return jnp.dot(pair[0], rel_weight[pair[1]], preferred_element_type=jnp.float32).astype(
            jnp.bfloat16
        )

    messages = lax.map(project_arrived, (widened, target_relation.reshape(slots)), batch_size=8)
    summed = jnp.einsum("sij,sjc->sic", adjacency, messages, preferred_element_type=jnp.float32)
    terms = scale[:, :, None] * summed
    total = jax.ops.segment_sum(terms, target_block.reshape(slots), num_segments=blk_count)
    return (total + selfs).reshape(rows_total, total.shape[2]).astype(jnp.bfloat16)


def solution(mesh):
    in_specs = (
        P("dom", "col"),
        P("dom"),
        P(None, None, "col"),
        P(None, None, "col"),
        P("dom", None, None),
        P("dom", None, None),
        P("dom", None, None),
        P("dom", None, None),
        P("dom", None, None),
        P("dom", None, None, None, None),
    )
    out_specs = P("dom", "col")
    return jax.shard_map(
        on_device, mesh=mesh, in_specs=in_specs, out_specs=out_specs, check_vma=False
    )
```

profile of v0, /device:TPU:4, one launch (start us, length us, event | category | flops | bytes accessed | tf_op | source)
XLA Modules:
  0.0 778.0 jit_solution(8290195940095522950)
XLA Ops:
  7.5 10.2 %gather_fusion.2 = bf16[128,128,512]{2,1,0:T(8,128)(2,1)} fusion(bf16[24,128,512]{2,1,0:T(8,128)(2,1)} %bitcast.79, s32[1024]{0:T(1024)S(1)} %pad_clamp_fusion), kind=kCustom, calls=%fused_computation.2 | custom fusion | bytes 33554944 | tf_op jit(solution)/shard_map/gather | solution.py:44
  17.6 11.7 %all-to-all-start = ((bf16[64,2,128,512]{3,2,1,0:T(8,128)(2,1)}), bf16[64,2,128,512]{3,2,1,0:T(8,128)(2,1)}, u32[]{:S(2)}, u32[]{:S(2)}) async-start(bf16[64,2,128,512]{3,2,1,0:T(8,128)(2,1)} %bitcast.80), calls=%async_computation | async-start | bytes 33554432 | tf_op jit(solution)/shard_map/all_to_all | solution.py:45
  30.1 265.0 %all-to-all-done = bf16[64,2,128,512]{3,2,1,0:T(8,128)(2,1)} async-done(((bf16[64,2,128,512]{3,2,1,0:T(8,128)(2,1)}), bf16[64,2,128,512]{3,2,1,0:T(8,128)(2,1)}, u32[]{:S(2)}, u32[]{:S(2)}) %all-to-all-start) | async-done | bytes 16777248 | tf_op jit(solution)/shard_map/all_to_all | solution.py:45
  302.3 23.3 %copy.29 = bf16[16,1024,512]{1,2,0:T(8,128)(2,1)} copy(bf16[16,1024,512]{2,1,0:T(8,128)(2,1)} %param.16) | data formatting | bytes 33554432 | tf_op jit(solution)/shard_map/while | solution.py:61
  339.7 39.5 %while.20 = (s32[]{:T(128)}, f32[3,8,128,512]{3,2,1,0:T(8,128)}, bf16[3,8,128,1024]{3,2,1,0:T(8,128)(2,1)}, s32[3,8]{1,0:T(4,128)S(1)}, bf16[3,1024,512]{1,2,0:T(8,128)(2,1)S(1)}, /*index=5*/s32[]{:T(128)}) while((s32[]{:T(128)}, f32[3,8,128,512]{3,2,1,0:T(8,128)}, bf16[3,8,128,1024]{3,2,1,0:T(8,128)(2,1)}, s32[3,8]{1,0:T(4,128)S(1)}, ...), condition=%wide.region_1.2_spmd, body=%wide.region_0.0_spmd.sunk | while | flops 1073741824 | bytes 29361384 | solution.py:43
  379.3 295.1 %while.21 = (s32[]{:T(128)}, bf16[16,8,128,512]{3,2,1,0:T(8,128)(2,1)}, bf16[16,8,128,1024]{3,2,1,0:T(8,128)(2,1)}, s32[16,8]{1,0:T(8,128)S(1)}, bf16[16,1024,512]{1,2,0:T(8,128)(2,1)}, /*index=5*/s32[]{:T(128)}) while((s32[]{:T(128)}, bf16[16,8,128,512]{3,2,1,0:T(8,128)(2,1)}, bf16[16,8,128,1024]{3,2,1,0:T(8,128)(2,1)}, ...), condition=%wide.region_4.5_spmd, body=%wide.region_3.4_spmd.sunk | while | flops 1074266112 | bytes 28312808 | solution.py:61
  379.3 10.4 %gather_fusion.1 = bf16[8,1024,512]{1,2,0:T(8,128)(2,1)} fusion(bf16[16,1024,512]{1,2,0:T(8,128)(2,1)} %get-tuple-element.197, s32[8]{0:T(128)S(1)} %shift-left_bitcast_fusion.5), kind=kCustom, calls=%fused_computation.1.clone.1 | custom fusion | bytes 16777312 | tf_op jit(solution)/shard_map/while/body/eval_jaxpr/vmap()/gather | solution.py:57
  397.6 10.4 %gather_fusion.1 = bf16[8,1024,512]{1,2,0:T(8,128)(2,1)} fusion(bf16[16,1024,512]{1,2,0:T(8,128)(2,1)} %get-tuple-element.197, s32[8]{0:T(128)S(1)} %shift-left_bitcast_fusion.5), kind=kCustom, calls=%fused_computation.1.clone.1 | custom fusion | bytes 16777312 | tf_op jit(solution)/shard_map/while/body/eval_jaxpr/vmap()/gather | solution.py:57
  416.0 10.5 %gather_fusion.1 = bf16[8,1024,512]{1,2,0:T(8,128)(2,1)} fusion(bf16[16,1024,512]{1,2,0:T(8,128)(2,1)} %get-tuple-element.197, s32[8]{0:T(128)S(1)} %shift-left_bitcast_fusion.5), kind=kCustom, calls=%fused_computation.1.clone.1 | custom fusion | bytes 16777312 | tf_op jit(solution)/shard_map/while/body/eval_jaxpr/vmap()/gather | solution.py:57
  434.5 10.5 %gather_fusion.1 = bf16[8,1024,512]{1,2,0:T(8,128)(2,1)} fusion(bf16[16,1024,512]{1,2,0:T(8,128)(2,1)} %get-tuple-element.197, s32[8]{0:T(128)S(1)} %shift-left_bitcast_fusion.5), kind=kCustom, calls=%fused_computation.1.clone.1 | custom fusion | bytes 16777312 | tf_op jit(solution)/shard_map/while/body/eval_jaxpr/vmap()/gather | solution.py:57
  452.9 10.5 %gather_fusion.1 = bf16[8,1024,512]{1,2,0:T(8,128)(2,1)} fusion(bf16[16,1024,512]{1,2,0:T(8,128)(2,1)} %get-tuple-element.197, s32[8]{0:T(128)S(1)} %shift-left_bitcast_fusion.5), kind=kCustom, calls=%fused_computation.1.clone.1 | custom fusion | bytes 16777312 | tf_op jit(solution)/shard_map/while/body/eval_jaxpr/vmap()/gather | solution.py:57
  471.4 10.4 %gather_fusion.1 = bf16[8,1024,512]{1,2,0:T(8,128)(2,1)} fusion(bf16[16,1024,512]{1,2,0:T(8,128)(2,1)} %get-tuple-element.197, s32[8]{0:T(128)S(1)} %shift-left_bitcast_fusion.5), kind=kCustom, calls=%fused_computation.1.clone.1 | custom fusion | bytes 16777312 | tf_op jit(solution)/shard_map/while/body/eval_jaxpr/vmap()/gather | solution.py:57
  489.8 10.5 %gather_fusion.1 = bf16[8,1024,512]{1,2,0:T(8,128)(2,1)} fusion(bf16[16,1024,512]{1,2,0:T(8,128)(2,1)} %get-tuple-element.197, s32[8]{0:T(128)S(1)} %shift-left_bitcast_fusion.5), kind=kCustom, calls=%fused_computation.1.clone.1 | custom fusion | bytes 16777312 | tf_op jit(solution)/shard_map/while/body/eval_jaxpr/vmap()/gather | solution.py:57
  508.2 10.5 %gather_fusion.1 = bf16[8,1024,512]{1,2,0:T(8,128)(2,1)} fusion(bf16[16,1024,512]{1,2,0:T(8,128)(2,1)} %get-tuple-element.197, s32[8]{0:T(128)S(1)} %shift-left_bitcast_fusion.5), kind=kCustom, calls=%fused_computation.1.clone.1 | custom fusion | bytes 16777312 | tf_op jit(solution)/shard_map/while/body/eval_jaxpr/vmap()/gather | solution.py:57
  526.7 10.5 %gather_fusion.1 = bf16[8,1024,512]{1,2,0:T(8,128)(2,1)} fusion(bf16[16,1024,512]{1,2,0:T(8,128)(2,1)} %get-tuple-element.197, s32[8]{0:T(128)S(1)} %shift-left_bitcast_fusion.5), kind=kCustom, calls=%fused_computation.1.clone.1 | custom fusion | bytes 16777312 | tf_op jit(solution)/shard_map/while/body/eval_jaxpr/vmap()/gather | solution.py:57
  545.2 10.5 %gather_fusion.1 = bf16[8,1024,512]{1,2,0:T(8,128)(2,1)} fusion(bf16[16,1024,512]{1,2,0:T(8,128)(2,1)} %get-tuple-element.197, s32[8]{0:T(128)S(1)} %shift-left_bitcast_fusion.5), kind=kCustom, calls=%fused_computation.1.clone.1 | custom fusion | bytes 16777312 | tf_op jit(solution)/shard_map/while/body/eval_jaxpr/vmap()/gather | solution.py:57
  563.7 10.5 %gather_fusion.1 = bf16[8,1024,512]{1,2,0:T(8,128)(2,1)} fusion(bf16[16,1024,512]{1,2,0:T(8,128)(2,1)} %get-tuple-element.197, s32[8]{0:T(128)S(1)} %shift-left_bitcast_fusion.5), kind=kCustom, calls=%fused_computation.1.clone.1 | custom fusion | bytes 16777312 | tf_op jit(solution)/shard_map/while/body/eval_jaxpr/vmap()/gather | solution.py:57
  582.1 10.4 %gather_fusion.1 = bf16[8,1024,512]{1,2,0:T(8,128)(2,1)} fusion(bf16[16,1024,512]{1,2,0:T(8,128)(2,1)} %get-tuple-element.197, s32[8]{0:T(128)S(1)} %shift-left_bitcast_fusion.5), kind=kCustom, calls=%fused_computation.1.clone.1 | custom fusion | bytes 16777312 | tf_op jit(solution)/shard_map/while/body/eval_jaxpr/vmap()/gather | solution.py:57
  600.5 10.5 %gather_fusion.1 = bf16[8,1024,512]{1,2,0:T(8,128)(2,1)} fusion(bf16[16,1024,512]{1,2,0:T(8,128)(2,1)} %get-tuple-element.197, s32[8]{0:T(128)S(1)} %shift-left_bitcast_fusion.5), kind=kCustom, calls=%fused_computation.1.clone.1 | custom fusion | bytes 16777312 | tf_op jit(solution)/shard_map/while/body/eval_jaxpr/vmap()/gather | solution.py:57
  619.1 10.5 %gather_fusion.1 = bf16[8,1024,512]{1,2,0:T(8,128)(2,1)} fusion(bf16[16,1024,512]{1,2,0:T(8,128)(2,1)} %get-tuple-element.197, s32[8]{0:T(128)S(1)} %shift-left_bitcast_fusion.5), kind=kCustom, calls=%fused_computation.1.clone.1 | custom fusion | bytes 16777312 | tf_op jit(solution)/shard_map/while/body/eval_jaxpr/vmap()/gather | solution.py:57
  637.5 10.5 %gather_fusion.1 = bf16[8,1024,512]{1,2,0:T(8,128)(2,1)} fusion(bf16[16,1024,512]{1,2,0:T(8,128)(2,1)} %get-tuple-element.197, s32[8]{0:T(128)S(1)} %shift-left_bitcast_fusion.5), kind=kCustom, calls=%fused_computation.1.clone.1 | custom fusion | bytes 16777312 | tf_op jit(solution)/shard_map/while/body/eval_jaxpr/vmap()/gather | solution.py:57
  655.9 10.5 %gather_fusion.1 = bf16[8,1024,512]{1,2,0:T(8,128)(2,1)} fusion(bf16[16,1024,512]{1,2,0:T(8,128)(2,1)} %get-tuple-element.197, s32[8]{0:T(128)S(1)} %shift-left_bitcast_fusion.5), kind=kCustom, calls=%fused_computation.1.clone.1 | custom fusion | bytes 16777312 | tf_op jit(solution)/shard_map/while/body/eval_jaxpr/vmap()/gather | solution.py:57
  674.3 19.7 %broadcast_multiply_fusion = f32[128,128,512]{2,1,0:T(8,128)} fusion(f32[128,128]{1,0:T(8,128)S(1)} %fusion.23, bf16[128,128,128]{2,1,0:T(8,128)(2,1)} %fusion.21, bf16[128,128,512]{2,1,0:T(8,128)(2,1)} %bitcast.81), kind=kOutput, calls=%fused_computation.24 | convolution fusion | flops 2155872256 | bytes 54591488 | tf_op jit(solution)/shard_map/sij,sjc->sic/dot_general | solution.py:62
  694.0 72.2 %scatter_fusion = f32[24,128,512]{2,1,0:T(8,128)} fusion(f32[24,128,512]{2,1,0:T(8,128)} %bitcast.78, s32[128]{0:T(128)S(1)} %reshape.167, f32[128,128,512]{2,1,0:T(8,128)} %broadcast_multiply_fusion), kind=kCustom, calls=%fused_computation.3 | custom fusion | flops 8388608 | bytes 100663808 | tf_op jit(solution)/shard_map/scatter-add | solution.py:64
  (79 shorter events, 194.7 us)
Async XLA Ops:
  17.6 277.4 %all-to-all-start = ((bf16[64,2,128,512]{3,2,1,0:T(8,128)(2,1)}), bf16[64,2,128,512]{3,2,1,0:T(8,128)(2,1)}, u32[]{:S(2)}, u32[]{:S(2)}) async-start(bf16[64,2,128,512]{3,2,1,0:T(8,128)(2,1)} %bitcast.80), calls=%async_computation | async-start | bytes 33554432 | tf_op jit(solution)/shard_map/all_to_all | solution.py:45
  29.3 310.4 %all-gather.3.cloned.1.call-start = ((), (), s32[]{:S(2)}) async-start(), calls=%async_computation.1 | async-start | bytes 9437184 | tf_op jit(solution)/shard_map/all_gather | solution.py:27
  30.0 349.2 %all-gather.5.cloned.1.call-start = ((), (), s32[]{:S(2)}) async-start(), calls=%async_computation.2 | async-start | bytes 50331648 | tf_op jit(solution)/shard_map/all_gather | solution.py:52
  295.1 0.7 copy-start.1
  295.1 0.8 copy-start
  295.1 1.1 copy-start.2
  302.3 27.7 %copy-start.3 = (s32[24]{0:T(128)S(1)}, s32[24]{0:T(128)}, u32[]{:S(2)}) copy-start(s32[24]{0:T(128)} %param.15) | copy-start | bytes 292
Sparse Core Ops, SparseCore 0:
  31.8 20.7 all-gather.2
  295.3 63.4 all-gather.4
where the time goes:
time: 789 us; the launch traced here: 778 us
  waiting for transfers between devices  266 us (34%)
  local copies, waits for them, and re-layouts  223 us (28%)
  matrix products  172 us (22%)
  other arithmetic  92 us (12%)
  between operations  13.5 us (2%)
  starting transfers between devices  11.7 us (1%)
    all_to_all x1, waiting for transfers between devices, on_device(): lax.all_to_all(picked.reshape(partitions, capacity, block_rows, col_width...  265 us
    gather x16, local copies, waits for them, and re-layouts, project_arrived(): rel_weight[pair[1]]  168 us
    dot_general x16, matrix products, project_arrived(): jnp.dot(pair[0], rel_weight[pair[1]], preferred_element_type=jnp.float32)  127 us
    scatter-add x1, other arithmetic, on_device(): jax.ops.segment_sum(terms, target_block.reshape(slots), num_segments=blk_...  72.2 us
    dot_general x3, matrix products, self_one(): jnp.dot(pair[0], self_weight[pair[1]], preferred_element_type=jnp.float32)  24.7 us
    while x1, local copies, waits for them, and re-layouts, on_device(): lax.map(project_arrived, (widened, target_relation.reshape(slots)), batch...  23.3 us
    dot_general x1, matrix products, on_device(): jnp.einsum('sij,sjc->sic', adjacency, messages, preferred_element_type=jn...  19.7 us
  transfers between devices with their start and end apart: 3, of which 1 were waited for; matrix products, arithmetic and copies ran while one was open for 11% of the time, Pallas kernels for 0%

commit v1 on v0

v1 whole, which is shorter than its diff:
```python
import functools

import jax
import jax.numpy as jnp
from jax import lax
from jax.experimental import pallas as pl
from jax.experimental.pallas import tpu as pltpu
from jax.sharding import PartitionSpec as P


def _bmm_kernel(dst_ref, src_ref, widx_ref, x_ref, w_ref, o_ref):
    o_ref[...] = jnp.dot(x_ref[...], w_ref[...], preferred_element_type=jnp.float32).astype(
        o_ref.dtype
    )


def _block_matmul(x, w, dst, src, widx, n_out, block_rows, out_dtype):
    k_dim = x.shape[1]
    n_dim = w.shape[2]
    steps = dst.shape[0]
    grid_spec = pltpu.PrefetchScalarGridSpec(
        num_scalar_prefetch=3,
        grid=(steps,),
        in_specs=[
            pl.BlockSpec((block_rows, k_dim), lambda s, d, r, g: (r[s], 0)),
            pl.BlockSpec((None, k_dim, n_dim), lambda s, d, r, g: (g[s], 0, 0)),
        ],
        out_specs=pl.BlockSpec((None, block_rows, n_dim), lambda s, d, r, g: (d[s], 0, 0)),
    )
    out_bytes = jnp.dtype(out_dtype).itemsize
    cost = pl.CostEstimate(
        flops=2 * steps * block_rows * k_dim * n_dim,
        bytes_accessed=steps * block_rows * (k_dim * 2 + n_dim * out_bytes) + w.size * 2,
        transcendentals=0,
    )
    return pl.pallas_call(
        _bmm_kernel,
        grid_spec=grid_spec,
        out_shape=jax.ShapeDtypeStruct((n_out, block_rows, n_dim), out_dtype),
        compiler_params=pltpu.CompilerParams(dimension_semantics=("arbitrary",)),
        cost_estimate=cost,
    )(dst, src, widx, x, w)


def _agg_kernel(tb_ref, live_ref, tiles_ref, msg_ref, inv_ref, acc_in_ref, acc_ref):
    s = pl.program_id(0)

    @pl.when(s == 0)
    def _():
        acc_ref[...] = acc_in_ref[...]

    block_rows = msg_ref.shape[0]
    adj = (tiles_ref[...] * live_ref[s]).astype(jnp.float32).astype(jnp.bfloat16)
    term = jnp.dot(adj, msg_ref[...], preferred_element_type=jnp.float32) * inv_ref[...]
    rows = pl.ds(pl.multiple_of(tb_ref[s] * block_rows, block_rows), block_rows)
    acc_ref[rows, :] += term


def _aggregate(acc, tiles, msgs, inv, tb, live, k):
    steps, block_rows, n_dim = msgs.shape
    rows = acc.shape[0]
    grid_spec = pltpu.PrefetchScalarGridSpec(
        num_scalar_prefetch=2,
        grid=(steps,),
        in_specs=[
            pl.BlockSpec((None, None, block_rows, block_rows), lambda s, t, l: (s, k, 0, 0)),
            pl.BlockSpec((None, block_rows, n_dim), lambda s, t, l: (s, 0, 0)),
            pl.BlockSpec((None, block_rows, 1), lambda s, t, l: (s, 0, 0)),
            pl.BlockSpec((rows, n_dim), lambda s, t, l: (0, 0)),
        ],
        out_specs=pl.BlockSpec((rows, n_dim), lambda s, t, l: (0, 0)),
    )
    cost = pl.CostEstimate(
        flops=2 * steps * block_rows * block_rows * n_dim,
        bytes_accessed=steps * block_rows * (block_rows * 4 + n_dim * 2 + 4) + 2 * rows * n_dim * 4,
        transcendentals=0,
    )
    return pl.pallas_call(
        _agg_kernel,
        grid_spec=grid_spec,
        out_shape=jax.ShapeDtypeStruct(acc.shape, jnp.float32),
        input_output_aliases={5: 0},
        compiler_params=pltpu.CompilerParams(
            dimension_semantics=("arbitrary",), vmem_limit_bytes=56 * 1024 * 1024
        ),
        cost_estimate=cost,
    )(tb, live, tiles, msgs, inv, acc)


def on_device(
    features,
    block_type,
    rel_weight,
    self_weight,
    source_relation,
    source_block,
    target_relation,
    target_block,
    live,
    tiles,
):
    blk_count = block_type.shape[0]
    rows_total = features.shape[0]
    block_rows = rows_total // blk_count
    relations = rel_weight.shape[0]
    partitions = live.shape[1]
    capacity = live.shape[2]
    slots = partitions * capacity

    full_rows = lax.all_gather(features, "col", axis=1, tiled=True)

    tiles4 = tiles.reshape(partitions, capacity, block_rows, block_rows)
    live2 = live.reshape(partitions, capacity)
    row_sums = (jnp.sum(tiles4, axis=3) * live2[:, :, None]).astype(jnp.float32)
    keys = target_relation.reshape(slots) * blk_count + target_block.reshape(slots)
    table = (keys[:, None] == jnp.arange(relations * blk_count)[None, :]).astype(jnp.float32)
    degree = jnp.dot(
        table.T, row_sums.reshape(slots, block_rows), precision=lax.Precision.HIGHEST
    )
    inverse = 1.0 / jnp.maximum(degree, 1.0)
    scale = jnp.dot(table, inverse, precision=lax.Precision.HIGHEST)
    scale = scale.reshape(partitions, capacity, block_rows, 1)

    src_blocks = source_block.reshape(partitions, capacity)
    src_rels = source_relation.reshape(partitions, capacity)
    dst_blocks = target_block.reshape(partitions, capacity)

    arrived = []
    for k in range(capacity):
        rel_k = src_rels[:, k]
        order = jnp.argsort(rel_k).astype(jnp.int32)
        msgs = _block_matmul(
            full_rows,
            rel_weight,
            order,
            src_blocks[:, k][order],
            rel_k[order],
            partitions,
            block_rows,
            jnp.bfloat16,
        )
        arrived.append(lax.all_to_all(msgs, "dom", split_axis=0, concat_axis=0, tiled=True))

    type_order = jnp.argsort(block_type).astype(jnp.int32)
    selfs = _block_matmul(
        full_rows,
        self_weight,
        type_order,
        type_order,
        block_type[type_order],
        blk_count,
        block_rows,
        jnp.float32,
    )
    acc = selfs.reshape(rows_total, selfs.shape[2])
    for k in range(capacity):
        acc = _aggregate(
            acc, tiles4, arrived[k], scale[:, k], dst_blocks[:, k], live2[:, k], k
        )
    return acc.astype(jnp.bfloat16)


def solution(mesh):
    in_specs = (
        P("dom", "col"),
        P("dom"),
        P(None, None, "col"),
        P(None, None, "col"),
        P("dom", None, None),
        P("dom", None, None),
        P("dom", None, None),
        P("dom", None, None),
        P("dom", None, None),
        P("dom", None, None, None, None),
    )
    out_specs = P("dom", "col")
    return jax.shard_map(
        on_device, mesh=mesh, in_specs=in_specs, out_specs=out_specs, check_vma=False
    )
```

time: 789 us -> 403 us (0.51)
  local copies, waits for them, and re-layouts: 223 us -> 14.4 us
  Pallas kernels: 0 us -> 204 us
  matrix products: 172 us -> 0.72 us
  waiting for transfers between devices: 266 us -> 131 us
  other arithmetic: 92 us -> 16.2 us
    pallas_call x0 -> x5, Pallas kernels: none -> 204 us  [the longest x3 119 us: _block_matmul(): pl.pallas_call(_bmm_kernel, grid_spec=grid_spec, out_shape=jax.ShapeDtype...]
    gather x20 -> x5, local copies, waits for them, and re-layouts: 193 us -> 6.53 us  [the longest x2 2.73 us: on_device(): src_blocks[:, k][order]]
    dot_general x21 -> x1, matrix products: 172 us -> 0.42 us  [on_device(): jnp.dot(table.T, row_sums.reshape(slots, block_rows), precision=lax.Preci...]
    all_to_all x1 -> x2, waiting for transfers between devices: 265 us -> 112 us  [on_device(): lax.all_to_all(msgs, 'dom', split_axis=0, concat_axis=0, tiled=True)]
    scatter-add x1 -> x0, other arithmetic: 72.2 us -> none  [on_device(): jax.ops.segment_sum(terms, target_block.reshape(slots), num_segments=blk_...]
    while x2 -> x0, local copies, waits for them, and re-layouts: 27.5 us -> none  [the longest x1 23.3 us: on_device(): lax.map(project_arrived, (widened, target_relation.reshape(slots)), batch...]
    all_gather x1, waiting for transfers between devices: 0.01 us -> 17.4 us  [on_device(): full_rows = lax.all_gather(features, 'col', axis=1, tiled=True)]
    convert_element_type x3 -> x1, other arithmetic: 13.8 us -> 4.85 us  [on_device(): return acc.astype(jnp.bfloat16)]
  transfers between devices with their start and end apart: 3 -> 3, of which waited for: 1 -> 3; matrix products, arithmetic and copies ran while one was open for 11% -> 7% of each run, Pallas kernels for 0% -> 28%
where the time goes in v1:
time: 403 us; the launch traced here: 397 us
  Pallas kernels  204 us (51%)
  waiting for transfers between devices  131 us (33%)
  starting transfers between devices  16.9 us (4%)
  other arithmetic  16.2 us (4%)
  local copies, waits for them, and re-layouts  14.4 us (4%)
  between operations  13.5 us (3%)
    pallas_call x3, Pallas kernels, _block_matmul(): pl.pallas_call(_bmm_kernel, grid_spec=grid_spec, out_shape=jax.ShapeDtype...  119 us
    all_to_all x2, waiting for transfers between devices, on_device(): lax.all_to_all(msgs, 'dom', split_axis=0, concat_axis=0, tiled=True)  112 us
    pallas_call x2, Pallas kernels, _aggregate(): pl.pallas_call(_agg_kernel, grid_spec=grid_spec, out_shape=jax.ShapeDtype...  85.4 us
    all_gather x1, waiting for transfers between devices, on_device(): full_rows = lax.all_gather(features, 'col', axis=1, tiled=True)  17.4 us
    all_to_all x2, starting transfers between devices, on_device(): lax.all_to_all(msgs, 'dom', split_axis=0, concat_axis=0, tiled=True)  16.9 us
  transfers between devices with their start and end apart: 3, of which 3 were waited for; matrix products, arithmetic and copies ran while one was open for 7% of the time, Pallas kernels for 28%

profile of v1, /device:TPU:4, one launch (start us, length us, event | category | flops | bytes accessed | tf_op | source)
XLA Modules:
  0.0 396.7 jit_solution(3832166245467742321)
XLA Ops:
  7.3 0.8 slice_bitcast_fusion.1
  8.0 2.0 sort.49
  10.1 1.3 gather_fusion.3
  11.3 0.8 slice_bitcast_fusion
  12.1 1.4 gather_fusion.2
  13.5 17.4 %all-gather.2.cloned.1.call-done.x_ref = bf16[3072,1024]{1,0:T(8,128)(2,1)} async-done(((bf16[3072,512]{1,0:T(8,128)(2,1)}), bf16[3072,1024]{1,0:T(8,128)(2,1)}) %all-gather.2.cloned.1.call-update) | async-done | bytes 6291472 | tf_op jit(solution)/shard_map/all_gather | solution.py:110
  30.9 49.8 %shard_map.101 = bf16[64,128,512]{2,1,0:T(8,128)(2,1)} custom-call(s32[64]{0:T(128)} %copy-done.5, s32[64]{0:T(128)} %gather_fusion.2, s32[64]{0:T(128)} %gather_fusion.3, bf16[3072,1024]{1,0:T(8,128)(2,1)} %all-gather.2.cloned.1.call-done.x_ref, bf16[16,1024,512]{2,1,0:T(8,128)(2,1)} %w_ref.4), custom_call_target="tpu_custom_call" | custom-call | flops 8589934592 | bytes 41943040 | tf_op jit(solution)/shard_map/pallas_call | solution.py:36
  80.7 10.4 %all-to-all-start.1 = ((bf16[64,128,512]{2,1,0:T(8,128)(2,1)}), bf16[64,128,512]{2,1,0:T(8,128)(2,1)}, u32[]{:S(2)}, u32[]{:S(2)}) async-start(bf16[64,128,512]{2,1,0:T(8,128)(2,1)} %shard_map.101), calls=%async_computation.1 | async-start | bytes 16777216 | tf_op jit(solution)/shard_map/all_to_all | solution.py:142
  91.2 2.0 sort.48
  93.2 1.3 gather_fusion.1
  94.6 1.4 gather_fusion
  95.9 49.7 %shard_map.100 = bf16[64,128,512]{2,1,0:T(8,128)(2,1)} custom-call(s32[64]{0:T(128)} %copy-done.6, s32[64]{0:T(128)} %gather_fusion, s32[64]{0:T(128)} %gather_fusion.1, bf16[3072,1024]{1,0:T(8,128)(2,1)} %all-gather.2.cloned.1.call-done.x_ref, bf16[16,1024,512]{2,1,0:T(8,128)(2,1)} %w_ref.4), custom_call_target="tpu_custom_call" | custom-call | flops 8589934592 | bytes 41943040 | tf_op jit(solution)/shard_map/pallas_call | solution.py:36
  145.6 73.0 %all-to-all-done.1.msg_ref = bf16[64,128,512]{2,1,0:T(8,128)(2,1)} async-done(((bf16[64,128,512]{2,1,0:T(8,128)(2,1)}), bf16[64,128,512]{2,1,0:T(8,128)(2,1)}, u32[]{:S(2)}, u32[]{:S(2)}) %all-to-all-start.1) | async-done | bytes 8388640 | tf_op jit(solution)/shard_map/all_to_all | solution.py:142
  218.6 6.4 %all-to-all-start = ((bf16[64,128,512]{2,1,0:T(8,128)(2,1)}), bf16[64,128,512]{2,1,0:T(8,128)(2,1)}, u32[]{:S(2)}, u32[]{:S(2)}) async-start(bf16[64,128,512]{2,1,0:T(8,128)(2,1)} %shard_map.100), calls=%async_computation | async-start | bytes 16777216 | tf_op jit(solution)/shard_map/all_to_all | solution.py:142
  225.1 1.6 sort.50
  226.7 1.2 gather_fusion.4
  228.4 5.7 %reduce_sum.11 = s32[64,2,128]{2,1,0:T(2,128)S(1)} reduce(s32[1,64,2,128,128]{4,3,2,1,0:T(8,128)} %param.19, s32[]{:T(128)} %constant.4.clone.1), dimensions={0,4}, to_apply=%region_1.0 | reduce | flops 2080768 | bytes 8454148 | tf_op jit(solution)/shard_map/reduce_sum | solution.py:114
  234.8 2.6 copy.22.inv_ref
  237.5 2.6 copy.23.inv_ref
  240.6 19.6 %shard_map.102 = f32[24,128,512]{2,1,0:T(8,128)} custom-call(s32[24]{0:T(128)} %copy-done.3, s32[24]{0:T(128)} %copy-done.3, s32[24]{0:T(128)} %gather_fusion.4, bf16[3072,1024]{1,0:T(8,128)(2,1)} %all-gather.2.cloned.1.call-done.x_ref, bf16[3,1024,512]{2,1,0:T(8,128)(2,1)} %w_ref.5), custom_call_target="tpu_custom_call" | custom-call | flops 3221225472 | bytes 15728640 | tf_op jit(solution)/shard_map/pallas_call | solution.py:36
  260.3 42.7 %shard_map.103.acc_in_ref = f32[3072,512]{1,0:T(8,128)} custom-call(s32[64]{0:T(128)} %get-tuple-element.22.tb_ref, s32[64]{0:T(128)} %get-tuple-element.17.live_ref, s32[64,2,128,128]{3,2,1,0:T(8,128)} %bitcast.28, bf16[64,128,512]{2,1,0:T(8,128)(2,1)} %all-to-all-done.1.msg_ref, f32[64,128,1]{2,1,0:T(8,128)} %copy.22.inv_ref, ...), custom_call_target="tpu_custom_call", output_to_operand_aliasing={{}: (5, {})} | custom-call | flops 1073741824 | bytes 25198592 | tf_op jit(solution)/shard_map/pallas_call | solution.py:78
  303.0 39.4 %all-to-all-done.msg_ref = bf16[64,128,512]{2,1,0:T(8,128)(2,1)} async-done(((bf16[64,128,512]{2,1,0:T(8,128)(2,1)}), bf16[64,128,512]{2,1,0:T(8,128)(2,1)}, u32[]{:S(2)}, u32[]{:S(2)}) %all-to-all-start) | async-done | bytes 8388640 | tf_op jit(solution)/shard_map/all_to_all | solution.py:142
  342.3 42.7 %shard_map.104 = f32[3072,512]{1,0:T(8,128)} custom-call(s32[64]{0:T(128)} %get-tuple-element.21.tb_ref, s32[64]{0:T(128)} %get-tuple-element.18.live_ref, s32[64,2,128,128]{3,2,1,0:T(8,128)} %bitcast.29, bf16[64,128,512]{2,1,0:T(8,128)(2,1)} %all-to-all-done.msg_ref, f32[64,128,1]{2,1,0:T(8,128)} %copy.23.inv_ref, ...), custom_call_target="tpu_custom_call", output_to_operand_aliasing={{}: (5, {})} | custom-call | flops 1073741824 | bytes 25198592 | tf_op jit(solution)/shard_map/pallas_call | solution.py:78
  385.0 4.8 %convert_element_type.9 = bf16[3072,512]{1,0:T(8,128)(2,1)} convert(f32[3072,512]{1,0:T(8,128)} %shard_map.104) | non-fusion elementwise | flops 1572864 | bytes 9437184 | tf_op jit(solution)/shard_map/convert_element_type | solution.py:160
  (34 shorter events, 2.6 us)
Async XLA Ops:
  6.5 24.4 %all-gather.2.cloned.1.call-start = ((), (), s32[]{:S(2)}) async-start(), calls=%async_computation.2 | async-start | bytes 9437184 | tf_op jit(solution)/shard_map/all_gather | solution.py:110
  10.1 20.8 %copy-start.5 = (s32[64]{0:T(128)}, s32[64]{0:T(128)S(1)}, u32[]{:S(2)}) copy-start(s32[64]{0:T(128)S(1)} %get-tuple-element.9.dst_ref) | copy-start | bytes 772
  80.7 137.9 %all-to-all-start.1 = ((bf16[64,128,512]{2,1,0:T(8,128)(2,1)}), bf16[64,128,512]{2,1,0:T(8,128)(2,1)}, u32[]{:S(2)}, u32[]{:S(2)}) async-start(bf16[64,128,512]{2,1,0:T(8,128)(2,1)} %shard_map.101), calls=%async_computation.1 | async-start | bytes 16777216 | tf_op jit(solution)/shard_map/all_to_all | solution.py:142
  93.2 2.7 copy-start.6
  145.6 79.5 %copy-start = (s32[24]{0:T(128)S(1)}, s32[24]{0:T(128)}, u32[]{:S(2)}) copy-start(s32[24]{0:T(128)} %param.11) | copy-start | bytes 292
  145.6 82.3 %copy-start.2 = (s32[1,64,2]{1,2,0:T(2,128)S(1)}, s32[1,64,2]{1,2,0:T(2,128)}, u32[]{:S(2)}) copy-start(s32[1,64,2]{1,2,0:T(2,128)} %param.17) | copy-start | bytes 1540
  145.6 82.3 %copy-start.4 = (s32[1,64,2]{1,2,0:T(2,128)S(1)}, s32[1,64,2]{1,2,0:T(2,128)}, u32[]{:S(2)}) copy-start(s32[1,64,2]{1,2,0:T(2,128)} %param.16) | copy-start | bytes 1540
  145.6 82.6 %copy-start.1 = (s32[1,64,2]{1,2,0:T(2,128)S(1)}, s32[1,64,2]{1,2,0:T(2,128)}, u32[]{:S(2)}) copy-start(s32[1,64,2]{1,2,0:T(2,128)} %param.18) | copy-start | bytes 1540
  218.6 123.7 %all-to-all-start = ((bf16[64,128,512]{2,1,0:T(8,128)(2,1)}), bf16[64,128,512]{2,1,0:T(8,128)(2,1)}, u32[]{:S(2)}, u32[]{:S(2)}) async-start(bf16[64,128,512]{2,1,0:T(8,128)(2,1)} %shard_map.100), calls=%async_computation | async-start | bytes 16777216 | tf_op jit(solution)/shard_map/all_to_all | solution.py:142
  226.7 10.8 %copy-start.3 = (s32[24]{0:T(128)}, s32[24]{0:T(128)S(1)}, u32[]{:S(2)}) copy-start(s32[24]{0:T(128)S(1)} %get-tuple-element.10.dst_ref.src_ref) | copy-start | bytes 292
Sparse Core Ops, SparseCore 0:
  9.0 21.8 all-gather.1

commit v2 on v1

v2 whole, which is shorter than its diff:
```python
import functools

import jax
import jax.numpy as jnp
from jax import lax
from jax.experimental import pallas as pl
from jax.experimental.pallas import tpu as pltpu
from jax.sharding import PartitionSpec as P


def _bmm_kernel(group, src_ref, widx_ref, x_ref, w_ref, o_ref):
    step = pl.program_id(0)
    block_rows = o_ref.shape[1]
    for j in range(group):
        slot = step * group + j
        rows = pl.ds(pl.multiple_of(src_ref[slot] * block_rows, block_rows), block_rows)
        o_ref[j] = jnp.dot(
            x_ref[rows, :], w_ref[widx_ref[slot]], preferred_element_type=jnp.float32
        ).astype(o_ref.dtype)


def _block_matmul(x, w, src, widx, block_rows, out_dtype, group=8):
    k_dim = x.shape[1]
    n_dim = w.shape[2]
    steps = src.shape[0]
    grid_spec = pltpu.PrefetchScalarGridSpec(
        num_scalar_prefetch=2,
        grid=(steps // group,),
        in_specs=[
            pl.BlockSpec(x.shape, lambda i, r, g: (0, 0), pipeline_mode=pl.Buffered(1)),
            pl.BlockSpec(w.shape, lambda i, r, g: (0, 0, 0), pipeline_mode=pl.Buffered(1)),
        ],
        out_specs=pl.BlockSpec((group, block_rows, n_dim), lambda i, r, g: (i, 0, 0)),
    )
    out_bytes = jnp.dtype(out_dtype).itemsize
    cost = pl.CostEstimate(
        flops=2 * steps * block_rows * k_dim * n_dim,
        bytes_accessed=x.size * 2 + w.size * 2 + steps * block_rows * n_dim * out_bytes,
        transcendentals=0,
    )
    return pl.pallas_call(
        functools.partial(_bmm_kernel, group),
        grid_spec=grid_spec,
        out_shape=jax.ShapeDtypeStruct((steps, block_rows, n_dim), out_dtype),
        compiler_params=pltpu.CompilerParams(
            dimension_semantics=("arbitrary",), vmem_limit_bytes=48 * 1024 * 1024
        ),
        cost_estimate=cost,
    )(src, widx, x, w)


def _agg_kernel(group, final, tb_ref, live_ref, tiles_ref, msg_ref, inv_ref, acc_in_ref, out_ref, *scratch):
    step = pl.program_id(0)
    acc_ref = scratch[0] if final else out_ref

    @pl.when(step == 0)
    def _():
        acc_ref[...] = acc_in_ref[...]

    block_rows = msg_ref.shape[1]
    for j in range(group):
        slot = step * group + j
        adj = (tiles_ref[j] * live_ref[slot]).astype(jnp.float32).astype(jnp.bfloat16)
        term = jnp.dot(adj, msg_ref[j], preferred_element_type=jnp.float32) * inv_ref[j]
        rows = pl.ds(pl.multiple_of(tb_ref[slot] * block_rows, block_rows), block_rows)
        acc_ref[rows, :] += term

    if final:
        @pl.when(step == pl.num_programs(0) - 1)
        def _():
            out_ref[...] = acc_ref[...].astype(out_ref.dtype)


def _aggregate(acc, tiles, msgs, inv, tb, live, k, final, group=8):
    steps, block_rows, n_dim = msgs.shape
    rows = acc.shape[0]
    out_dtype = jnp.bfloat16 if final else jnp.float32
    grid_spec = pltpu.PrefetchScalarGridSpec(
        num_scalar_prefetch=2,
        grid=(steps // group,),
        in_specs=[
            pl.BlockSpec((group, None, block_rows, block_rows), lambda i, t, l: (i, k, 0, 0)),
            pl.BlockSpec((group, block_rows, n_dim), lambda i, t, l: (i, 0, 0)),
            pl.BlockSpec((group, block_rows, 1), lambda i, t, l: (i, 0, 0)),
            pl.BlockSpec((rows, n_dim), lambda i, t, l: (0, 0), pipeline_mode=pl.Buffered(1)),
        ],
        out_specs=pl.BlockSpec((rows, n_dim), lambda i, t, l: (0, 0)),
        scratch_shapes=[pltpu.VMEM((rows, n_dim), jnp.float32)] if final else [],
    )
    cost = pl.CostEstimate(
        flops=2 * steps * block_rows * block_rows * n_dim,
        bytes_accessed=steps * block_rows * (block_rows * 4 + n_dim * 2 + 4)
        + rows * n_dim * (4 + jnp.dtype(out_dtype).itemsize),
        transcendentals=0,
    )
    return pl.pallas_call(
        functools.partial(_agg_kernel, group, final),
        grid_spec=grid_spec,
        out_shape=jax.ShapeDtypeStruct(acc.shape, out_dtype),
        compiler_params=pltpu.CompilerParams(
            dimension_semantics=("arbitrary",), vmem_limit_bytes=56 * 1024 * 1024
        ),
        cost_estimate=cost,
    )(tb, live, tiles, msgs, inv, acc)


def on_device(
    features,
    block_type,
    rel_weight,
    self_weight,
    source_relation,
    source_block,
    target_relation,
    target_block,
    live,
    tiles,
):
    blk_count = block_type.shape[0]
    rows_total = features.shape[0]
    block_rows = rows_total // blk_count
    relations = rel_weight.shape[0]
    partitions = live.shape[1]
    capacity = live.shape[2]
    slots = partitions * capacity

    full_rows = lax.all_gather(features, "col", axis=1, tiled=True)

    tiles4 = tiles.reshape(partitions, capacity, block_rows, block_rows)
    live2 = live.reshape(partitions, capacity)
    row_sums = (jnp.sum(tiles4, axis=3) * live2[:, :, None]).astype(jnp.float32)
    keys = target_relation.reshape(slots) * blk_count + target_block.reshape(slots)
    table = (keys[:, None] == jnp.arange(relations * blk_count)[None, :]).astype(jnp.float32)
    degree = jnp.dot(
        table.T, row_sums.reshape(slots, block_rows), precision=lax.Precision.HIGHEST
    )
    inverse = 1.0 / jnp.maximum(degree, 1.0)
    scale = jnp.dot(table, inverse, precision=lax.Precision.HIGHEST)
    scale = scale.reshape(partitions, capacity, block_rows, 1)

    src_blocks = source_block.reshape(partitions, capacity)
    src_rels = source_relation.reshape(partitions, capacity)
    dst_blocks = target_block.reshape(partitions, capacity)

    arrived = []
    for k in range(capacity):
        msgs = _block_matmul(
            full_rows, rel_weight, src_blocks[:, k], src_rels[:, k], block_rows, jnp.bfloat16
        )
        arrived.append(lax.all_to_all(msgs, "dom", split_axis=0, concat_axis=0, tiled=True))

    selfs = _block_matmul(
        full_rows,
        self_weight,
        jnp.arange(blk_count, dtype=jnp.int32),
        block_type,
        block_rows,
        jnp.float32,
    )
    acc = selfs.reshape(rows_total, selfs.shape[2])
    for k in range(capacity):
        acc = _aggregate(
            acc,
            tiles4,
            arrived[k],
            scale[:, k],
            dst_blocks[:, k],
            live2[:, k],
            k,
            final=k == capacity - 1,
        )
    return acc


def solution(mesh):
    in_specs = (
        P("dom", "col"),
        P("dom"),
        P(None, None, "col"),
        P(None, None, "col"),
        P("dom", None, None),
        P("dom", None, None),
        P("dom", None, None),
        P("dom", None, None),
        P("dom", None, None),
        P("dom", None, None, None, None),
    )
    out_specs = P("dom", "col")
    return jax.shard_map(
        on_device, mesh=mesh, in_specs=in_specs, out_specs=out_specs, check_vma=False
    )
```

time: 403 us -> 336 us (0.83); the launches traced: 397 us -> 335 us
  Pallas kernels: 204 us -> 75.9 us
  waiting for transfers between devices: 131 us -> 210 us
  other arithmetic: 16.2 us -> 5.66 us
  local copies, waits for them, and re-layouts: 14.4 us -> 7.18 us
  starting transfers between devices: 16.9 us -> 22.6 us
    pallas_call x5, Pallas kernels: 204 us -> 75.9 us  [the longest x3 47.4 us: _block_matmul(): pl.pallas_call(functools.partial(_bmm_kernel, group), grid_spec=grid_spec...]
    all_to_all x2, waiting for transfers between devices: 112 us -> 186 us  [on_device(): lax.all_to_all(msgs, 'dom', split_axis=0, concat_axis=0, tiled=True)]
    gather x5 -> x0, local copies, waits for them, and re-layouts: 6.53 us -> none  [the longest x2 2.73 us: on_device(): src_blocks[:, k][order]]
    all_to_all x2, starting transfers between devices: 16.9 us -> 22.6 us  [on_device(): lax.all_to_all(msgs, 'dom', split_axis=0, concat_axis=0, tiled=True)]
    sort x3 -> x0, other arithmetic: 5.68 us -> none  [the longest x2 4.07 us: on_device(): order = jnp.argsort(rel_k).astype(jnp.int32)]
    all_gather x1, waiting for transfers between devices: 17.4 us -> 22.9 us  [on_device(): full_rows = lax.all_gather(features, 'col', axis=1, tiled=True)]
    convert_element_type x1 -> x0, other arithmetic: 4.85 us -> none  [on_device(): return acc.astype(jnp.bfloat16)]
  transfers between devices with their start and end apart: 3 -> 3, of which waited for: 3 -> 3; matrix products, arithmetic and copies ran while one was open for 7% -> 4% of each run, Pallas kernels for 28% -> 13%
where the time goes in v2:
time: 336 us; the launch traced here: 335 us
  waiting for transfers between devices  210 us (62%)
  Pallas kernels  75.9 us (23%)
  starting transfers between devices  22.6 us (7%)
  between operations  13.5 us (4%)
  local copies, waits for them, and re-layouts  7.18 us (2%)
  other arithmetic  5.66 us (2%)
    all_to_all x2, waiting for transfers between devices, on_device(): lax.all_to_all(msgs, 'dom', split_axis=0, concat_axis=0, tiled=True)  186 us
    pallas_call x3, Pallas kernels, _block_matmul(): pl.pallas_call(functools.partial(_bmm_kernel, group), grid_spec=grid_spec...  47.4 us
    pallas_call x2, Pallas kernels, _aggregate(): pl.pallas_call(functools.partial(_agg_kernel, group, final), grid_spec=gr...  28.5 us
    all_gather x1, waiting for transfers between devices, on_device(): full_rows = lax.all_gather(features, 'col', axis=1, tiled=True)  22.9 us
    all_to_all x2, starting transfers between devices, on_device(): lax.all_to_all(msgs, 'dom', split_axis=0, concat_axis=0, tiled=True)  22.6 us
  transfers between devices with their start and end apart: 3, of which 3 were waited for; matrix products, arithmetic and copies ran while one was open for 4% of the time, Pallas kernels for 13%

profile of v2, /device:TPU:4, one launch (start us, length us, event | category | flops | bytes accessed | tf_op | source)
XLA Modules:
  0.0 335.5 jit_solution(6352286343891617584)
XLA Ops:
  6.5 0.7 all-gather.2.cloned.1.call-update
  7.3 0.8 slice_bitcast_fusion
  8.0 22.9 %all-gather.2.cloned.1.call-done.x_ref = bf16[3072,1024]{1,0:T(8,128)(2,1)} async-done(((bf16[3072,512]{1,0:T(8,128)(2,1)}), bf16[3072,1024]{1,0:T(8,128)(2,1)}) %all-gather.2.cloned.1.call-update) | async-done | bytes 6291472 | tf_op jit(solution)/shard_map/all_gather | solution.py:127
  30.9 19.4 %shard_map.101 = bf16[64,128,512]{2,1,0:T(8,128)(2,1)} custom-call(s32[64]{0:T(128)S(1)} %get-tuple-element.16.src_ref, s32[64]{0:T(128)S(1)} %get-tuple-element.7.widx_ref, bf16[3072,1024]{1,0:T(8,128)(2,1)} %all-gather.2.cloned.1.call-done.x_ref, bf16[16,1024,512]{2,1,0:T(8,128)(2,1)} %w_ref.4), custom_call_target="tpu_custom_call" | custom-call | flops 8589934592 | bytes 31457280 | tf_op jit(solution)/shard_map/pallas_call | solution.py:41
  50.3 10.6 %all-to-all-start.1 = ((bf16[64,128,512]{2,1,0:T(8,128)(2,1)}), bf16[64,128,512]{2,1,0:T(8,128)(2,1)}, u32[]{:S(2)}, u32[]{:S(2)}) async-start(bf16[64,128,512]{2,1,0:T(8,128)(2,1)} %shard_map.101), calls=%async_computation.1 | async-start | bytes 16777216 | tf_op jit(solution)/shard_map/all_to_all | solution.py:150
  60.9 19.4 %shard_map.100 = bf16[64,128,512]{2,1,0:T(8,128)(2,1)} custom-call(s32[64]{0:T(128)S(1)} %get-tuple-element.15.src_ref, s32[64]{0:T(128)S(1)} %get-tuple-element.8.widx_ref, bf16[3072,1024]{1,0:T(8,128)(2,1)} %all-gather.2.cloned.1.call-done.x_ref, bf16[16,1024,512]{2,1,0:T(8,128)(2,1)} %w_ref.4), custom_call_target="tpu_custom_call" | custom-call | flops 8589934592 | bytes 31457280 | tf_op jit(solution)/shard_map/pallas_call | solution.py:41
  80.3 106.0 %all-to-all-done.1.msg_ref = bf16[64,128,512]{2,1,0:T(8,128)(2,1)} async-done(((bf16[64,128,512]{2,1,0:T(8,128)(2,1)}), bf16[64,128,512]{2,1,0:T(8,128)(2,1)}, u32[]{:S(2)}, u32[]{:S(2)}) %all-to-all-start.1) | async-done | bytes 8388640 | tf_op jit(solution)/shard_map/all_to_all | solution.py:150
  186.3 12.0 %all-to-all-start = ((bf16[64,128,512]{2,1,0:T(8,128)(2,1)}), bf16[64,128,512]{2,1,0:T(8,128)(2,1)}, u32[]{:S(2)}, u32[]{:S(2)}) async-start(bf16[64,128,512]{2,1,0:T(8,128)(2,1)} %shard_map.100), calls=%async_computation | async-start | bytes 16777216 | tf_op jit(solution)/shard_map/all_to_all | solution.py:150
  198.3 0.1 copy.18
  198.4 0.1 add.11
  198.6 0.1 copy.19
  198.7 0.1 mul.24
  198.8 5.7 %reduce_sum.11 = s32[64,2,128]{2,1,0:T(2,128)S(1)} reduce(s32[1,64,2,128,128]{4,3,2,1,0:T(8,128)} %param.19, s32[]{:T(128)} %constant.2.clone.1), dimensions={0,4}, to_apply=%region_0.0 | reduce | flops 2080768 | bytes 8454148 | tf_op jit(solution)/shard_map/reduce_sum | solution.py:131
  204.5 0.0 copy-start
  204.5 0.4 fusion
  204.9 0.3 fusion.1
  205.2 0.1 fusion.7
  205.3 2.6 copy.20.inv_ref
  207.9 2.6 copy.21.inv_ref
  210.6 0.6 slice_bitcast_fusion.2
  211.2 8.6 %shard_map.102 = f32[24,128,512]{2,1,0:T(8,128)} custom-call(s32[24]{0:T(128)S(1)} %iota.7.src_ref, s32[24]{0:T(128)S(1)} %copy-done.1, bf16[3072,1024]{1,0:T(8,128)(2,1)} %all-gather.2.cloned.1.call-done.x_ref, bf16[3,1024,512]{2,1,0:T(8,128)(2,1)S(1)} %copy-done), custom_call_target="tpu_custom_call" | custom-call | flops 3221225472 | bytes 15728640 | tf_op jit(solution)/shard_map/pallas_call | solution.py:41
  219.8 14.6 %shard_map.103.acc_in_ref = f32[3072,512]{1,0:T(8,128)} custom-call(s32[64]{0:T(128)} %get-tuple-element.18.tb_ref, s32[64]{0:T(128)} %get-tuple-element.11.live_ref, s32[64,2,128,128]{3,2,1,0:T(8,128)} %bitcast.27, bf16[64,128,512]{2,1,0:T(8,128)(2,1)} %all-to-all-done.1.msg_ref, f32[64,128,1]{2,1,0:T(8,128)} %copy.20.inv_ref, f32[3072,512]{1,0:T(8,128)} %bitcast.29), custom_call_target="tpu_custom_call" | custom-call | flops 1073741824 | bytes 25198592 | tf_op jit(solution)/shard_map/pallas_call | solution.py:96
  234.3 80.4 %all-to-all-done.msg_ref = bf16[64,128,512]{2,1,0:T(8,128)(2,1)} async-done(((bf16[64,128,512]{2,1,0:T(8,128)(2,1)}), bf16[64,128,512]{2,1,0:T(8,128)(2,1)}, u32[]{:S(2)}, u32[]{:S(2)}) %all-to-all-start) | async-done | bytes 8388640 | tf_op jit(solution)/shard_map/all_to_all | solution.py:150
  314.7 13.9 %shard_map.104 = bf16[3072,512]{1,0:T(8,128)(2,1)} custom-call(s32[64]{0:T(128)} %get-tuple-element.17.tb_ref, s32[64]{0:T(128)} %get-tuple-element.12.live_ref, s32[64,2,128,128]{3,2,1,0:T(8,128)} %bitcast.28, bf16[64,128,512]{2,1,0:T(8,128)(2,1)} %all-to-all-done.msg_ref, f32[64,128,1]{2,1,0:T(8,128)} %copy.21.inv_ref, f32[3072,512]{1,0:T(8,128)} %shard_map.103.acc_in_ref), custom_call_target="tpu_custom_call" | custom-call | flops 1073741824 | bytes 22052864 | tf_op jit(solution)/shard_map/pallas_call | solution.py:96
  (12 shorter events, 0.0 us)
Async XLA Ops:
  6.5 24.4 %all-gather.2.cloned.1.call-start = ((), (), s32[]{:S(2)}) async-start(), calls=%async_computation.2 | async-start | bytes 9437184 | tf_op jit(solution)/shard_map/all_gather | solution.py:127
  50.3 136.1 %all-to-all-start.1 = ((bf16[64,128,512]{2,1,0:T(8,128)(2,1)}), bf16[64,128,512]{2,1,0:T(8,128)(2,1)}, u32[]{:S(2)}, u32[]{:S(2)}) async-start(bf16[64,128,512]{2,1,0:T(8,128)(2,1)} %shard_map.101), calls=%async_computation.1 | async-start | bytes 16777216 | tf_op jit(solution)/shard_map/all_to_all | solution.py:150
  80.3 118.0 %copy-start.3 = (s32[1,64,2]{1,2,0:T(2,128)S(1)}, s32[1,64,2]{1,2,0:T(2,128)}, u32[]{:S(2)}) copy-start(s32[1,64,2]{1,2,0:T(2,128)} %param.17) | copy-start | bytes 1540
  80.3 118.0 %copy-start.4 = (s32[1,64,2]{1,2,0:T(2,128)S(1)}, s32[1,64,2]{1,2,0:T(2,128)}, u32[]{:S(2)}) copy-start(s32[1,64,2]{1,2,0:T(2,128)} %param.16) | copy-start | bytes 1540
  80.3 118.3 %copy-start.2 = (s32[1,64,2]{1,2,0:T(2,128)S(1)}, s32[1,64,2]{1,2,0:T(2,128)}, u32[]{:S(2)}) copy-start(s32[1,64,2]{1,2,0:T(2,128)} %param.18) | copy-start | bytes 1540
  186.3 128.4 %all-to-all-start = ((bf16[64,128,512]{2,1,0:T(8,128)(2,1)}), bf16[64,128,512]{2,1,0:T(8,128)(2,1)}, u32[]{:S(2)}, u32[]{:S(2)}) async-start(bf16[64,128,512]{2,1,0:T(8,128)(2,1)} %shard_map.100), calls=%async_computation | async-start | bytes 16777216 | tf_op jit(solution)/shard_map/all_to_all | solution.py:150
  204.5 6.7 %copy-start = (bf16[3,1024,512]{2,1,0:T(8,128)(2,1)S(1)}, bf16[3,1024,512]{2,1,0:T(8,128)(2,1)}, u32[]{:S(2)}) copy-start(bf16[3,1024,512]{2,1,0:T(8,128)(2,1)} %w_ref.5) | copy-start | bytes 9437188
  204.5 6.7 %copy-start.1 = (s32[24]{0:T(128)S(1)}, s32[24]{0:T(128)}, u32[]{:S(2)}) copy-start(s32[24]{0:T(128)} %widx_ref.1) | copy-start | bytes 292
Sparse Core Ops, SparseCore 0:
  9.0 21.8 all-gather.1

commit v3 on v2

--- a/solution.py
+++ b/solution.py
@@ -43,7 +43,7 @@
         grid_spec=grid_spec,
         out_shape=jax.ShapeDtypeStruct((steps, block_rows, n_dim), out_dtype),
         compiler_params=pltpu.CompilerParams(
-            dimension_semantics=("arbitrary",), vmem_limit_bytes=48 * 1024 * 1024
+            dimension_semantics=("arbitrary",), vmem_limit_bytes=56 * 1024 * 1024
         ),
         cost_estimate=cost,
     )(src, widx, x, w)
@@ -142,11 +142,14 @@
     src_rels = source_relation.reshape(partitions, capacity)
     dst_blocks = target_block.reshape(partitions, capacity)
 
-    arrived = []
-    for k in range(capacity):
+    feature_blocks = features.reshape(blk_count, block_rows, features.shape[1])
+    raw = feature_blocks[src_blocks[:, 0]]
+    arrived = [lax.all_to_all(raw, "dom", split_axis=0, concat_axis=0, tiled=True)]
+    for k in range(1, capacity):
         msgs = _block_matmul(
             full_rows, rel_weight, src_blocks[:, k], src_rels[:, k], block_rows, jnp.bfloat16
         )
+        arrived[0], msgs = lax.optimization_barrier((arrived[0], msgs))
         arrived.append(lax.all_to_all(msgs, "dom", split_axis=0, concat_axis=0, tiled=True))
 
     selfs = _block_matmul(
@@ -158,6 +161,15 @@
         jnp.float32,
     )
     acc = selfs.reshape(rows_total, selfs.shape[2])
+    wide = lax.all_gather(arrived[0], "col", axis=2, tiled=True)
+    arrived[0] = _block_matmul(
+        wide.reshape(partitions * block_rows, wide.shape[2]),
+        rel_weight,
+        jnp.arange(partitions, dtype=jnp.int32),
+        target_relation.reshape(partitions, capacity)[:, 0],
+        block_rows,
+        jnp.bfloat16,
+    )
     for k in range(capacity):
         acc = _aggregate(
             acc,

time: 336 us -> 297 us (0.88)
  waiting for transfers between devices: 210 us -> 154 us
  local copies, waits for them, and re-layouts: 7.18 us -> 17 us
  Pallas kernels: 75.9 us -> 80.2 us
  other arithmetic: 5.66 us -> 9.46 us
    all_to_all x2 -> x1, waiting for transfers between devices: 186 us -> 54.9 us  [on_device(): lax.all_to_all(msgs, 'dom', split_axis=0, concat_axis=0, tiled=True)]
    all_to_all x0 -> x1, waiting for transfers between devices: none -> 76.9 us  [on_device(): lax.all_to_all(raw, 'dom', split_axis=0, concat_axis=0, tiled=True)]
    all_to_all x2 -> x1, starting transfers between devices: 22.6 us -> 9.04 us  [on_device(): lax.all_to_all(msgs, 'dom', split_axis=0, concat_axis=0, tiled=True)]
    all_to_all x0 -> x1, starting transfers between devices: none -> 11.8 us  [on_device(): lax.all_to_all(raw, 'dom', split_axis=0, concat_axis=0, tiled=True)]
    gather x0 -> x1, local copies, waits for them, and re-layouts: none -> 7.43 us  [on_device(): raw = feature_blocks[src_blocks[:, 0]]]
    pallas_call x3, Pallas kernels: 47.4 us -> 51.7 us  [_block_matmul(): pl.pallas_call(functools.partial(_bmm_kernel, group), grid_spec=grid_spec...]
  transfers between devices with their start and end apart: 3 -> 4, of which waited for: 3 -> 3; matrix products, arithmetic and copies ran while one was open for 4% -> 6% of each run, Pallas kernels for 13% -> 22%
where the time goes in v3:
time: 297 us; the launch traced here: 296 us
  waiting for transfers between devices  154 us (52%)
  Pallas kernels  80.2 us (27%)
  starting transfers between devices  20.9 us (7%)
  local copies, waits for them, and re-layouts  17 us (6%)
  between operations  13.5 us (5%)
  other arithmetic  9.46 us (3%)
    all_to_all x1, waiting for transfers between devices, on_device(): lax.all_to_all(raw, 'dom', split_axis=0, concat_axis=0, tiled=True)  76.9 us
    all_to_all x1, waiting for transfers between devices, on_device(): lax.all_to_all(msgs, 'dom', split_axis=0, concat_axis=0, tiled=True)  54.9 us
    pallas_call x3, Pallas kernels, _block_matmul(): pl.pallas_call(functools.partial(_bmm_kernel, group), grid_spec=grid_spec...  51.7 us
    pallas_call x2, Pallas kernels, _aggregate(): pl.pallas_call(functools.partial(_agg_kernel, group, final), grid_spec=gr...  28.5 us
    all_gather x1, waiting for transfers between devices, on_device(): full_rows = lax.all_gather(features, 'col', axis=1, tiled=True)  21.9 us
    all_to_all x1, starting transfers between devices, on_device(): lax.all_to_all(raw, 'dom', split_axis=0, concat_axis=0, tiled=True)  11.8 us
    all_to_all x1, starting transfers between devices, on_device(): lax.all_to_all(msgs, 'dom', split_axis=0, concat_axis=0, tiled=True)  9.04 us
    reduce_sum x1, other arithmetic, on_device(): row_sums = (jnp.sum(tiles4, axis=3) * live2[:, :, None]).astype(jnp.float32)  8.18 us
  transfers between devices with their start and end apart: 4, of which 3 were waited for; matrix products, arithmetic and copies ran while one was open for 6% of the time, Pallas kernels for 22%

profile of v3, /device:TPU:4, one launch (start us, length us, event | category | flops | bytes accessed | tf_op | source)
XLA Modules:
  0.0 296.1 jit_solution(10404627076069882952)
XLA Ops:
  6.5 1.3 slice_bitcast_fusion.4
  7.8 7.4 %gather_fusion = bf16[64,128,512]{2,1,0:T(8,128)(2,1)} fusion(bf16[24,128,512]{2,1,0:T(8,128)(2,1)} %bitcast.32, s32[1024]{0:T(1024)S(1)} %pad_clamp_fusion), kind=kCustom, calls=%fused_computation | custom fusion | bytes 16777472 | tf_op jit(solution)/shard_map/gather | solution.py:146
  15.2 11.8 %all-to-all-start = ((bf16[64,128,512]{2,1,0:T(8,128)(2,1)}), bf16[64,128,512]{2,1,0:T(8,128)(2,1)}, u32[]{:S(2)}, u32[]{:S(2)}) async-start(bf16[64,128,512]{2,1,0:T(8,128)(2,1)} %gather_fusion), calls=%async_computation | async-start | bytes 16777216 | tf_op jit(solution)/shard_map/all_to_all | solution.py:147
  27.1 0.7 all-gather.3.cloned.1.call-update
  27.8 0.5 slice_bitcast_fusion.3.widx_ref
  28.4 21.9 %all-gather.3.cloned.1.call-done.x_ref = bf16[3072,1024]{1,0:T(8,128)(2,1)} async-done(((bf16[3072,512]{1,0:T(8,128)(2,1)}), bf16[3072,1024]{1,0:T(8,128)(2,1)}) %all-gather.3.cloned.1.call-update) | async-done | bytes 6291472 | tf_op jit(solution)/shard_map/all_gather | solution.py:127
  50.2 19.6 %shard_map.100 = bf16[64,128,512]{2,1,0:T(8,128)(2,1)} custom-call(s32[64]{0:T(128)} %get-tuple-element.15.src_ref, s32[64]{0:T(128)} %slice_bitcast_fusion.3.widx_ref, bf16[3072,1024]{1,0:T(8,128)(2,1)} %all-gather.3.cloned.1.call-done.x_ref, bf16[16,1024,512]{2,1,0:T(8,128)(2,1)} %w_ref.4), custom_call_target="tpu_custom_call" | custom-call | flops 8589934592 | bytes 31457280 | tf_op jit(solution)/shard_map/pallas_call | solution.py:41
  69.8 76.9 %all-to-all-done = bf16[64,128,512]{2,1,0:T(8,128)(2,1)} async-done(((bf16[64,128,512]{2,1,0:T(8,128)(2,1)}), bf16[64,128,512]{2,1,0:T(8,128)(2,1)}, u32[]{:S(2)}, u32[]{:S(2)}) %all-to-all-start) | async-done | bytes 8388640 | tf_op jit(solution)/shard_map/all_to_all | solution.py:147
  146.8 9.0 %all-to-all-start.1 = ((bf16[64,128,512]{2,1,0:T(8,128)(2,1)}), bf16[64,128,512]{2,1,0:T(8,128)(2,1)}, u32[]{:S(2)}, u32[]{:S(2)}) async-start(bf16[64,128,512]{2,1,0:T(8,128)(2,1)} %shard_map.100), calls=%async_computation.1 | async-start | bytes 16777216 | tf_op jit(solution)/shard_map/all_to_all | solution.py:153
  155.9 0.1 add.20
  156.3 8.2 %reduce_sum.11 = s32[64,2,128]{2,1,0:T(2,128)S(1)} reduce(s32[1,64,2,128,128]{4,3,2,1,0:T(8,128)} %param.19, s32[]{:T(128)} %constant.3.clone.1), dimensions={0,4}, to_apply=%region_0.0 | reduce | flops 2080768 | bytes 8454148 | tf_op jit(solution)/shard_map/reduce_sum | solution.py:131
  164.5 0.4 fusion
  164.9 0.3 fusion.1
  165.3 2.8 copy.20.inv_ref
  168.1 3.4 %copy.21.inv_ref = f32[64,128,1]{2,1,0:T(8,128)} copy(f32[64,128,1]{1,0,2:T(8,128)S(1)} %bitcast.36) | data formatting | bytes 65536 | tf_op jit(solution)/shard_map/squeeze | solution.py:178
  171.6 0.5 slice_bitcast_fusion.widx_ref
  172.1 0.6 slice_bitcast_fusion.1
  172.7 0.5 iota.11.src_ref
  173.2 9.6 %shard_map.102 = f32[24,128,512]{2,1,0:T(8,128)} custom-call(s32[24]{0:T(128)} %iota.11.src_ref, s32[24]{0:T(128)} %widx_ref.1, bf16[3072,1024]{1,0:T(8,128)(2,1)} %all-gather.3.cloned.1.call-done.x_ref, bf16[3,1024,512]{2,1,0:T(8,128)(2,1)} %w_ref.5), custom_call_target="tpu_custom_call" | custom-call | flops 3221225472 | bytes 15728640 | tf_op jit(solution)/shard_map/pallas_call | solution.py:41
  182.9 0.5 iota.10.src_ref
  183.4 22.5 %shard_map.101.msg_ref = bf16[64,128,512]{2,1,0:T(8,128)(2,1)} custom-call(s32[64]{0:T(128)} %iota.10.src_ref, s32[64]{0:T(128)} %slice_bitcast_fusion.widx_ref, bf16[8192,1024]{1,0:T(8,128)(2,1)} %bitcast.34, bf16[16,1024,512]{2,1,0:T(8,128)(2,1)} %w_ref.4), custom_call_target="tpu_custom_call" | custom-call | flops 8589934592 | bytes 41943040 | tf_op jit(solution)/shard_map/pallas_call | solution.py:41
  205.9 14.6 %shard_map.103.acc_in_ref = f32[3072,512]{1,0:T(8,128)} custom-call(s32[64]{0:T(128)} %get-tuple-element.18.tb_ref, s32[64]{0:T(128)} %get-tuple-element.11.live_ref, s32[64,2,128,128]{3,2,1,0:T(8,128)} %bitcast.30, bf16[64,128,512]{2,1,0:T(8,128)(2,1)} %shard_map.101.msg_ref, f32[64,128,1]{2,1,0:T(8,128)} %copy.20.inv_ref, f32[3072,512]{1,0:T(8,128)} %bitcast.33), custom_call_target="tpu_custom_call" | custom-call | flops 1073741824 | bytes 25198592 | tf_op jit(solution)/shard_map/pallas_call | solution.py:96
  220.5 54.9 %all-to-all-done.1.msg_ref = bf16[64,128,512]{2,1,0:T(8,128)(2,1)} async-done(((bf16[64,128,512]{2,1,0:T(8,128)(2,1)}), bf16[64,128,512]{2,1,0:T(8,128)(2,1)}, u32[]{:S(2)}, u32[]{:S(2)}) %all-to-all-start.1) | async-done | bytes 8388640 | tf_op jit(solution)/shard_map/all_to_all | solution.py:153
  275.4 13.9 %shard_map.104 = bf16[3072,512]{1,0:T(8,128)(2,1)} custom-call(s32[64]{0:T(128)} %get-tuple-element.17.tb_ref, s32[64]{0:T(128)} %get-tuple-element.12.live_ref, s32[64,2,128,128]{3,2,1,0:T(8,128)} %bitcast.31, bf16[64,128,512]{2,1,0:T(8,128)(2,1)} %all-to-all-done.1.msg_ref, f32[64,128,1]{2,1,0:T(8,128)} %copy.21.inv_ref, f32[3072,512]{1,0:T(8,128)} %shard_map.103.acc_in_ref), custom_call_target="tpu_custom_call" | custom-call | flops 1073741824 | bytes 22052864 | tf_op jit(solution)/shard_map/pallas_call | solution.py:96
  (18 shorter events, 0.5 us)
Async XLA Ops:
  15.2 12.6 %copy-start.3 = (s32[1,64,2]{1,2,0:T(2,128)S(1)}, s32[1,64,2]{1,2,0:T(2,128)}, u32[]{:S(2)}) copy-start(s32[1,64,2]{1,2,0:T(2,128)} %param.14) | copy-start | bytes 1540
  15.2 131.5 %all-to-all-start = ((bf16[64,128,512]{2,1,0:T(8,128)(2,1)}), bf16[64,128,512]{2,1,0:T(8,128)(2,1)}, u32[]{:S(2)}, u32[]{:S(2)}) async-start(bf16[64,128,512]{2,1,0:T(8,128)(2,1)} %gather_fusion), calls=%async_computation | async-start | bytes 16777216 | tf_op jit(solution)/shard_map/all_to_all | solution.py:147
  27.0 23.2 %all-gather.3.cloned.1.call-start = ((), (), s32[]{:S(2)}) async-start(), calls=%async_computation.2 | async-start | bytes 9437184 | tf_op jit(solution)/shard_map/all_gather | solution.py:127
  27.7 155.1 %all-gather.5.cloned.1.call-start = ((), (), s32[]{:S(2)}) async-start(), calls=%async_computation.3 | async-start | bytes 25165824 | tf_op jit(solution)/shard_map/all_gather | solution.py:164
  146.7 9.1 %copy-start.1 = (s32[1,64,2]{1,2,0:T(2,128)S(1)}, s32[1,64,2]{1,2,0:T(2,128)}, u32[]{:S(2)}) copy-start(s32[1,64,2]{1,2,0:T(2,128)} %param.17) | copy-start | bytes 1540
  146.7 9.1 %copy-start.2 = (s32[1,64,2]{1,2,0:T(2,128)S(1)}, s32[1,64,2]{1,2,0:T(2,128)}, u32[]{:S(2)}) copy-start(s32[1,64,2]{1,2,0:T(2,128)} %param.16) | copy-start | bytes 1540
  146.7 9.3 %copy-start = (s32[1,64,2]{1,2,0:T(2,128)S(1)}, s32[1,64,2]{1,2,0:T(2,128)}, u32[]{:S(2)}) copy-start(s32[1,64,2]{1,2,0:T(2,128)} %param.18) | copy-start | bytes 1540
  146.8 128.6 %all-to-all-start.1 = ((bf16[64,128,512]{2,1,0:T(8,128)(2,1)}), bf16[64,128,512]{2,1,0:T(8,128)(2,1)}, u32[]{:S(2)}, u32[]{:S(2)}) async-start(bf16[64,128,512]{2,1,0:T(8,128)(2,1)} %shard_map.100), calls=%async_computation.1 | async-start | bytes 16777216 | tf_op jit(solution)/shard_map/all_to_all | solution.py:153
Sparse Core Ops, SparseCore 0:
  29.5 20.7 all-gather.2
  146.8 32.4 all-gather.4

commit v4 on v3

--- a/solution.py
+++ b/solution.py
@@ -102,6 +102,14 @@
         ),
         cost_estimate=cost,
     )(tb, live, tiles, msgs, inv, acc)
+
+
+def _widen(x, axis):
+    other = lax.ppermute(x, "col", [(0, 1), (1, 0)])
+    first = lax.axis_index("col") == 0
+    low = jnp.where(first, x, other)
+    high = jnp.where(first, other, x)
+    return jnp.concatenate([low, high], axis=axis)
 
 
 def on_device(
@@ -124,7 +132,7 @@
     capacity = live.shape[2]
     slots = partitions * capacity
 
-    full_rows = lax.all_gather(features, "col", axis=1, tiled=True)
+    full_rows = _widen(features, 1)
 
     tiles4 = tiles.reshape(partitions, capacity, block_rows, block_rows)
     live2 = live.reshape(partitions, capacity)
@@ -161,7 +169,7 @@
         jnp.float32,
     )
     acc = selfs.reshape(rows_total, selfs.shape[2])
-    wide = lax.all_gather(arrived[0], "col", axis=2, tiled=True)
+    wide = _widen(arrived[0], 2)
     arrived[0] = _block_matmul(
         wide.reshape(partitions * block_rows, wide.shape[2]),
         rel_weight,

time: 297 us -> 292 us (0.983)
  other arithmetic: 9.46 us -> 26.3 us
  between operations: 13.5 us -> 0.15 us
  waiting for transfers between devices: 154 us -> 145 us
    all_gather x2 -> x0, waiting for transfers between devices: 21.9 us -> none  [the longest x1 21.9 us: on_device(): full_rows = lax.all_gather(features, 'col', axis=1, tiled=True)]
    all_to_all x1, waiting for transfers between devices: 76.9 us -> 88.3 us  [on_device(): lax.all_to_all(raw, 'dom', split_axis=0, concat_axis=0, tiled=True)]
    concatenate x0 -> x2, other arithmetic: none -> 10.6 us  [_widen(): return jnp.concatenate([low, high], axis=axis)]
    select_n x0 -> x2, other arithmetic: none -> 8.78 us  [_widen(): low = jnp.where(first, x, other)]
    ppermute x0 -> x2, waiting for transfers between devices: none -> 5.28 us  [_widen(): other = lax.ppermute(x, 'col', [(0, 1), (1, 0)])]
    all_to_all x1, waiting for transfers between devices: 54.9 us -> 51.4 us  [on_device(): lax.all_to_all(msgs, 'dom', split_axis=0, concat_axis=0, tiled=True)]
  transfers between devices with their start and end apart: 4 -> 4, of which waited for: 3 -> 3; matrix products, arithmetic and copies ran while one was open for 6% -> 12% of each run, Pallas kernels for 22% -> 23%
where the time goes in v4:
time: 292 us; the launch traced here: 289 us
  waiting for transfers between devices  145 us (50%)
  Pallas kernels  80.1 us (27%)
  other arithmetic  26.3 us (9%)
  starting transfers between devices  20.9 us (7%)
  local copies, waits for them, and re-layouts  15.8 us (5%)
    all_to_all x1, waiting for transfers between devices, on_device(): lax.all_to_all(raw, 'dom', split_axis=0, concat_axis=0, tiled=True)  88.3 us
    pallas_call x3, Pallas kernels, _block_matmul(): pl.pallas_call(functools.partial(_bmm_kernel, group), grid_spec=grid_spec...  51.7 us
    all_to_all x1, waiting for transfers between devices, on_device(): lax.all_to_all(msgs, 'dom', split_axis=0, concat_axis=0, tiled=True)  51.4 us
    pallas_call x2, Pallas kernels, _aggregate(): pl.pallas_call(functools.partial(_agg_kernel, group, final), grid_spec=gr...  28.4 us
    all_to_all x1, starting transfers between devices, on_device(): lax.all_to_all(raw, 'dom', split_axis=0, concat_axis=0, tiled=True)  11.9 us
    concatenate x2, other arithmetic, _widen(): return jnp.concatenate([low, high], axis=axis)  10.6 us
    all_to_all x1, starting transfers between devices, on_device(): lax.all_to_all(msgs, 'dom', split_axis=0, concat_axis=0, tiled=True)  8.91 us
    select_n x2, other arithmetic, _widen(): low = jnp.where(first, x, other)  8.78 us
  transfers between devices with their start and end apart: 4, of which 3 were waited for; matrix products, arithmetic and copies ran while one was open for 12% of the time, Pallas kernels for 23%

profile of v4, /device:TPU:4, one launch (start us, length us, event | category | flops | bytes accessed | tf_op | source)
XLA Modules:
  0.0 289.1 jit_solution(4112302937486421612)
XLA Ops:
  0.0 1.3 slice_bitcast_fusion.4
  1.3 7.4 %gather_fusion = bf16[64,128,512]{2,1,0:T(8,128)(2,1)} fusion(bf16[24,128,512]{2,1,0:T(8,128)(2,1)} %bitcast.33, s32[1024]{0:T(1024)S(1)} %pad_clamp_fusion), kind=kCustom, calls=%fused_computation | custom fusion | bytes 16777472 | tf_op jit(solution)/shard_map/gather | solution.py:154
  8.7 11.9 %all-to-all-start = ((bf16[64,128,512]{2,1,0:T(8,128)(2,1)}), bf16[64,128,512]{2,1,0:T(8,128)(2,1)}, u32[]{:S(2)}, u32[]{:S(2)}) async-start(bf16[64,128,512]{2,1,0:T(8,128)(2,1)} %gather_fusion), calls=%async_computation | async-start | bytes 16777216 | tf_op jit(solution)/shard_map/all_to_all | solution.py:155
  20.7 0.5 slice_bitcast_fusion.3.widx_ref
  21.2 5.3 %collective-permute-done = bf16[3072,512]{1,0:T(8,128)(2,1)} collective-permute-done((bf16[3072,512]{1,0:T(8,128)(2,1)S(1)}, bf16[3072,512]{1,0:T(8,128)(2,1)}, u32[]{:S(2)}, u32[]{:S(2)}) %collective-permute-start) | collective-permute-done | bytes 3145760 | tf_op jit(solution)/shard_map/ppermute | solution.py:108
  26.5 2.3 broadcast_select_fusion.3
  28.8 3.6 %pad_maximum_fusion.1.x_ref = bf16[3072,1024]{1,0:T(8,128)(2,1)} fusion(bf16[3072,512]{1,0:T(8,128)(2,1)S(1)} %get-tuple-element.12, bf16[3072,512]{1,0:T(8,128)(2,1)S(1)} %get-tuple-element.11), kind=kLoop, calls=%fused_computation.4 | loop fusion | flops 12582912 | bytes 12582912 | tf_op jit(solution)/shard_map/concatenate | solution.py:112
  32.4 19.6 %shard_map.100 = bf16[64,128,512]{2,1,0:T(8,128)(2,1)} custom-call(s32[64]{0:T(128)} %get-tuple-element.19.src_ref, s32[64]{0:T(128)} %slice_bitcast_fusion.3.widx_ref, bf16[3072,1024]{1,0:T(8,128)(2,1)} %pad_maximum_fusion.1.x_ref, bf16[16,1024,512]{2,1,0:T(8,128)(2,1)} %w_ref.4), custom_call_target="tpu_custom_call" | custom-call | flops 8589934592 | bytes 31457280 | tf_op jit(solution)/shard_map/pallas_call | solution.py:41
  52.0 88.3 %all-to-all-done = bf16[64,128,512]{2,1,0:T(8,128)(2,1)} async-done(((bf16[64,128,512]{2,1,0:T(8,128)(2,1)}), bf16[64,128,512]{2,1,0:T(8,128)(2,1)}, u32[]{:S(2)}, u32[]{:S(2)}) %all-to-all-start) | async-done | bytes 8388640 | tf_op jit(solution)/shard_map/all_to_all | solution.py:155
  140.3 8.9 %all-to-all-start.1 = ((bf16[64,128,512]{2,1,0:T(8,128)(2,1)}), bf16[64,128,512]{2,1,0:T(8,128)(2,1)}, u32[]{:S(2)}, u32[]{:S(2)}) async-start(bf16[64,128,512]{2,1,0:T(8,128)(2,1)} %shard_map.100), calls=%async_computation.1 | async-start | bytes 16777216 | tf_op jit(solution)/shard_map/all_to_all | solution.py:161
  149.5 5.7 %reduce_sum.11 = s32[64,2,128]{2,1,0:T(2,128)S(1)} reduce(s32[1,64,2,128,128]{4,3,2,1,0:T(8,128)} %param.19, s32[]{:T(128)} %constant.4.clone.1), dimensions={0,4}, to_apply=%region_0.1 | reduce | flops 2080768 | bytes 8454148 | tf_op jit(solution)/shard_map/reduce_sum | solution.py:139
  156.2 2.6 copy.20.inv_ref
  158.8 2.6 copy.21.inv_ref
  161.5 0.5 slice_bitcast_fusion.widx_ref
  162.0 0.6 slice_bitcast_fusion.1
  162.6 0.5 iota.11.src_ref
  163.1 9.7 %shard_map.102 = f32[24,128,512]{2,1,0:T(8,128)} custom-call(s32[24]{0:T(128)} %iota.11.src_ref, s32[24]{0:T(128)} %widx_ref.1, bf16[3072,1024]{1,0:T(8,128)(2,1)} %pad_maximum_fusion.1.x_ref, bf16[3,1024,512]{2,1,0:T(8,128)(2,1)} %w_ref.5), custom_call_target="tpu_custom_call" | custom-call | flops 3221225472 | bytes 15728640 | tf_op jit(solution)/shard_map/pallas_call | solution.py:41
  172.8 6.5 %broadcast_select_fusion.1 = (bf16[64,128,512]{2,1,0:T(8,128)(2,1)S(1)}, bf16[64,128,512]{2,1,0:T(8,128)(2,1)S(1)}) fusion(bf16[64,128,512]{2,1,0:T(8,128)(2,1)} %all-to-all-done, bf16[64,128,512]{2,1,0:T(8,128)(2,1)} %collective-permute-done.1, pred[]{:T(512)S(6)} %eq.8), kind=kLoop, calls=%fused_computation.3 | loop fusion | flops 8388608 | bytes 33554432 | tf_op jit(solution)/shard_map/jit(_where)/select_n | solution.py:110
  179.3 7.0 %pad_maximum_fusion = bf16[64,128,1024]{2,1,0:T(8,128)(2,1)} fusion(bf16[64,128,512]{2,1,0:T(8,128)(2,1)S(1)} %get-tuple-element.10, bf16[64,128,512]{2,1,0:T(8,128)(2,1)S(1)} %get-tuple-element.9), kind=kLoop, calls=%fused_computation.1 | loop fusion | flops 33554432 | bytes 33554432 | tf_op jit(solution)/shard_map/concatenate | solution.py:112
  186.3 0.5 iota.10.src_ref
  186.8 22.5 %shard_map.101.msg_ref = bf16[64,128,512]{2,1,0:T(8,128)(2,1)} custom-call(s32[64]{0:T(128)} %iota.10.src_ref, s32[64]{0:T(128)} %slice_bitcast_fusion.widx_ref, bf16[8192,1024]{1,0:T(8,128)(2,1)} %bitcast.32, bf16[16,1024,512]{2,1,0:T(8,128)(2,1)} %w_ref.4), custom_call_target="tpu_custom_call" | custom-call | flops 8589934592 | bytes 41943040 | tf_op jit(solution)/shard_map/pallas_call | solution.py:41
  209.3 14.5 %shard_map.103.acc_in_ref = f32[3072,512]{1,0:T(8,128)} custom-call(s32[64]{0:T(128)} %get-tuple-element.22.tb_ref, s32[64]{0:T(128)} %get-tuple-element.15.live_ref, s32[64,2,128,128]{3,2,1,0:T(8,128)} %bitcast.30, bf16[64,128,512]{2,1,0:T(8,128)(2,1)} %shard_map.101.msg_ref, f32[64,128,1]{2,1,0:T(8,128)} %copy.20.inv_ref, f32[3072,512]{1,0:T(8,128)} %bitcast.34), custom_call_target="tpu_custom_call" | custom-call | flops 1073741824 | bytes 25198592 | tf_op jit(solution)/shard_map/pallas_call | solution.py:96
  223.8 51.4 %all-to-all-done.1.msg_ref = bf16[64,128,512]{2,1,0:T(8,128)(2,1)} async-done(((bf16[64,128,512]{2,1,0:T(8,128)(2,1)}), bf16[64,128,512]{2,1,0:T(8,128)(2,1)}, u32[]{:S(2)}, u32[]{:S(2)}) %all-to-all-start.1) | async-done | bytes 8388640 | tf_op jit(solution)/shard_map/all_to_all | solution.py:161
  275.2 13.9 %shard_map.104 = bf16[3072,512]{1,0:T(8,128)(2,1)} custom-call(s32[64]{0:T(128)} %get-tuple-element.21.tb_ref, s32[64]{0:T(128)} %get-tuple-element.16.live_ref, s32[64,2,128,128]{3,2,1,0:T(8,128)} %bitcast.31, bf16[64,128,512]{2,1,0:T(8,128)(2,1)} %all-to-all-done.1.msg_ref, f32[64,128,1]{2,1,0:T(8,128)} %copy.21.inv_ref, f32[3072,512]{1,0:T(8,128)} %shard_map.103.acc_in_ref), custom_call_target="tpu_custom_call" | custom-call | flops 1073741824 | bytes 22052864 | tf_op jit(solution)/shard_map/pallas_call | solution.py:96
  (22 shorter events, 1.4 us)
Async XLA Ops:
  8.7 11.9 %copy-start = (bf16[3072,512]{1,0:T(8,128)(2,1)S(1)}, bf16[3072,512]{1,0:T(8,128)(2,1)}, u32[]{:S(2)}) copy-start(bf16[3072,512]{1,0:T(8,128)(2,1)} %param.10) | copy-start | bytes 9437188
  8.7 12.0 %copy-start.4 = (s32[1,64,2]{1,2,0:T(2,128)S(1)}, s32[1,64,2]{1,2,0:T(2,128)}, u32[]{:S(2)}) copy-start(s32[1,64,2]{1,2,0:T(2,128)} %param.14) | copy-start | bytes 1540
  8.7 131.6 %all-to-all-start = ((bf16[64,128,512]{2,1,0:T(8,128)(2,1)}), bf16[64,128,512]{2,1,0:T(8,128)(2,1)}, u32[]{:S(2)}, u32[]{:S(2)}) async-start(bf16[64,128,512]{2,1,0:T(8,128)(2,1)} %gather_fusion), calls=%async_computation | async-start | bytes 16777216 | tf_op jit(solution)/shard_map/all_to_all | solution.py:155
  20.6 5.9 %collective-permute-start = (bf16[3072,512]{1,0:T(8,128)(2,1)S(1)}, bf16[3072,512]{1,0:T(8,128)(2,1)}, u32[]{:S(2)}, u32[]{:S(2)}) collective-permute-start(bf16[3072,512]{1,0:T(8,128)(2,1)S(1)} %copy-done), channel_id=1, source_target_pairs={{0,1},{1,0},{2,3},{3,2},{4,5},{5,4},{6,7},{7,6},{8,9},{9,8},{10,11... | collective-permute-start | bytes 9437192 | tf_op jit(solution)/shard_map/ppermute | solution.py:108
  52.0 97.3 %copy-start.2 = (s32[1,64,2]{1,2,0:T(2,128)S(1)}, s32[1,64,2]{1,2,0:T(2,128)}, u32[]{:S(2)}) copy-start(s32[1,64,2]{1,2,0:T(2,128)} %param.17) | copy-start | bytes 1540
  52.0 97.3 %copy-start.3 = (s32[1,64,2]{1,2,0:T(2,128)S(1)}, s32[1,64,2]{1,2,0:T(2,128)}, u32[]{:S(2)}) copy-start(s32[1,64,2]{1,2,0:T(2,128)} %param.16) | copy-start | bytes 1540
  140.3 32.5 %collective-permute-start.1 = (bf16[64,128,512]{2,1,0:T(8,128)(2,1)}, bf16[64,128,512]{2,1,0:T(8,128)(2,1)}, u32[]{:S(2)}, u32[]{:S(2)}) collective-permute-start(bf16[64,128,512]{2,1,0:T(8,128)(2,1)} %all-to-all-done), channel_id=1, source_target_pairs={{0,1},{1,0},{2,3},{3,2},{4,5},{5,4},{6,7},{7,6},{8,9},{9,8},{10,11... | collective-permute-start | bytes 25165832 | tf_op jit(solution)/shard_map/ppermute | solution.py:108
  140.3 134.9 %all-to-all-start.1 = ((bf16[64,128,512]{2,1,0:T(8,128)(2,1)}), bf16[64,128,512]{2,1,0:T(8,128)(2,1)}, u32[]{:S(2)}, u32[]{:S(2)}) async-start(bf16[64,128,512]{2,1,0:T(8,128)(2,1)} %shard_map.100), calls=%async_computation.1 | async-start | bytes 16777216 | tf_op jit(solution)/shard_map/all_to_all | solution.py:161
  149.2 5.9 %copy-start.1 = (s32[1,64,2]{1,2,0:T(2,128)S(1)}, s32[1,64,2]{1,2,0:T(2,128)}, u32[]{:S(2)}) copy-start(s32[1,64,2]{1,2,0:T(2,128)} %param.18) | copy-start | bytes 1540

commit v5 on v4

--- a/solution.py
+++ b/solution.py
@@ -49,14 +49,36 @@
     )(src, widx, x, w)
 
 
-def _agg_kernel(group, final, tb_ref, live_ref, tiles_ref, msg_ref, inv_ref, acc_in_ref, out_ref, *scratch):
+def _pick_kernel(group, src_ref, x_ref, o_ref):
     step = pl.program_id(0)
-    acc_ref = scratch[0] if final else out_ref
-
-    @pl.when(step == 0)
-    def _():
-        acc_ref[...] = acc_in_ref[...]
-
+    block_rows = o_ref.shape[1]
+    for j in range(group):
+        rows = pl.ds(pl.multiple_of(src_ref[step * group + j] * block_rows, block_rows), block_rows)
+        o_ref[j] = x_ref[rows, :]
+
+
+def _pick_blocks(x, src, block_rows, group=8):
+    steps = src.shape[0]
+    grid_spec = pltpu.PrefetchScalarGridSpec(
+        num_scalar_prefetch=1,
+        grid=(steps // group,),
+        in_specs=[pl.BlockSpec(x.shape, lambda i, r: (0, 0), pipeline_mode=pl.Buffered(1))],
+        out_specs=pl.BlockSpec((group, block_rows, x.shape[1]), lambda i, r: (i, 0, 0)),
+    )
+    return pl.pallas_call(
+        functools.partial(_pick_kernel, group),
+        grid_spec=grid_spec,
+        out_shape=jax.ShapeDtypeStruct((steps, block_rows, x.shape[1]), x.dtype),
+        compiler_params=pltpu.CompilerParams(dimension_semantics=("arbitrary",)),
+        cost_estimate=pl.CostEstimate(
+            flops=0, bytes_accessed=x.size * 2 + steps * block_rows * x.shape[1] * 2,
+            transcendentals=0,
+        ),
+    )(src, x)
+
+
+def _agg_kernel(group, final, tb_ref, live_ref, tiles_ref, msg_ref, inv_ref, acc_ref, out_ref):
+    step = pl.program_id(0)
     block_rows = msg_ref.shape[1]
     for j in range(group):
         slot = step * group + j
@@ -65,10 +87,9 @@
         rows = pl.ds(pl.multiple_of(tb_ref[slot] * block_rows, block_rows), block_rows)
         acc_ref[rows, :] += term
 
-    if final:
-        @pl.when(step == pl.num_programs(0) - 1)
-        def _():
-            out_ref[...] = acc_ref[...].astype(out_ref.dtype)
+    @pl.when(step == pl.num_programs(0) - 1)
+    def _():
+        out_ref[...] = acc_ref[...].astype(out_ref.dtype)
 
 
 def _aggregate(acc, tiles, msgs, inv, tb, live, k, final, group=8):
@@ -85,7 +106,6 @@
             pl.BlockSpec((rows, n_dim), lambda i, t, l: (0, 0), pipeline_mode=pl.Buffered(1)),
         ],
         out_specs=pl.BlockSpec((rows, n_dim), lambda i, t, l: (0, 0)),
-        scratch_shapes=[pltpu.VMEM((rows, n_dim), jnp.float32)] if final else [],
     )
     cost = pl.CostEstimate(
         flops=2 * steps * block_rows * block_rows * n_dim,
@@ -150,8 +170,7 @@
     src_rels = source_relation.reshape(partitions, capacity)
     dst_blocks = target_block.reshape(partitions, capacity)
 
-    feature_blocks = features.reshape(blk_count, block_rows, features.shape[1])
-    raw = feature_blocks[src_blocks[:, 0]]
+    raw = _pick_blocks(features, src_blocks[:, 0], block_rows)
     arrived = [lax.all_to_all(raw, "dom", split_axis=0, concat_axis=0, tiled=True)]
     for k in range(1, capacity):
         msgs = _block_matmul(

time: 292 us -> 291 us (level)
  Pallas kernels: 80.1 us -> 87 us
  local copies, waits for them, and re-layouts: 15.8 us -> 9.68 us
    gather x1 -> x0, local copies, waits for them, and re-layouts: 7.41 us -> none  [on_device(): raw = feature_blocks[src_blocks[:, 0]]]
    pallas_call x0 -> x1, Pallas kernels: none -> 7.26 us  [_pick_blocks(): pl.pallas_call(functools.partial(_pick_kernel, group), grid_spec=grid_spe...]
where the time goes in v5:
time: 291 us; the launch traced here: 289 us
  waiting for transfers between devices  145 us (50%)
  Pallas kernels  87 us (30%)
  other arithmetic  25.1 us (9%)
  starting transfers between devices  20.9 us (7%)
  local copies, waits for them, and re-layouts  9.68 us (3%)
    all_to_all x1, waiting for transfers between devices, on_device(): lax.all_to_all(raw, 'dom', split_axis=0, concat_axis=0, tiled=True)  88.3 us
    pallas_call x3, Pallas kernels, _block_matmul(): pl.pallas_call(functools.partial(_bmm_kernel, group), grid_spec=grid_spec...  51.7 us
    all_to_all x1, waiting for transfers between devices, on_device(): lax.all_to_all(msgs, 'dom', split_axis=0, concat_axis=0, tiled=True)  51.4 us
    pallas_call x2, Pallas kernels, _aggregate(): pl.pallas_call(functools.partial(_agg_kernel, group, final), grid_spec=gr...  28 us
    all_to_all x1, starting transfers between devices, on_device(): lax.all_to_all(raw, 'dom', split_axis=0, concat_axis=0, tiled=True)  11.9 us
    concatenate x2, other arithmetic, _widen(): return jnp.concatenate([low, high], axis=axis)  10.6 us
    all_to_all x1, starting transfers between devices, on_device(): lax.all_to_all(msgs, 'dom', split_axis=0, concat_axis=0, tiled=True)  8.92 us
    select_n x2, other arithmetic, _widen(): low = jnp.where(first, x, other)  8.78 us
  transfers between devices with their start and end apart: 4, of which 3 were waited for; matrix products, arithmetic and copies ran while one was open for 12% of the time, Pallas kernels for 23%

profile of v5, /device:TPU:4, one launch (start us, length us, event | category | flops | bytes accessed | tf_op | source)
XLA Modules:
  0.0 288.5 jit_solution(4469429103668261680)
XLA Ops:
  0.0 1.3 slice_bitcast_fusion.4
  1.3 7.3 %shard_map.100 = bf16[64,128,512]{2,1,0:T(8,128)(2,1)} custom-call(s32[64]{0:T(128)} %get-tuple-element.20.src_ref, bf16[3072,512]{1,0:T(8,128)(2,1)} %x_ref.1), custom_call_target="tpu_custom_call" | custom-call | bytes 11534336 | tf_op jit(solution)/shard_map/pallas_call | solution.py:68
  8.5 11.9 %all-to-all-start = ((bf16[64,128,512]{2,1,0:T(8,128)(2,1)}), bf16[64,128,512]{2,1,0:T(8,128)(2,1)}, u32[]{:S(2)}, u32[]{:S(2)}) async-start(bf16[64,128,512]{2,1,0:T(8,128)(2,1)} %shard_map.100), calls=%async_computation | async-start | bytes 16777216 | tf_op jit(solution)/shard_map/all_to_all | solution.py:174
  20.6 0.5 slice_bitcast_fusion.3.widx_ref
  21.1 5.3 %collective-permute-done = bf16[3072,512]{1,0:T(8,128)(2,1)} collective-permute-done((bf16[3072,512]{1,0:T(8,128)(2,1)S(1)}, bf16[3072,512]{1,0:T(8,128)(2,1)}, u32[]{:S(2)}, u32[]{:S(2)}) %collective-permute-start) | collective-permute-done | bytes 3145760 | tf_op jit(solution)/shard_map/ppermute | solution.py:128
  26.3 2.3 broadcast_select_fusion.3
  28.6 3.6 %pad_maximum_fusion.1.x_ref = bf16[3072,1024]{1,0:T(8,128)(2,1)} fusion(bf16[3072,512]{1,0:T(8,128)(2,1)S(1)} %get-tuple-element.12, bf16[3072,512]{1,0:T(8,128)(2,1)S(1)} %get-tuple-element.11), kind=kLoop, calls=%fused_computation.3 | loop fusion | flops 12582912 | bytes 12582912 | tf_op jit(solution)/shard_map/concatenate | solution.py:132
  32.3 19.5 %shard_map.101 = bf16[64,128,512]{2,1,0:T(8,128)(2,1)} custom-call(s32[64]{0:T(128)} %get-tuple-element.19.src_ref, s32[64]{0:T(128)} %slice_bitcast_fusion.3.widx_ref, bf16[3072,1024]{1,0:T(8,128)(2,1)} %pad_maximum_fusion.1.x_ref, bf16[16,1024,512]{2,1,0:T(8,128)(2,1)} %w_ref.4), custom_call_target="tpu_custom_call" | custom-call | flops 8589934592 | bytes 31457280 | tf_op jit(solution)/shard_map/pallas_call | solution.py:41
  51.8 88.3 %all-to-all-done = bf16[64,128,512]{2,1,0:T(8,128)(2,1)} async-done(((bf16[64,128,512]{2,1,0:T(8,128)(2,1)}), bf16[64,128,512]{2,1,0:T(8,128)(2,1)}, u32[]{:S(2)}, u32[]{:S(2)}) %all-to-all-start) | async-done | bytes 8388640 | tf_op jit(solution)/shard_map/all_to_all | solution.py:174
  140.2 8.9 %all-to-all-start.1 = ((bf16[64,128,512]{2,1,0:T(8,128)(2,1)}), bf16[64,128,512]{2,1,0:T(8,128)(2,1)}, u32[]{:S(2)}, u32[]{:S(2)}) async-start(bf16[64,128,512]{2,1,0:T(8,128)(2,1)} %shard_map.101), calls=%async_computation.1 | async-start | bytes 16777216 | tf_op jit(solution)/shard_map/all_to_all | solution.py:180
  149.4 5.7 %reduce_sum.11 = s32[64,2,128]{2,1,0:T(2,128)S(1)} reduce(s32[1,64,2,128,128]{4,3,2,1,0:T(8,128)} %param.19, s32[]{:T(128)} %constant.1.clone.1), dimensions={0,4}, to_apply=%region_0.1 | reduce | flops 2080768 | bytes 8454148 | tf_op jit(solution)/shard_map/reduce_sum | solution.py:159
  156.1 2.6 copy.20.inv_ref
  158.7 2.6 copy.21.inv_ref
  161.3 0.5 slice_bitcast_fusion.widx_ref
  161.8 0.6 slice_bitcast_fusion.1
  162.4 0.5 iota.11.src_ref
  162.9 9.7 %shard_map.103 = f32[24,128,512]{2,1,0:T(8,128)} custom-call(s32[24]{0:T(128)} %iota.11.src_ref, s32[24]{0:T(128)} %widx_ref.1, bf16[3072,1024]{1,0:T(8,128)(2,1)} %pad_maximum_fusion.1.x_ref, bf16[3,1024,512]{2,1,0:T(8,128)(2,1)} %w_ref.5), custom_call_target="tpu_custom_call" | custom-call | flops 3221225472 | bytes 15728640 | tf_op jit(solution)/shard_map/pallas_call | solution.py:41
  172.6 6.5 %broadcast_select_fusion.1 = (bf16[64,128,512]{2,1,0:T(8,128)(2,1)S(1)}, bf16[64,128,512]{2,1,0:T(8,128)(2,1)S(1)}) fusion(bf16[64,128,512]{2,1,0:T(8,128)(2,1)} %all-to-all-done, bf16[64,128,512]{2,1,0:T(8,128)(2,1)} %collective-permute-done.1, pred[]{:T(512)S(6)} %eq.8), kind=kLoop, calls=%fused_computation.2 | loop fusion | flops 8388608 | bytes 33554432 | tf_op jit(solution)/shard_map/jit(_where)/select_n | solution.py:130
  179.1 7.0 %pad_maximum_fusion = bf16[64,128,1024]{2,1,0:T(8,128)(2,1)} fusion(bf16[64,128,512]{2,1,0:T(8,128)(2,1)S(1)} %get-tuple-element.10, bf16[64,128,512]{2,1,0:T(8,128)(2,1)S(1)} %get-tuple-element.9), kind=kLoop, calls=%fused_computation | loop fusion | flops 33554432 | bytes 33554432 | tf_op jit(solution)/shard_map/concatenate | solution.py:132
  186.1 0.5 iota.10.src_ref
  186.6 22.5 %shard_map.102.msg_ref = bf16[64,128,512]{2,1,0:T(8,128)(2,1)} custom-call(s32[64]{0:T(128)} %iota.10.src_ref, s32[64]{0:T(128)} %slice_bitcast_fusion.widx_ref, bf16[8192,1024]{1,0:T(8,128)(2,1)} %bitcast.31, bf16[16,1024,512]{2,1,0:T(8,128)(2,1)} %w_ref.4), custom_call_target="tpu_custom_call" | custom-call | flops 8589934592 | bytes 41943040 | tf_op jit(solution)/shard_map/pallas_call | solution.py:41
  209.1 14.5 %shard_map.104.acc_ref = f32[3072,512]{1,0:T(8,128)} custom-call(s32[64]{0:T(128)} %get-tuple-element.22.tb_ref, s32[64]{0:T(128)} %get-tuple-element.15.live_ref, s32[64,2,128,128]{3,2,1,0:T(8,128)} %bitcast.29, bf16[64,128,512]{2,1,0:T(8,128)(2,1)} %shard_map.102.msg_ref, f32[64,128,1]{2,1,0:T(8,128)} %copy.20.inv_ref, f32[3072,512]{1,0:T(8,128)} %bitcast.32), custom_call_target="tpu_custom_call" | custom-call | flops 1073741824 | bytes 25198592 | tf_op jit(solution)/shard_map/pallas_call | solution.py:116
  223.7 51.4 %all-to-all-done.1.msg_ref = bf16[64,128,512]{2,1,0:T(8,128)(2,1)} async-done(((bf16[64,128,512]{2,1,0:T(8,128)(2,1)}), bf16[64,128,512]{2,1,0:T(8,128)(2,1)}, u32[]{:S(2)}, u32[]{:S(2)}) %all-to-all-start.1) | async-done | bytes 8388640 | tf_op jit(solution)/shard_map/all_to_all | solution.py:180
  275.0 13.5 %shard_map.105 = bf16[3072,512]{1,0:T(8,128)(2,1)} custom-call(s32[64]{0:T(128)} %get-tuple-element.21.tb_ref, s32[64]{0:T(128)} %get-tuple-element.16.live_ref, s32[64,2,128,128]{3,2,1,0:T(8,128)} %bitcast.30, bf16[64,128,512]{2,1,0:T(8,128)(2,1)} %all-to-all-done.1.msg_ref, f32[64,128,1]{2,1,0:T(8,128)} %copy.21.inv_ref, f32[3072,512]{1,0:T(8,128)} %shard_map.104.acc_ref), custom_call_target="tpu_custom_call" | custom-call | flops 1073741824 | bytes 22052864 | tf_op jit(solution)/shard_map/pallas_call | solution.py:116
  (21 shorter events, 1.4 us)
Async XLA Ops:
  8.5 11.9 %copy-start = (bf16[3072,512]{1,0:T(8,128)(2,1)S(1)}, bf16[3072,512]{1,0:T(8,128)(2,1)}, u32[]{:S(2)}) copy-start(bf16[3072,512]{1,0:T(8,128)(2,1)} %x_ref.1) | copy-start | bytes 9437188
  8.5 12.0 %copy-start.4 = (s32[1,64,2]{1,2,0:T(2,128)S(1)}, s32[1,64,2]{1,2,0:T(2,128)}, u32[]{:S(2)}) copy-start(s32[1,64,2]{1,2,0:T(2,128)} %param.14) | copy-start | bytes 1540
  8.5 131.6 %all-to-all-start = ((bf16[64,128,512]{2,1,0:T(8,128)(2,1)}), bf16[64,128,512]{2,1,0:T(8,128)(2,1)}, u32[]{:S(2)}, u32[]{:S(2)}) async-start(bf16[64,128,512]{2,1,0:T(8,128)(2,1)} %shard_map.100), calls=%async_computation | async-start | bytes 16777216 | tf_op jit(solution)/shard_map/all_to_all | solution.py:174
  20.5 5.9 %collective-permute-start = (bf16[3072,512]{1,0:T(8,128)(2,1)S(1)}, bf16[3072,512]{1,0:T(8,128)(2,1)}, u32[]{:S(2)}, u32[]{:S(2)}) collective-permute-start(bf16[3072,512]{1,0:T(8,128)(2,1)S(1)} %copy-done), channel_id=1, source_target_pairs={{0,1},{1,0},{2,3},{3,2},{4,5},{5,4},{6,7},{7,6},{8,9},{9,8},{10,11... | collective-permute-start | bytes 9437192 | tf_op jit(solution)/shard_map/ppermute | solution.py:128
  51.8 97.3 %copy-start.2 = (s32[1,64,2]{1,2,0:T(2,128)S(1)}, s32[1,64,2]{1,2,0:T(2,128)}, u32[]{:S(2)}) copy-start(s32[1,64,2]{1,2,0:T(2,128)} %param.17) | copy-start | bytes 1540
  51.8 97.3 %copy-start.3 = (s32[1,64,2]{1,2,0:T(2,128)S(1)}, s32[1,64,2]{1,2,0:T(2,128)}, u32[]{:S(2)}) copy-start(s32[1,64,2]{1,2,0:T(2,128)} %param.16) | copy-start | bytes 1540
  140.2 32.5 %collective-permute-start.1 = (bf16[64,128,512]{2,1,0:T(8,128)(2,1)}, bf16[64,128,512]{2,1,0:T(8,128)(2,1)}, u32[]{:S(2)}, u32[]{:S(2)}) collective-permute-start(bf16[64,128,512]{2,1,0:T(8,128)(2,1)} %all-to-all-done), channel_id=1, source_target_pairs={{0,1},{1,0},{2,3},{3,2},{4,5},{5,4},{6,7},{7,6},{8,9},{9,8},{10,11... | collective-permute-start | bytes 25165832 | tf_op jit(solution)/shard_map/ppermute | solution.py:128
  140.2 134.9 %all-to-all-start.1 = ((bf16[64,128,512]{2,1,0:T(8,128)(2,1)}), bf16[64,128,512]{2,1,0:T(8,128)(2,1)}, u32[]{:S(2)}, u32[]{:S(2)}) async-start(bf16[64,128,512]{2,1,0:T(8,128)(2,1)} %shard_map.101), calls=%async_computation.1 | async-start | bytes 16777216 | tf_op jit(solution)/shard_map/all_to_all | solution.py:180
  149.1 5.9 %copy-start.1 = (s32[1,64,2]{1,2,0:T(2,128)S(1)}, s32[1,64,2]{1,2,0:T(2,128)}, u32[]{:S(2)}) copy-start(s32[1,64,2]{1,2,0:T(2,128)} %param.18) | copy-start | bytes 1540

commit v6 on v5

--- a/solution.py
+++ b/solution.py
@@ -8,34 +8,43 @@
 from jax.sharding import PartitionSpec as P
 
 
-def _bmm_kernel(group, src_ref, widx_ref, x_ref, w_ref, o_ref):
+def _bmm_kernel(group, src_ref, widx_ref, col_ref, mine_ref, other_ref, w_ref, o_ref):
     step = pl.program_id(0)
     block_rows = o_ref.shape[1]
+    first = col_ref[0] == 0
     for j in range(group):
         slot = step * group + j
         rows = pl.ds(pl.multiple_of(src_ref[slot] * block_rows, block_rows), block_rows)
+        mine = mine_ref[rows, :]
+        other = other_ref[rows, :]
+        x = jnp.concatenate(
+            [jnp.where(first, mine, other), jnp.where(first, other, mine)], axis=1
+        )
         o_ref[j] = jnp.dot(
-            x_ref[rows, :], w_ref[widx_ref[slot]], preferred_element_type=jnp.float32
+            x, w_ref[widx_ref[slot]], preferred_element_type=jnp.float32
         ).astype(o_ref.dtype)
 
 
-def _block_matmul(x, w, src, widx, block_rows, out_dtype, group=8):
-    k_dim = x.shape[1]
+def _block_matmul(halves, w, src, widx, block_rows, out_dtype, group=8):
+    mine, other = halves
+    k_dim = 2 * mine.shape[1]
     n_dim = w.shape[2]
     steps = src.shape[0]
+    col = lax.axis_index("col").astype(jnp.int32).reshape(1)
     grid_spec = pltpu.PrefetchScalarGridSpec(
-        num_scalar_prefetch=2,
+        num_scalar_prefetch=3,
         grid=(steps // group,),
         in_specs=[
-            pl.BlockSpec(x.shape, lambda i, r, g: (0, 0), pipeline_mode=pl.Buffered(1)),
-            pl.BlockSpec(w.shape, lambda i, r, g: (0, 0, 0), pipeline_mode=pl.Buffered(1)),
+            pl.BlockSpec(mine.shape, lambda i, r, g, c: (0, 0), pipeline_mode=pl.Buffered(1)),
+            pl.BlockSpec(other.shape, lambda i, r, g, c: (0, 0), pipeline_mode=pl.Buffered(1)),
+            pl.BlockSpec(w.shape, lambda i, r, g, c: (0, 0, 0), pipeline_mode=pl.Buffered(1)),
         ],
-        out_specs=pl.BlockSpec((group, block_rows, n_dim), lambda i, r, g: (i, 0, 0)),
+        out_specs=pl.BlockSpec((group, block_rows, n_dim), lambda i, r, g, c: (i, 0, 0)),
     )
     out_bytes = jnp.dtype(out_dtype).itemsize
     cost = pl.CostEstimate(
         flops=2 * steps * block_rows * k_dim * n_dim,
-        bytes_accessed=x.size * 2 + w.size * 2 + steps * block_rows * n_dim * out_bytes,
+        bytes_accessed=mine.size * 4 + w.size * 2 + steps * block_rows * n_dim * out_bytes,
         transcendentals=0,
     )
     return pl.pallas_call(
@@ -46,7 +55,7 @@
             dimension_semantics=("arbitrary",), vmem_limit_bytes=56 * 1024 * 1024
         ),
         cost_estimate=cost,
-    )(src, widx, x, w)
+    )(src, widx, col, mine, other, w)
 
 
 def _pick_kernel(group, src_ref, x_ref, o_ref):
@@ -124,12 +133,8 @@
     )(tb, live, tiles, msgs, inv, acc)
 
 
-def _widen(x, axis):
-    other = lax.ppermute(x, "col", [(0, 1), (1, 0)])
-    first = lax.axis_index("col") == 0
-    low = jnp.where(first, x, other)
-    high = jnp.where(first, other, x)
-    return jnp.concatenate([low, high], axis=axis)
+def _with_partner(x):
+    return x, lax.ppermute(x, "col", [(0, 1), (1, 0)])
 
 
 def on_device(
@@ -152,7 +157,7 @@
     capacity = live.shape[2]
     slots = partitions * capacity
 
-    full_rows = _widen(features, 1)
+    full_rows = _with_partner(features)
 
     tiles4 = tiles.reshape(partitions, capacity, block_rows, block_rows)
     live2 = live.reshape(partitions, capacity)
@@ -188,9 +193,12 @@
         jnp.float32,
     )
     acc = selfs.reshape(rows_total, selfs.shape[2])
-    wide = _widen(arrived[0], 2)
+    mine, other = _with_partner(arrived[0])
     arrived[0] = _block_matmul(
-        wide.reshape(partitions * block_rows, wide.shape[2]),
+        (
+            mine.reshape(partitions * block_rows, mine.shape[2]),
+            other.reshape(partitions * block_rows, other.shape[2]),
+        ),
         rel_weight,
         jnp.arange(partitions, dtype=jnp.int32),
         target_relation.reshape(partitions, capacity)[:, 0],

time: 291 us -> 290 us (level)
  other arithmetic: 25.1 us -> 5.66 us
  waiting for transfers between devices: 145 us -> 164 us
    all_to_all x1, waiting for transfers between devices: 51.4 us -> 65 us  [on_device(): lax.all_to_all(msgs, 'dom', split_axis=0, concat_axis=0, tiled=True)]
    concatenate x2 -> x0, other arithmetic: 10.6 us -> none  [_widen(): return jnp.concatenate([low, high], axis=axis)]
    select_n x2 -> x0, other arithmetic: 8.78 us -> none  [_widen(): low = jnp.where(first, x, other)]
    all_to_all x1, waiting for transfers between devices: 88.3 us -> 94.2 us  [on_device(): lax.all_to_all(raw, 'dom', split_axis=0, concat_axis=0, tiled=True)]
  transfers between devices with their start and end apart: 4 -> 4, of which waited for: 3 -> 3; matrix products, arithmetic and copies ran while one was open for 12% -> 5% of each run, Pallas kernels for 23% -> 23%
where the time goes in v6:
time: 290 us; the launch traced here: 289 us
  waiting for transfers between devices  164 us (57%)
  Pallas kernels  87 us (30%)
  starting transfers between devices  20.9 us (7%)
  local copies, waits for them, and re-layouts  9.84 us (3%)
  other arithmetic  5.66 us (2%)
    all_to_all x1, waiting for transfers between devices, on_device(): lax.all_to_all(raw, 'dom', split_axis=0, concat_axis=0, tiled=True)  94.2 us
    all_to_all x1, waiting for transfers between devices, on_device(): lax.all_to_all(msgs, 'dom', split_axis=0, concat_axis=0, tiled=True)  65 us
    pallas_call x3, Pallas kernels, _block_matmul(): pl.pallas_call(functools.partial(_bmm_kernel, group), grid_spec=grid_spec...  51.7 us
    pallas_call x2, Pallas kernels, _aggregate(): pl.pallas_call(functools.partial(_agg_kernel, group, final), grid_spec=gr...  28 us
    all_to_all x1, starting transfers between devices, on_device(): lax.all_to_all(raw, 'dom', split_axis=0, concat_axis=0, tiled=True)  11.9 us
    all_to_all x1, starting transfers between devices, on_device(): lax.all_to_all(msgs, 'dom', split_axis=0, concat_axis=0, tiled=True)  8.9 us
    pallas_call x1, Pallas kernels, _pick_blocks(): pl.pallas_call(functools.partial(_pick_kernel, group), grid_spec=grid_spe...  7.23 us
  transfers between devices with their start and end apart: 4, of which 3 were waited for; matrix products, arithmetic and copies ran while one was open for 5% of the time, Pallas kernels for 23%

profile of v6, /device:TPU:4, one launch (start us, length us, event | category | flops | bytes accessed | tf_op | source)
XLA Modules:
  0.0 288.7 jit_solution(7671863569928211453)
XLA Ops:
  0.0 1.3 slice_bitcast_fusion.4
  1.3 7.2 %shard_map.100 = bf16[64,128,512]{2,1,0:T(8,128)(2,1)} custom-call(s32[64]{0:T(128)} %get-tuple-element.16.src_ref, bf16[3072,512]{1,0:T(8,128)(2,1)} %mine_ref.3), custom_call_target="tpu_custom_call" | custom-call | bytes 11534336 | tf_op jit(solution)/shard_map/pallas_call | solution.py:77
  8.6 11.9 %all-to-all-start = ((bf16[64,128,512]{2,1,0:T(8,128)(2,1)}), bf16[64,128,512]{2,1,0:T(8,128)(2,1)}, u32[]{:S(2)}, u32[]{:S(2)}) async-start(bf16[64,128,512]{2,1,0:T(8,128)(2,1)} %shard_map.100), calls=%async_computation | async-start | bytes 16777216 | tf_op jit(solution)/shard_map/all_to_all | solution.py:179
  20.6 0.6 slice_bitcast_fusion.3.widx_ref
  21.2 5.2 %collective-permute-done.other_ref = bf16[3072,512]{1,0:T(8,128)(2,1)} collective-permute-done((bf16[3072,512]{1,0:T(8,128)(2,1)S(1)}, bf16[3072,512]{1,0:T(8,128)(2,1)}, u32[]{:S(2)}, u32[]{:S(2)}) %collective-permute-start) | collective-permute-done | bytes 3145760 | tf_op jit(solution)/shard_map/ppermute | solution.py:137
  26.4 19.6 %shard_map.101 = bf16[64,128,512]{2,1,0:T(8,128)(2,1)} custom-call(s32[64]{0:T(128)} %get-tuple-element.15.src_ref, s32[64]{0:T(128)} %slice_bitcast_fusion.3.widx_ref, s32[1]{0:T(128)} %bitcast.10.col_ref, bf16[3072,512]{1,0:T(8,128)(2,1)} %mine_ref.3, bf16[3072,512]{1,0:T(8,128)(2,1)} %collective-permute-done.other_ref, bf16[16,1024,512]{2,1,0:T(8,128)(2,1)} %w_ref.4), custom_call_target="tpu_custom_call" | custom-call | flops 8589934592 | bytes 31457280 | tf_op jit(solution)/shard_map/pallas_call | solution.py:50
  46.0 94.2 %all-to-all-done = bf16[64,128,512]{2,1,0:T(8,128)(2,1)} async-done(((bf16[64,128,512]{2,1,0:T(8,128)(2,1)}), bf16[64,128,512]{2,1,0:T(8,128)(2,1)}, u32[]{:S(2)}, u32[]{:S(2)}) %all-to-all-start) | async-done | bytes 8388640 | tf_op jit(solution)/shard_map/all_to_all | solution.py:179
  140.2 8.9 %all-to-all-start.1 = ((bf16[64,128,512]{2,1,0:T(8,128)(2,1)}), bf16[64,128,512]{2,1,0:T(8,128)(2,1)}, u32[]{:S(2)}, u32[]{:S(2)}) async-start(bf16[64,128,512]{2,1,0:T(8,128)(2,1)} %shard_map.101), calls=%async_computation.1 | async-start | bytes 16777216 | tf_op jit(solution)/shard_map/all_to_all | solution.py:185
  149.2 0.1 add.11
  149.5 0.1 mul.24
  149.6 5.7 %reduce_sum.11 = s32[64,2,128]{2,1,0:T(2,128)S(1)} reduce(s32[1,64,2,128,128]{4,3,2,1,0:T(8,128)} %param.19, s32[]{:T(128)} %constant.3.clone.1), dimensions={0,4}, to_apply=%region_0.0 | reduce | flops 2080768 | bytes 8454148 | tf_op jit(solution)/shard_map/reduce_sum | solution.py:164
  155.3 0.4 fusion
  155.7 0.3 fusion.1
  156.1 2.6 copy.20.inv_ref
  158.7 2.6 copy.21.inv_ref
  161.3 0.6 slice_bitcast_fusion.widx_ref
  161.9 0.5 slice_bitcast_fusion.1
  162.5 0.5 iota.11.src_ref
  162.9 9.7 %shard_map.103 = f32[24,128,512]{2,1,0:T(8,128)} custom-call(s32[24]{0:T(128)} %iota.11.src_ref, s32[24]{0:T(128)} %widx_ref.1, s32[1]{0:T(128)} %bitcast.10.col_ref, bf16[3072,512]{1,0:T(8,128)(2,1)} %mine_ref.3, bf16[3072,512]{1,0:T(8,128)(2,1)} %collective-permute-done.other_ref, bf16[3,1024,512]{2,1,0:T(8,128)(2,1)} %w_ref.5), custom_call_target="tpu_custom_call" | custom-call | flops 3221225472 | bytes 15728640 | tf_op jit(solution)/shard_map/pallas_call | solution.py:50
  172.6 0.5 iota.10.src_ref
  173.1 22.5 %shard_map.102.msg_ref = bf16[64,128,512]{2,1,0:T(8,128)(2,1)} custom-call(s32[64]{0:T(128)} %iota.10.src_ref, s32[64]{0:T(128)} %slice_bitcast_fusion.widx_ref, s32[1]{0:T(128)} %bitcast.10.col_ref, bf16[8192,512]{1,0:T(8,128)(2,1)} %bitcast.18.mine_ref, bf16[8192,512]{1,0:T(8,128)(2,1)} %bitcast.19.other_ref, bf16[16,1024,512]{2,1,0:T(8,128)(2,1)} %w_ref.4), custom_call_target="tpu_custom_call" | custom-call | flops 8589934592 | bytes 41943040 | tf_op jit(solution)/shard_map/pallas_call | solution.py:50
  195.6 14.6 %shard_map.104.acc_ref = f32[3072,512]{1,0:T(8,128)} custom-call(s32[64]{0:T(128)} %get-tuple-element.18.tb_ref, s32[64]{0:T(128)} %get-tuple-element.11.live_ref, s32[64,2,128,128]{3,2,1,0:T(8,128)} %bitcast.31, bf16[64,128,512]{2,1,0:T(8,128)(2,1)} %shard_map.102.msg_ref, f32[64,128,1]{2,1,0:T(8,128)} %copy.20.inv_ref, f32[3072,512]{1,0:T(8,128)} %bitcast.33), custom_call_target="tpu_custom_call" | custom-call | flops 1073741824 | bytes 25198592 | tf_op jit(solution)/shard_map/pallas_call | solution.py:125
  210.2 65.0 %all-to-all-done.1.msg_ref = bf16[64,128,512]{2,1,0:T(8,128)(2,1)} async-done(((bf16[64,128,512]{2,1,0:T(8,128)(2,1)}), bf16[64,128,512]{2,1,0:T(8,128)(2,1)}, u32[]{:S(2)}, u32[]{:S(2)}) %all-to-all-start.1) | async-done | bytes 8388640 | tf_op jit(solution)/shard_map/all_to_all | solution.py:185
  275.2 13.5 %shard_map.105 = bf16[3072,512]{1,0:T(8,128)(2,1)} custom-call(s32[64]{0:T(128)} %get-tuple-element.17.tb_ref, s32[64]{0:T(128)} %get-tuple-element.12.live_ref, s32[64,2,128,128]{3,2,1,0:T(8,128)} %bitcast.32, bf16[64,128,512]{2,1,0:T(8,128)(2,1)} %all-to-all-done.1.msg_ref, f32[64,128,1]{2,1,0:T(8,128)} %copy.21.inv_ref, f32[3072,512]{1,0:T(8,128)} %shard_map.104.acc_ref), custom_call_target="tpu_custom_call" | custom-call | flops 1073741824 | bytes 22052864 | tf_op jit(solution)/shard_map/pallas_call | solution.py:125
  (17 shorter events, 0.4 us)
Async XLA Ops:
  8.6 11.9 %copy-start = (bf16[3072,512]{1,0:T(8,128)(2,1)S(1)}, bf16[3072,512]{1,0:T(8,128)(2,1)}, u32[]{:S(2)}) copy-start(bf16[3072,512]{1,0:T(8,128)(2,1)} %mine_ref.3) | copy-start | bytes 9437188
  8.6 12.0 %copy-start.4 = (s32[1,64,2]{1,2,0:T(2,128)S(1)}, s32[1,64,2]{1,2,0:T(2,128)}, u32[]{:S(2)}) copy-start(s32[1,64,2]{1,2,0:T(2,128)} %param.14) | copy-start | bytes 1540
  8.6 131.6 %all-to-all-start = ((bf16[64,128,512]{2,1,0:T(8,128)(2,1)}), bf16[64,128,512]{2,1,0:T(8,128)(2,1)}, u32[]{:S(2)}, u32[]{:S(2)}) async-start(bf16[64,128,512]{2,1,0:T(8,128)(2,1)} %shard_map.100), calls=%async_computation | async-start | bytes 16777216 | tf_op jit(solution)/shard_map/all_to_all | solution.py:179
  20.5 5.9 %collective-permute-start = (bf16[3072,512]{1,0:T(8,128)(2,1)S(1)}, bf16[3072,512]{1,0:T(8,128)(2,1)}, u32[]{:S(2)}, u32[]{:S(2)}) collective-permute-start(bf16[3072,512]{1,0:T(8,128)(2,1)S(1)} %copy-done), channel_id=1, source_target_pairs={{0,1},{1,0},{2,3},{3,2},{4,5},{5,4},{6,7},{7,6},{8,9},{9,8},{10,11... | collective-permute-start | bytes 9437192 | tf_op jit(solution)/shard_map/ppermute | solution.py:137
  45.9 103.2 %copy-start.2 = (s32[1,64,2]{1,2,0:T(2,128)S(1)}, s32[1,64,2]{1,2,0:T(2,128)}, u32[]{:S(2)}) copy-start(s32[1,64,2]{1,2,0:T(2,128)} %param.17) | copy-start | bytes 1540
  45.9 103.2 %copy-start.3 = (s32[1,64,2]{1,2,0:T(2,128)S(1)}, s32[1,64,2]{1,2,0:T(2,128)}, u32[]{:S(2)}) copy-start(s32[1,64,2]{1,2,0:T(2,128)} %param.16) | copy-start | bytes 1540
  46.0 103.4 %copy-start.1 = (s32[1,64,2]{1,2,0:T(2,128)S(1)}, s32[1,64,2]{1,2,0:T(2,128)}, u32[]{:S(2)}) copy-start(s32[1,64,2]{1,2,0:T(2,128)} %param.18) | copy-start | bytes 1540
  140.2 32.4 %collective-permute-start.1 = (bf16[64,128,512]{2,1,0:T(8,128)(2,1)}, bf16[64,128,512]{2,1,0:T(8,128)(2,1)}, u32[]{:S(2)}, u32[]{:S(2)}) collective-permute-start(bf16[64,128,512]{2,1,0:T(8,128)(2,1)} %all-to-all-done), channel_id=1, source_target_pairs={{0,1},{1,0},{2,3},{3,2},{4,5},{5,4},{6,7},{7,6},{8,9},{9,8},{10,11... | collective-permute-start | bytes 25165832 | tf_op jit(solution)/shard_map/ppermute | solution.py:137
  140.2 135.0 %all-to-all-start.1 = ((bf16[64,128,512]{2,1,0:T(8,128)(2,1)}), bf16[64,128,512]{2,1,0:T(8,128)(2,1)}, u32[]{:S(2)}, u32[]{:S(2)}) async-start(bf16[64,128,512]{2,1,0:T(8,128)(2,1)} %shard_map.101), calls=%async_computation.1 | async-start | bytes 16777216 | tf_op jit(solution)/shard_map/all_to_all | solution.py:185

commit v7 on v6

--- a/solution.py
+++ b/solution.py
@@ -86,13 +86,12 @@
     )(src, x)
 
 
-def _agg_kernel(group, final, tb_ref, live_ref, tiles_ref, msg_ref, inv_ref, acc_ref, out_ref):
+def _agg_kernel(group, final, tb_ref, adj_ref, msg_ref, inv_ref, acc_ref, out_ref):
     step = pl.program_id(0)
     block_rows = msg_ref.shape[1]
     for j in range(group):
         slot = step * group + j
-        adj = (tiles_ref[j] * live_ref[slot]).astype(jnp.float32).astype(jnp.bfloat16)
-        term = jnp.dot(adj, msg_ref[j], preferred_element_type=jnp.float32) * inv_ref[j]
+        term = jnp.dot(adj_ref[j], msg_ref[j], preferred_element_type=jnp.float32) * inv_ref[j]
         rows = pl.ds(pl.multiple_of(tb_ref[slot] * block_rows, block_rows), block_rows)
         acc_ref[rows, :] += term
 
@@ -101,24 +100,24 @@
         out_ref[...] = acc_ref[...].astype(out_ref.dtype)
 
 
-def _aggregate(acc, tiles, msgs, inv, tb, live, k, final, group=8):
+def _aggregate(acc, adj, msgs, inv, tb, k, final, group=16):
     steps, block_rows, n_dim = msgs.shape
     rows = acc.shape[0]
     out_dtype = jnp.bfloat16 if final else jnp.float32
     grid_spec = pltpu.PrefetchScalarGridSpec(
-        num_scalar_prefetch=2,
+        num_scalar_prefetch=1,
         grid=(steps // group,),
         in_specs=[
-            pl.BlockSpec((group, None, block_rows, block_rows), lambda i, t, l: (i, k, 0, 0)),
-            pl.BlockSpec((group, block_rows, n_dim), lambda i, t, l: (i, 0, 0)),
-            pl.BlockSpec((group, block_rows, 1), lambda i, t, l: (i, 0, 0)),
-            pl.BlockSpec((rows, n_dim), lambda i, t, l: (0, 0), pipeline_mode=pl.Buffered(1)),
+            pl.BlockSpec((group, None, block_rows, block_rows), lambda i, t: (i, k, 0, 0)),
+            pl.BlockSpec((group, block_rows, n_dim), lambda i, t: (i, 0, 0)),
+            pl.BlockSpec((group, block_rows, 1), lambda i, t: (i, 0, 0)),
+            pl.BlockSpec((rows, n_dim), lambda i, t: (0, 0), pipeline_mode=pl.Buffered(1)),
         ],
-        out_specs=pl.BlockSpec((rows, n_dim), lambda i, t, l: (0, 0)),
+        out_specs=pl.BlockSpec((rows, n_dim), lambda i, t: (0, 0)),
     )
     cost = pl.CostEstimate(
         flops=2 * steps * block_rows * block_rows * n_dim,
-        bytes_accessed=steps * block_rows * (block_rows * 4 + n_dim * 2 + 4)
+        bytes_accessed=steps * block_rows * (block_rows * 2 + n_dim * 2 + 4)
         + rows * n_dim * (4 + jnp.dtype(out_dtype).itemsize),
         transcendentals=0,
     )
@@ -130,7 +129,7 @@
             dimension_semantics=("arbitrary",), vmem_limit_bytes=56 * 1024 * 1024
         ),
         cost_estimate=cost,
-    )(tb, live, tiles, msgs, inv, acc)
+    )(tb, adj, msgs, inv, acc)
 
 
 def _with_partner(x):
@@ -205,14 +204,14 @@
         block_rows,
         jnp.bfloat16,
     )
+    adjacency = (tiles4 * live2[:, :, None, None]).astype(jnp.bfloat16)
     for k in range(capacity):
         acc = _aggregate(
             acc,
-            tiles4,
+            adjacency,
             arrived[k],
             scale[:, k],
             dst_blocks[:, k],
-            live2[:, k],
             k,
             final=k == capacity - 1,
         )

time: 290 us -> 289 us (level)
  other arithmetic: 5.66 us -> 12 us
  Pallas kernels: 87 us -> 82.6 us
  waiting for transfers between devices: 164 us -> 160 us
    convert_element_type x0 -> x1, other arithmetic: none -> 6.35 us  [on_device(): adjacency = (tiles4 * live2[:, :, None, None]).astype(jnp.bfloat16)]
    all_to_all x1, waiting for transfers between devices: 65 us -> 60.5 us  [on_device(): lax.all_to_all(msgs, 'dom', split_axis=0, concat_axis=0, tiled=True)]
    pallas_call x2, Pallas kernels: 28 us -> 23.7 us  [_aggregate(): pl.pallas_call(functools.partial(_agg_kernel, group, final), grid_spec=gr...]
  transfers between devices with their start and end apart: 4 -> 4, of which waited for: 3 -> 3; matrix products, arithmetic and copies ran while one was open for 5% -> 7% of each run, Pallas kernels for 23% -> 22%
where the time goes in v7:
time: 289 us; the launch traced here: 286 us
  waiting for transfers between devices  160 us (55%)
  Pallas kernels  82.6 us (29%)
  starting transfers between devices  20.9 us (7%)
  other arithmetic  12 us (4%)
  local copies, waits for them, and re-layouts  10.1 us (3%)
    all_to_all x1, waiting for transfers between devices, on_device(): lax.all_to_all(raw, 'dom', split_axis=0, concat_axis=0, tiled=True)  94.2 us
    all_to_all x1, waiting for transfers between devices, on_device(): lax.all_to_all(msgs, 'dom', split_axis=0, concat_axis=0, tiled=True)  60.5 us
    pallas_call x3, Pallas kernels, _block_matmul(): pl.pallas_call(functools.partial(_bmm_kernel, group), grid_spec=grid_spec...  51.7 us
    pallas_call x2, Pallas kernels, _aggregate(): pl.pallas_call(functools.partial(_agg_kernel, group, final), grid_spec=gr...  23.7 us
    all_to_all x1, starting transfers between devices, on_device(): lax.all_to_all(raw, 'dom', split_axis=0, concat_axis=0, tiled=True)  11.9 us
    all_to_all x1, starting transfers between devices, on_device(): lax.all_to_all(msgs, 'dom', split_axis=0, concat_axis=0, tiled=True)  8.91 us
    pallas_call x1, Pallas kernels, _pick_blocks(): pl.pallas_call(functools.partial(_pick_kernel, group), grid_spec=grid_spe...  7.23 us
    convert_element_type x1, other arithmetic, on_device(): adjacency = (tiles4 * live2[:, :, None, None]).astype(jnp.bfloat16)  6.35 us
  transfers between devices with their start and end apart: 4, of which 3 were waited for; matrix products, arithmetic and copies ran while one was open for 7% of the time, Pallas kernels for 22%

profile of v7, /device:TPU:4, one launch (start us, length us, event | category | flops | bytes accessed | tf_op | source)
XLA Modules:
  0.0 286.4 jit_solution(15400877585612257217)
XLA Ops:
  0.0 1.3 slice_bitcast_fusion.3
  1.3 7.2 %shard_map.100 = bf16[64,128,512]{2,1,0:T(8,128)(2,1)} custom-call(s32[64]{0:T(128)} %get-tuple-element.14.src_ref, bf16[3072,512]{1,0:T(8,128)(2,1)} %mine_ref.3), custom_call_target="tpu_custom_call" | custom-call | bytes 11534336 | tf_op jit(solution)/shard_map/pallas_call | solution.py:77
  8.6 11.9 %all-to-all-start = ((bf16[64,128,512]{2,1,0:T(8,128)(2,1)}), bf16[64,128,512]{2,1,0:T(8,128)(2,1)}, u32[]{:S(2)}, u32[]{:S(2)}) async-start(bf16[64,128,512]{2,1,0:T(8,128)(2,1)} %shard_map.100), calls=%async_computation | async-start | bytes 16777216 | tf_op jit(solution)/shard_map/all_to_all | solution.py:178
  20.6 0.6 slice_bitcast_fusion.2.widx_ref
  21.2 5.2 %collective-permute-done.other_ref = bf16[3072,512]{1,0:T(8,128)(2,1)} collective-permute-done((bf16[3072,512]{1,0:T(8,128)(2,1)S(1)}, bf16[3072,512]{1,0:T(8,128)(2,1)}, u32[]{:S(2)}, u32[]{:S(2)}) %collective-permute-start) | collective-permute-done | bytes 3145760 | tf_op jit(solution)/shard_map/ppermute | solution.py:136
  26.4 19.6 %shard_map.101 = bf16[64,128,512]{2,1,0:T(8,128)(2,1)} custom-call(s32[64]{0:T(128)} %get-tuple-element.13.src_ref, s32[64]{0:T(128)} %slice_bitcast_fusion.2.widx_ref, s32[1]{0:T(128)} %bitcast.9.col_ref, bf16[3072,512]{1,0:T(8,128)(2,1)} %mine_ref.3, bf16[3072,512]{1,0:T(8,128)(2,1)} %collective-permute-done.other_ref, bf16[16,1024,512]{2,1,0:T(8,128)(2,1)} %w_ref.4), custom_call_target="tpu_custom_call" | custom-call | flops 8589934592 | bytes 31457280 | tf_op jit(solution)/shard_map/pallas_call | solution.py:50
  46.0 94.2 %all-to-all-done = bf16[64,128,512]{2,1,0:T(8,128)(2,1)} async-done(((bf16[64,128,512]{2,1,0:T(8,128)(2,1)}), bf16[64,128,512]{2,1,0:T(8,128)(2,1)}, u32[]{:S(2)}, u32[]{:S(2)}) %all-to-all-start) | async-done | bytes 8388640 | tf_op jit(solution)/shard_map/all_to_all | solution.py:178
  140.2 8.9 %all-to-all-start.1 = ((bf16[64,128,512]{2,1,0:T(8,128)(2,1)}), bf16[64,128,512]{2,1,0:T(8,128)(2,1)}, u32[]{:S(2)}, u32[]{:S(2)}) async-start(bf16[64,128,512]{2,1,0:T(8,128)(2,1)} %shard_map.101), calls=%async_computation.1 | async-start | bytes 16777216 | tf_op jit(solution)/shard_map/all_to_all | solution.py:184
  149.2 0.1 add.11
  149.6 5.7 %reduce_sum.11 = s32[64,2,128]{2,1,0:T(2,128)S(1)} reduce(s32[1,64,2,128,128]{4,3,2,1,0:T(8,128)} %param.19, s32[]{:T(128)} %constant.3.clone.1), dimensions={0,4}, to_apply=%region_0.0 | reduce | flops 2080768 | bytes 8454148 | tf_op jit(solution)/shard_map/reduce_sum | solution.py:163
  155.3 0.4 fusion.1
  155.7 0.3 fusion.2
  156.1 2.7 copy.23.inv_ref
  158.9 2.6 copy.24.inv_ref
  161.5 0.5 slice_bitcast_fusion.widx_ref
  162.0 0.6 slice_bitcast_fusion.1
  162.6 6.3 %fusion.adj_ref = bf16[64,2,128,128]{3,2,1,0:T(8,128)(2,1)} fusion(s32[1,64,2,128,128]{4,3,2,1,0:T(8,128)} %param.19, s32[64,2]{1,0:T(8,128)S(1)} %copy.20), kind=kLoop, calls=%fused_computation.1 | loop fusion | flops 4194304 | bytes 12583424 | tf_op jit(solution)/shard_map/convert_element_type | solution.py:207
  169.0 0.5 iota.11.src_ref
  169.5 9.7 %shard_map.103 = f32[24,128,512]{2,1,0:T(8,128)} custom-call(s32[24]{0:T(128)} %iota.11.src_ref, s32[24]{0:T(128)} %widx_ref.1, s32[1]{0:T(128)} %bitcast.9.col_ref, bf16[3072,512]{1,0:T(8,128)(2,1)} %mine_ref.3, bf16[3072,512]{1,0:T(8,128)(2,1)} %collective-permute-done.other_ref, bf16[3,1024,512]{2,1,0:T(8,128)(2,1)} %w_ref.5), custom_call_target="tpu_custom_call" | custom-call | flops 3221225472 | bytes 15728640 | tf_op jit(solution)/shard_map/pallas_call | solution.py:50
  179.1 0.6 iota.10.src_ref
  179.7 22.5 %shard_map.102.msg_ref = bf16[64,128,512]{2,1,0:T(8,128)(2,1)} custom-call(s32[64]{0:T(128)} %iota.10.src_ref, s32[64]{0:T(128)} %slice_bitcast_fusion.widx_ref, s32[1]{0:T(128)} %bitcast.9.col_ref, bf16[8192,512]{1,0:T(8,128)(2,1)} %bitcast.16.mine_ref, bf16[8192,512]{1,0:T(8,128)(2,1)} %bitcast.17.other_ref, bf16[16,1024,512]{2,1,0:T(8,128)(2,1)} %w_ref.4), custom_call_target="tpu_custom_call" | custom-call | flops 8589934592 | bytes 41943040 | tf_op jit(solution)/shard_map/pallas_call | solution.py:50
  202.2 12.4 %shard_map.104.acc_ref = f32[3072,512]{1,0:T(8,128)} custom-call(s32[64]{0:T(128)} %get-tuple-element.11.tb_ref, bf16[64,2,128,128]{3,2,1,0:T(8,128)(2,1)} %fusion.adj_ref, bf16[64,128,512]{2,1,0:T(8,128)(2,1)} %shard_map.102.msg_ref, f32[64,128,1]{2,1,0:T(8,128)} %copy.23.inv_ref, f32[3072,512]{1,0:T(8,128)} %bitcast.30), custom_call_target="tpu_custom_call" | custom-call | flops 1073741824 | bytes 23101440 | tf_op jit(solution)/shard_map/pallas_call | solution.py:124
  214.5 60.5 %all-to-all-done.1.msg_ref = bf16[64,128,512]{2,1,0:T(8,128)(2,1)} async-done(((bf16[64,128,512]{2,1,0:T(8,128)(2,1)}), bf16[64,128,512]{2,1,0:T(8,128)(2,1)}, u32[]{:S(2)}, u32[]{:S(2)}) %all-to-all-start.1) | async-done | bytes 8388640 | tf_op jit(solution)/shard_map/all_to_all | solution.py:184
  275.1 11.3 %shard_map.105 = bf16[3072,512]{1,0:T(8,128)(2,1)} custom-call(s32[64]{0:T(128)} %get-tuple-element.12.tb_ref, bf16[64,2,128,128]{3,2,1,0:T(8,128)(2,1)} %fusion.adj_ref, bf16[64,128,512]{2,1,0:T(8,128)(2,1)} %all-to-all-done.1.msg_ref, f32[64,128,1]{2,1,0:T(8,128)} %copy.24.inv_ref, f32[3072,512]{1,0:T(8,128)} %shard_map.104.acc_ref), custom_call_target="tpu_custom_call" | custom-call | flops 1073741824 | bytes 19955712 | tf_op jit(solution)/shard_map/pallas_call | solution.py:124
  (19 shorter events, 0.6 us)
Async XLA Ops:
  8.6 11.9 %copy-start = (bf16[3072,512]{1,0:T(8,128)(2,1)S(1)}, bf16[3072,512]{1,0:T(8,128)(2,1)}, u32[]{:S(2)}) copy-start(bf16[3072,512]{1,0:T(8,128)(2,1)} %mine_ref.3) | copy-start | bytes 9437188
  8.6 12.0 %copy-start.4 = (s32[1,64,2]{1,2,0:T(2,128)S(1)}, s32[1,64,2]{1,2,0:T(2,128)}, u32[]{:S(2)}) copy-start(s32[1,64,2]{1,2,0:T(2,128)} %param.14) | copy-start | bytes 1540
  8.6 131.6 %all-to-all-start = ((bf16[64,128,512]{2,1,0:T(8,128)(2,1)}), bf16[64,128,512]{2,1,0:T(8,128)(2,1)}, u32[]{:S(2)}, u32[]{:S(2)}) async-start(bf16[64,128,512]{2,1,0:T(8,128)(2,1)} %shard_map.100), calls=%async_computation | async-start | bytes 16777216 | tf_op jit(solution)/shard_map/all_to_all | solution.py:178
  20.5 5.9 %collective-permute-start = (bf16[3072,512]{1,0:T(8,128)(2,1)S(1)}, bf16[3072,512]{1,0:T(8,128)(2,1)}, u32[]{:S(2)}, u32[]{:S(2)}) collective-permute-start(bf16[3072,512]{1,0:T(8,128)(2,1)S(1)} %copy-done), channel_id=1, source_target_pairs={{0,1},{1,0},{2,3},{3,2},{4,5},{5,4},{6,7},{7,6},{8,9},{9,8},{10,11... | collective-permute-start | bytes 9437192 | tf_op jit(solution)/shard_map/ppermute | solution.py:136
  45.9 103.2 %copy-start.2 = (s32[1,64,2]{1,2,0:T(2,128)S(1)}, s32[1,64,2]{1,2,0:T(2,128)}, u32[]{:S(2)}) copy-start(s32[1,64,2]{1,2,0:T(2,128)} %param.17) | copy-start | bytes 1540
  45.9 103.2 %copy-start.3 = (s32[1,64,2]{1,2,0:T(2,128)S(1)}, s32[1,64,2]{1,2,0:T(2,128)}, u32[]{:S(2)}) copy-start(s32[1,64,2]{1,2,0:T(2,128)} %param.16) | copy-start | bytes 1540
  46.0 103.4 %copy-start.1 = (s32[1,64,2]{1,2,0:T(2,128)S(1)}, s32[1,64,2]{1,2,0:T(2,128)}, u32[]{:S(2)}) copy-start(s32[1,64,2]{1,2,0:T(2,128)} %param.18) | copy-start | bytes 1540
  140.2 39.0 %collective-permute-start.1 = (bf16[64,128,512]{2,1,0:T(8,128)(2,1)}, bf16[64,128,512]{2,1,0:T(8,128)(2,1)}, u32[]{:S(2)}, u32[]{:S(2)}) collective-permute-start(bf16[64,128,512]{2,1,0:T(8,128)(2,1)} %all-to-all-done), channel_id=1, source_target_pairs={{0,1},{1,0},{2,3},{3,2},{4,5},{5,4},{6,7},{7,6},{8,9},{9,8},{10,11... | collective-permute-start | bytes 25165832 | tf_op jit(solution)/shard_map/ppermute | solution.py:136
  140.2 134.9 %all-to-all-start.1 = ((bf16[64,128,512]{2,1,0:T(8,128)(2,1)}), bf16[64,128,512]{2,1,0:T(8,128)(2,1)}, u32[]{:S(2)}, u32[]{:S(2)}) async-start(bf16[64,128,512]{2,1,0:T(8,128)(2,1)} %shard_map.101), calls=%async_computation.1 | async-start | bytes 16777216 | tf_op jit(solution)/shard_map/all_to_all | solution.py:184

commit v8 on v7

--- a/solution.py
+++ b/solution.py
@@ -58,12 +58,17 @@
     )(src, widx, col, mine, other, w)
 
 
-def _pick_kernel(group, src_ref, x_ref, o_ref):
+def _pick_kernel(group, src_ref, x_hbm, o_ref, sems):
     step = pl.program_id(0)
     block_rows = o_ref.shape[1]
+    copies = []
     for j in range(group):
         rows = pl.ds(pl.multiple_of(src_ref[step * group + j] * block_rows, block_rows), block_rows)
-        o_ref[j] = x_ref[rows, :]
+        copy = pltpu.make_async_copy(x_hbm.at[rows, :], o_ref.at[j], sems.at[j])
+        copy.start()
+        copies.append(copy)
+    for copy in copies:
+        copy.wait()
 
 
 def _pick_blocks(x, src, block_rows, group=8):
@@ -71,8 +76,9 @@
     grid_spec = pltpu.PrefetchScalarGridSpec(
         num_scalar_prefetch=1,
         grid=(steps // group,),
-        in_specs=[pl.BlockSpec(x.shape, lambda i, r: (0, 0), pipeline_mode=pl.Buffered(1))],
+        in_specs=[pl.BlockSpec(memory_space=pl.ANY)],
         out_specs=pl.BlockSpec((group, block_rows, x.shape[1]), lambda i, r: (i, 0, 0)),
+        scratch_shapes=[pltpu.SemaphoreType.DMA((group,))],
     )
     return pl.pallas_call(
         functools.partial(_pick_kernel, group),
@@ -80,8 +86,7 @@
         out_shape=jax.ShapeDtypeStruct((steps, block_rows, x.shape[1]), x.dtype),
         compiler_params=pltpu.CompilerParams(dimension_semantics=("arbitrary",)),
         cost_estimate=pl.CostEstimate(
-            flops=0, bytes_accessed=x.size * 2 + steps * block_rows * x.shape[1] * 2,
-            transcendentals=0,
+            flops=0, bytes_accessed=2 * steps * block_rows * x.shape[1] * 2, transcendentals=0
         ),
     )(src, x)
 

time: 289 us -> 297 us (1.028)
  Pallas kernels: 82.6 us -> 89.9 us
    pallas_call x1, Pallas kernels: 7.23 us -> 14.5 us  [_pick_blocks(): pl.pallas_call(functools.partial(_pick_kernel, group), grid_spec=grid_spe...]
where the time goes in v8:
time: 297 us; the launch traced here: 294 us
  waiting for transfers between devices  160 us (54%)
  Pallas kernels  89.9 us (30%)
  starting transfers between devices  20.9 us (7%)
  other arithmetic  12 us (4%)
  local copies, waits for them, and re-layouts  10.1 us (3%)
    all_to_all x1, waiting for transfers between devices, on_device(): lax.all_to_all(raw, 'dom', split_axis=0, concat_axis=0, tiled=True)  94.2 us
    all_to_all x1, waiting for transfers between devices, on_device(): lax.all_to_all(msgs, 'dom', split_axis=0, concat_axis=0, tiled=True)  60.5 us
    pallas_call x3, Pallas kernels, _block_matmul(): pl.pallas_call(functools.partial(_bmm_kernel, group), grid_spec=grid_spec...  51.7 us
    pallas_call x2, Pallas kernels, _aggregate(): pl.pallas_call(functools.partial(_agg_kernel, group, final), grid_spec=gr...  23.6 us
    pallas_call x1, Pallas kernels, _pick_blocks(): pl.pallas_call(functools.partial(_pick_kernel, group), grid_spec=grid_spe...  14.5 us
    all_to_all x1, starting transfers between devices, on_device(): lax.all_to_all(raw, 'dom', split_axis=0, concat_axis=0, tiled=True)  11.9 us
    all_to_all x1, starting transfers between devices, on_device(): lax.all_to_all(msgs, 'dom', split_axis=0, concat_axis=0, tiled=True)  8.91 us
    convert_element_type x1, other arithmetic, on_device(): adjacency = (tiles4 * live2[:, :, None, None]).astype(jnp.bfloat16)  6.35 us
  transfers between devices with their start and end apart: 4, of which 3 were waited for; matrix products, arithmetic and copies ran while one was open for 7% of the time, Pallas kernels for 22%

profile of v8, /device:TPU:4, one launch (start us, length us, event | category | flops | bytes accessed | tf_op | source)
XLA Modules:
  0.0 293.7 jit_solution(16281149525775759844)
XLA Ops:
  0.0 1.3 slice_bitcast_fusion.3
  1.3 14.5 %shard_map.100 = bf16[64,128,512]{2,1,0:T(8,128)(2,1)} custom-call(s32[64]{0:T(128)} %get-tuple-element.14.src_ref, bf16[3072,512]{1,0:T(8,128)(2,1)} %mine_ref.3), custom_call_target="tpu_custom_call" | custom-call | bytes 16777216 | tf_op jit(solution)/shard_map/pallas_call | solution.py:83
  15.9 11.9 %all-to-all-start = ((bf16[64,128,512]{2,1,0:T(8,128)(2,1)}), bf16[64,128,512]{2,1,0:T(8,128)(2,1)}, u32[]{:S(2)}, u32[]{:S(2)}) async-start(bf16[64,128,512]{2,1,0:T(8,128)(2,1)} %shard_map.100), calls=%async_computation | async-start | bytes 16777216 | tf_op jit(solution)/shard_map/all_to_all | solution.py:183
  28.0 0.6 slice_bitcast_fusion.2.widx_ref
  28.6 5.2 %collective-permute-done.other_ref = bf16[3072,512]{1,0:T(8,128)(2,1)} collective-permute-done((bf16[3072,512]{1,0:T(8,128)(2,1)S(1)}, bf16[3072,512]{1,0:T(8,128)(2,1)}, u32[]{:S(2)}, u32[]{:S(2)}) %collective-permute-start) | collective-permute-done | bytes 3145760 | tf_op jit(solution)/shard_map/ppermute | solution.py:141
  33.7 19.6 %shard_map.101 = bf16[64,128,512]{2,1,0:T(8,128)(2,1)} custom-call(s32[64]{0:T(128)} %get-tuple-element.13.src_ref, s32[64]{0:T(128)} %slice_bitcast_fusion.2.widx_ref, s32[1]{0:T(128)} %bitcast.9.col_ref, bf16[3072,512]{1,0:T(8,128)(2,1)} %mine_ref.3, bf16[3072,512]{1,0:T(8,128)(2,1)} %collective-permute-done.other_ref, bf16[16,1024,512]{2,1,0:T(8,128)(2,1)} %w_ref.4), custom_call_target="tpu_custom_call" | custom-call | flops 8589934592 | bytes 31457280 | tf_op jit(solution)/shard_map/pallas_call | solution.py:50
  53.3 94.2 %all-to-all-done = bf16[64,128,512]{2,1,0:T(8,128)(2,1)} async-done(((bf16[64,128,512]{2,1,0:T(8,128)(2,1)}), bf16[64,128,512]{2,1,0:T(8,128)(2,1)}, u32[]{:S(2)}, u32[]{:S(2)}) %all-to-all-start) | async-done | bytes 8388640 | tf_op jit(solution)/shard_map/all_to_all | solution.py:183
  147.5 8.9 %all-to-all-start.1 = ((bf16[64,128,512]{2,1,0:T(8,128)(2,1)}), bf16[64,128,512]{2,1,0:T(8,128)(2,1)}, u32[]{:S(2)}, u32[]{:S(2)}) async-start(bf16[64,128,512]{2,1,0:T(8,128)(2,1)} %shard_map.101), calls=%async_computation.1 | async-start | bytes 16777216 | tf_op jit(solution)/shard_map/all_to_all | solution.py:189
  156.6 0.1 add.11
  157.0 5.7 %reduce_sum.11 = s32[64,2,128]{2,1,0:T(2,128)S(1)} reduce(s32[1,64,2,128,128]{4,3,2,1,0:T(8,128)} %param.19, s32[]{:T(128)} %constant.3.clone.1), dimensions={0,4}, to_apply=%region_0.0 | reduce | flops 2080768 | bytes 8454148 | tf_op jit(solution)/shard_map/reduce_sum | solution.py:168
  162.6 0.4 fusion.1
  163.1 0.3 fusion.2
  163.4 2.7 copy.23.inv_ref
  166.2 2.6 copy.24.inv_ref
  168.9 0.5 slice_bitcast_fusion.widx_ref
  169.4 0.6 slice_bitcast_fusion.1
  170.0 6.3 %fusion.adj_ref = bf16[64,2,128,128]{3,2,1,0:T(8,128)(2,1)} fusion(s32[1,64,2,128,128]{4,3,2,1,0:T(8,128)} %param.19, s32[64,2]{1,0:T(8,128)S(1)} %copy.20), kind=kLoop, calls=%fused_computation.1 | loop fusion | flops 4194304 | bytes 12583424 | tf_op jit(solution)/shard_map/convert_element_type | solution.py:212
  176.3 0.5 iota.11.src_ref
  176.8 9.7 %shard_map.103 = f32[24,128,512]{2,1,0:T(8,128)} custom-call(s32[24]{0:T(128)} %iota.11.src_ref, s32[24]{0:T(128)} %widx_ref.1, s32[1]{0:T(128)} %bitcast.9.col_ref, bf16[3072,512]{1,0:T(8,128)(2,1)} %mine_ref.3, bf16[3072,512]{1,0:T(8,128)(2,1)} %collective-permute-done.other_ref, bf16[3,1024,512]{2,1,0:T(8,128)(2,1)} %w_ref.5), custom_call_target="tpu_custom_call" | custom-call | flops 3221225472 | bytes 15728640 | tf_op jit(solution)/shard_map/pallas_call | solution.py:50
  186.5 0.6 iota.10.src_ref
  187.1 22.5 %shard_map.102.msg_ref = bf16[64,128,512]{2,1,0:T(8,128)(2,1)} custom-call(s32[64]{0:T(128)} %iota.10.src_ref, s32[64]{0:T(128)} %slice_bitcast_fusion.widx_ref, s32[1]{0:T(128)} %bitcast.9.col_ref, bf16[8192,512]{1,0:T(8,128)(2,1)} %bitcast.16.mine_ref, bf16[8192,512]{1,0:T(8,128)(2,1)} %bitcast.17.other_ref, bf16[16,1024,512]{2,1,0:T(8,128)(2,1)} %w_ref.4), custom_call_target="tpu_custom_call" | custom-call | flops 8589934592 | bytes 41943040 | tf_op jit(solution)/shard_map/pallas_call | solution.py:50
  209.5 12.4 %shard_map.104.acc_ref = f32[3072,512]{1,0:T(8,128)} custom-call(s32[64]{0:T(128)} %get-tuple-element.11.tb_ref, bf16[64,2,128,128]{3,2,1,0:T(8,128)(2,1)} %fusion.adj_ref, bf16[64,128,512]{2,1,0:T(8,128)(2,1)} %shard_map.102.msg_ref, f32[64,128,1]{2,1,0:T(8,128)} %copy.23.inv_ref, f32[3072,512]{1,0:T(8,128)} %bitcast.30), custom_call_target="tpu_custom_call" | custom-call | flops 1073741824 | bytes 23101440 | tf_op jit(solution)/shard_map/pallas_call | solution.py:129
  221.9 60.5 %all-to-all-done.1.msg_ref = bf16[64,128,512]{2,1,0:T(8,128)(2,1)} async-done(((bf16[64,128,512]{2,1,0:T(8,128)(2,1)}), bf16[64,128,512]{2,1,0:T(8,128)(2,1)}, u32[]{:S(2)}, u32[]{:S(2)}) %all-to-all-start.1) | async-done | bytes 8388640 | tf_op jit(solution)/shard_map/all_to_all | solution.py:189
  282.4 11.3 %shard_map.105 = bf16[3072,512]{1,0:T(8,128)(2,1)} custom-call(s32[64]{0:T(128)} %get-tuple-element.12.tb_ref, bf16[64,2,128,128]{3,2,1,0:T(8,128)(2,1)} %fusion.adj_ref, bf16[64,128,512]{2,1,0:T(8,128)(2,1)} %all-to-all-done.1.msg_ref, f32[64,128,1]{2,1,0:T(8,128)} %copy.24.inv_ref, f32[3072,512]{1,0:T(8,128)} %shard_map.104.acc_ref), custom_call_target="tpu_custom_call" | custom-call | flops 1073741824 | bytes 19955712 | tf_op jit(solution)/shard_map/pallas_call | solution.py:129
  (19 shorter events, 0.6 us)
Async XLA Ops:
  15.9 12.0 %copy-start = (bf16[3072,512]{1,0:T(8,128)(2,1)S(1)}, bf16[3072,512]{1,0:T(8,128)(2,1)}, u32[]{:S(2)}) copy-start(bf16[3072,512]{1,0:T(8,128)(2,1)} %mine_ref.3) | copy-start | bytes 9437188
  15.9 12.1 %copy-start.4 = (s32[1,64,2]{1,2,0:T(2,128)S(1)}, s32[1,64,2]{1,2,0:T(2,128)}, u32[]{:S(2)}) copy-start(s32[1,64,2]{1,2,0:T(2,128)} %param.14) | copy-start | bytes 1540
  15.9 131.6 %all-to-all-start = ((bf16[64,128,512]{2,1,0:T(8,128)(2,1)}), bf16[64,128,512]{2,1,0:T(8,128)(2,1)}, u32[]{:S(2)}, u32[]{:S(2)}) async-start(bf16[64,128,512]{2,1,0:T(8,128)(2,1)} %shard_map.100), calls=%async_computation | async-start | bytes 16777216 | tf_op jit(solution)/shard_map/all_to_all | solution.py:183
  27.9 5.9 %collective-permute-start = (bf16[3072,512]{1,0:T(8,128)(2,1)S(1)}, bf16[3072,512]{1,0:T(8,128)(2,1)}, u32[]{:S(2)}, u32[]{:S(2)}) collective-permute-start(bf16[3072,512]{1,0:T(8,128)(2,1)S(1)} %copy-done), channel_id=1, source_target_pairs={{0,1},{1,0},{2,3},{3,2},{4,5},{5,4},{6,7},{7,6},{8,9},{9,8},{10,11... | collective-permute-start | bytes 9437192 | tf_op jit(solution)/shard_map/ppermute | solution.py:141
  53.3 103.2 %copy-start.2 = (s32[1,64,2]{1,2,0:T(2,128)S(1)}, s32[1,64,2]{1,2,0:T(2,128)}, u32[]{:S(2)}) copy-start(s32[1,64,2]{1,2,0:T(2,128)} %param.17) | copy-start | bytes 1540
  53.3 103.2 %copy-start.3 = (s32[1,64,2]{1,2,0:T(2,128)S(1)}, s32[1,64,2]{1,2,0:T(2,128)}, u32[]{:S(2)}) copy-start(s32[1,64,2]{1,2,0:T(2,128)} %param.16) | copy-start | bytes 1540
  53.3 103.4 %copy-start.1 = (s32[1,64,2]{1,2,0:T(2,128)S(1)}, s32[1,64,2]{1,2,0:T(2,128)}, u32[]{:S(2)}) copy-start(s32[1,64,2]{1,2,0:T(2,128)} %param.18) | copy-start | bytes 1540
  147.5 39.0 %collective-permute-start.1 = (bf16[64,128,512]{2,1,0:T(8,128)(2,1)}, bf16[64,128,512]{2,1,0:T(8,128)(2,1)}, u32[]{:S(2)}, u32[]{:S(2)}) collective-permute-start(bf16[64,128,512]{2,1,0:T(8,128)(2,1)} %all-to-all-done), channel_id=1, source_target_pairs={{0,1},{1,0},{2,3},{3,2},{4,5},{5,4},{6,7},{7,6},{8,9},{9,8},{10,11... | collective-permute-start | bytes 25165832 | tf_op jit(solution)/shard_map/ppermute | solution.py:141
  147.5 134.9 %all-to-all-start.1 = ((bf16[64,128,512]{2,1,0:T(8,128)(2,1)}), bf16[64,128,512]{2,1,0:T(8,128)(2,1)}, u32[]{:S(2)}, u32[]{:S(2)}) async-start(bf16[64,128,512]{2,1,0:T(8,128)(2,1)} %shard_map.101), calls=%async_computation.1 | async-start | bytes 16777216 | tf_op jit(solution)/shard_map/all_to_all | solution.py:189

commit v9 on v7

--- a/solution.py
+++ b/solution.py
@@ -91,7 +91,12 @@
     block_rows = msg_ref.shape[1]
     for j in range(group):
         slot = step * group + j
-        term = jnp.dot(adj_ref[j], msg_ref[j], preferred_element_type=jnp.float32) * inv_ref[j]
+        scale = jnp.transpose(jnp.broadcast_to(inv_ref[j], (block_rows, block_rows)))
+        term = jnp.dot(adj_ref[j], msg_ref[j], preferred_element_type=jnp.float32)
+        lanes = scale.shape[1]
+        term = jnp.concatenate(
+            [term[:, c : c + lanes] * scale for c in range(0, term.shape[1], lanes)], axis=1
+        )
         rows = pl.ds(pl.multiple_of(tb_ref[slot] * block_rows, block_rows), block_rows)
         acc_ref[rows, :] += term
 
@@ -110,7 +115,7 @@
         in_specs=[
             pl.BlockSpec((group, None, block_rows, block_rows), lambda i, t: (i, k, 0, 0)),
             pl.BlockSpec((group, block_rows, n_dim), lambda i, t: (i, 0, 0)),
-            pl.BlockSpec((group, block_rows, 1), lambda i, t: (i, 0, 0)),
+            pl.BlockSpec((group, 1, block_rows), lambda i, t: (i, 0, 0)),
             pl.BlockSpec((rows, n_dim), lambda i, t: (0, 0), pipeline_mode=pl.Buffered(1)),
         ],
         out_specs=pl.BlockSpec((rows, n_dim), lambda i, t: (0, 0)),
@@ -168,7 +173,7 @@
     )
     inverse = 1.0 / jnp.maximum(degree, 1.0)
     scale = jnp.dot(table, inverse, precision=lax.Precision.HIGHEST)
-    scale = scale.reshape(partitions, capacity, block_rows, 1)
+    scale = scale.reshape(partitions, capacity, 1, block_rows)
 
     src_blocks = source_block.reshape(partitions, capacity)
     src_rels = source_relation.reshape(partitions, capacity)

time: 289 us -> 288 us (level)
  waiting for transfers between devices: 160 us -> 166 us
  local copies, waits for them, and re-layouts: 10.1 us -> 5.29 us
    all_to_all x1, waiting for transfers between devices: 60.5 us -> 66.2 us  [on_device(): lax.all_to_all(msgs, 'dom', split_axis=0, concat_axis=0, tiled=True)]
    squeeze x2 -> x1, local copies, waits for them, and re-layouts: 5.33 us -> 0.67 us  [on_device(): scale[:, k]]
  transfers between devices with their start and end apart: 4 -> 4, of which waited for: 3 -> 3; matrix products, arithmetic and copies ran while one was open for 7% -> 6% of each run, Pallas kernels for 22% -> 22%
where the time goes in v9:
time: 288 us; the launch traced here: 286 us
  waiting for transfers between devices  166 us (58%)
  Pallas kernels  80.9 us (28%)
  starting transfers between devices  20.9 us (7%)
  other arithmetic  12 us (4%)
  local copies, waits for them, and re-layouts  5.29 us (2%)
    all_to_all x1, waiting for transfers between devices, on_device(): lax.all_to_all(raw, 'dom', split_axis=0, concat_axis=0, tiled=True)  94.2 us
    all_to_all x1, waiting for transfers between devices, on_device(): lax.all_to_all(msgs, 'dom', split_axis=0, concat_axis=0, tiled=True)  66.2 us
    pallas_call x3, Pallas kernels, _block_matmul(): pl.pallas_call(functools.partial(_bmm_kernel, group), grid_spec=grid_spec...  51.7 us
    pallas_call x2, Pallas kernels, _aggregate(): pl.pallas_call(functools.partial(_agg_kernel, group, final), grid_spec=gr...  21.9 us
    all_to_all x1, starting transfers between devices, on_device(): lax.all_to_all(raw, 'dom', split_axis=0, concat_axis=0, tiled=True)  11.9 us
    all_to_all x1, starting transfers between devices, on_device(): lax.all_to_all(msgs, 'dom', split_axis=0, concat_axis=0, tiled=True)  8.91 us
    pallas_call x1, Pallas kernels, _pick_blocks(): pl.pallas_call(functools.partial(_pick_kernel, group), grid_spec=grid_spe...  7.23 us
    convert_element_type x1, other arithmetic, on_device(): adjacency = (tiles4 * live2[:, :, None, None]).astype(jnp.bfloat16)  6.35 us
  transfers between devices with their start and end apart: 4, of which 3 were waited for; matrix products, arithmetic and copies ran while one was open for 6% of the time, Pallas kernels for 22%

profile of v9, /device:TPU:4, one launch (start us, length us, event | category | flops | bytes accessed | tf_op | source)
XLA Modules:
  0.0 285.5 jit_solution(7575653917690190447)
XLA Ops:
  0.0 1.3 slice_bitcast_fusion.5
  1.3 7.2 %shard_map.100 = bf16[64,128,512]{2,1,0:T(8,128)(2,1)} custom-call(s32[64]{0:T(128)} %get-tuple-element.14.src_ref, bf16[3072,512]{1,0:T(8,128)(2,1)} %mine_ref.3), custom_call_target="tpu_custom_call" | custom-call | bytes 11534336 | tf_op jit(solution)/shard_map/pallas_call | solution.py:77
  8.6 11.9 %all-to-all-start = ((bf16[64,128,512]{2,1,0:T(8,128)(2,1)}), bf16[64,128,512]{2,1,0:T(8,128)(2,1)}, u32[]{:S(2)}, u32[]{:S(2)}) async-start(bf16[64,128,512]{2,1,0:T(8,128)(2,1)} %shard_map.100), calls=%async_computation | async-start | bytes 16777216 | tf_op jit(solution)/shard_map/all_to_all | solution.py:183
  20.6 0.6 slice_bitcast_fusion.4.widx_ref
  21.2 5.2 %collective-permute-done.other_ref = bf16[3072,512]{1,0:T(8,128)(2,1)} collective-permute-done((bf16[3072,512]{1,0:T(8,128)(2,1)S(1)}, bf16[3072,512]{1,0:T(8,128)(2,1)}, u32[]{:S(2)}, u32[]{:S(2)}) %collective-permute-start) | collective-permute-done | bytes 3145760 | tf_op jit(solution)/shard_map/ppermute | solution.py:141
  26.4 19.6 %shard_map.101 = bf16[64,128,512]{2,1,0:T(8,128)(2,1)} custom-call(s32[64]{0:T(128)} %get-tuple-element.13.src_ref, s32[64]{0:T(128)} %slice_bitcast_fusion.4.widx_ref, s32[1]{0:T(128)} %bitcast.9.col_ref, bf16[3072,512]{1,0:T(8,128)(2,1)} %mine_ref.3, bf16[3072,512]{1,0:T(8,128)(2,1)} %collective-permute-done.other_ref, bf16[16,1024,512]{2,1,0:T(8,128)(2,1)} %w_ref.4), custom_call_target="tpu_custom_call" | custom-call | flops 8589934592 | bytes 31457280 | tf_op jit(solution)/shard_map/pallas_call | solution.py:50
  46.0 94.2 %all-to-all-done = bf16[64,128,512]{2,1,0:T(8,128)(2,1)} async-done(((bf16[64,128,512]{2,1,0:T(8,128)(2,1)}), bf16[64,128,512]{2,1,0:T(8,128)(2,1)}, u32[]{:S(2)}, u32[]{:S(2)}) %all-to-all-start) | async-done | bytes 8388640 | tf_op jit(solution)/shard_map/all_to_all | solution.py:183
  140.2 8.9 %all-to-all-start.1 = ((bf16[64,128,512]{2,1,0:T(8,128)(2,1)}), bf16[64,128,512]{2,1,0:T(8,128)(2,1)}, u32[]{:S(2)}, u32[]{:S(2)}) async-start(bf16[64,128,512]{2,1,0:T(8,128)(2,1)} %shard_map.101), calls=%async_computation.1 | async-start | bytes 16777216 | tf_op jit(solution)/shard_map/all_to_all | solution.py:189
  149.2 0.1 add.11
  149.5 0.1 mul.37
  149.7 5.7 %reduce_sum.11 = s32[64,2,128]{2,1,0:T(2,128)S(1)} reduce(s32[1,64,2,128,128]{4,3,2,1,0:T(8,128)} %param.19, s32[]{:T(128)} %constant.3.clone.1), dimensions={0,4}, to_apply=%region_0.0 | reduce | flops 2080768 | bytes 8454148 | tf_op jit(solution)/shard_map/reduce_sum | solution.py:168
  155.4 0.5 slice_bitcast_fusion.2.widx_ref
  155.9 0.6 slice_bitcast_fusion.3
  156.5 0.4 fusion.1
  156.9 0.3 fusion.2
  157.2 0.7 slice_bitcast_fusion
  157.9 6.4 %fusion.adj_ref = bf16[64,2,128,128]{3,2,1,0:T(8,128)(2,1)} fusion(s32[1,64,2,128,128]{4,3,2,1,0:T(8,128)} %param.19, s32[64,2]{1,0:T(8,128)S(1)} %copy.15), kind=kLoop, calls=%fused_computation.1 | loop fusion | flops 4194304 | bytes 12583424 | tf_op jit(solution)/shard_map/convert_element_type | solution.py:212
  164.2 0.5 iota.11.src_ref
  164.7 9.7 %shard_map.103 = f32[24,128,512]{2,1,0:T(8,128)} custom-call(s32[24]{0:T(128)} %iota.11.src_ref, s32[24]{0:T(128)} %widx_ref.1, s32[1]{0:T(128)} %bitcast.9.col_ref, bf16[3072,512]{1,0:T(8,128)(2,1)} %mine_ref.3, bf16[3072,512]{1,0:T(8,128)(2,1)} %collective-permute-done.other_ref, bf16[3,1024,512]{2,1,0:T(8,128)(2,1)} %w_ref.5), custom_call_target="tpu_custom_call" | custom-call | flops 3221225472 | bytes 15728640 | tf_op jit(solution)/shard_map/pallas_call | solution.py:50
  174.4 0.5 iota.10.src_ref
  174.9 22.5 %shard_map.102.msg_ref = bf16[64,128,512]{2,1,0:T(8,128)(2,1)} custom-call(s32[64]{0:T(128)} %iota.10.src_ref, s32[64]{0:T(128)} %slice_bitcast_fusion.2.widx_ref, s32[1]{0:T(128)} %bitcast.9.col_ref, bf16[8192,512]{1,0:T(8,128)(2,1)} %bitcast.16.mine_ref, bf16[8192,512]{1,0:T(8,128)(2,1)} %bitcast.17.other_ref, bf16[16,1024,512]{2,1,0:T(8,128)(2,1)} %w_ref.4), custom_call_target="tpu_custom_call" | custom-call | flops 8589934592 | bytes 41943040 | tf_op jit(solution)/shard_map/pallas_call | solution.py:50
  197.4 11.5 %shard_map.104.acc_ref = f32[3072,512]{1,0:T(8,128)} custom-call(s32[64]{0:T(128)} %get-tuple-element.11.tb_ref, bf16[64,2,128,128]{3,2,1,0:T(8,128)(2,1)} %fusion.adj_ref, bf16[64,128,512]{2,1,0:T(8,128)(2,1)} %shard_map.102.msg_ref, f32[64,1,128]{2,1,0:T(1,128)} %get-tuple-element.9.inv_ref, f32[3072,512]{1,0:T(8,128)} %bitcast.36), custom_call_target="tpu_custom_call" | custom-call | flops 1073741824 | bytes 23101440 | tf_op jit(solution)/shard_map/pallas_call | solution.py:129
  208.9 66.2 %all-to-all-done.1.msg_ref = bf16[64,128,512]{2,1,0:T(8,128)(2,1)} async-done(((bf16[64,128,512]{2,1,0:T(8,128)(2,1)}), bf16[64,128,512]{2,1,0:T(8,128)(2,1)}, u32[]{:S(2)}, u32[]{:S(2)}) %all-to-all-start.1) | async-done | bytes 8388640 | tf_op jit(solution)/shard_map/all_to_all | solution.py:189
  275.1 10.4 %shard_map.105 = bf16[3072,512]{1,0:T(8,128)(2,1)} custom-call(s32[64]{0:T(128)} %get-tuple-element.12.tb_ref, bf16[64,2,128,128]{3,2,1,0:T(8,128)(2,1)} %fusion.adj_ref, bf16[64,128,512]{2,1,0:T(8,128)(2,1)} %all-to-all-done.1.msg_ref, f32[64,1,128]{2,1,0:T(1,128)} %get-tuple-element.10.inv_ref, f32[3072,512]{1,0:T(8,128)} %shard_map.104.acc_ref), custom_call_target="tpu_custom_call" | custom-call | flops 1073741824 | bytes 19955712 | tf_op jit(solution)/shard_map/pallas_call | solution.py:129
  (17 shorter events, 0.4 us)
Async XLA Ops:
  8.6 11.9 %copy-start = (bf16[3072,512]{1,0:T(8,128)(2,1)S(1)}, bf16[3072,512]{1,0:T(8,128)(2,1)}, u32[]{:S(2)}) copy-start(bf16[3072,512]{1,0:T(8,128)(2,1)} %mine_ref.3) | copy-start | bytes 9437188
  8.6 12.0 %copy-start.4 = (s32[1,64,2]{1,2,0:T(2,128)S(1)}, s32[1,64,2]{1,2,0:T(2,128)}, u32[]{:S(2)}) copy-start(s32[1,64,2]{1,2,0:T(2,128)} %param.14) | copy-start | bytes 1540
  8.6 131.6 %all-to-all-start = ((bf16[64,128,512]{2,1,0:T(8,128)(2,1)}), bf16[64,128,512]{2,1,0:T(8,128)(2,1)}, u32[]{:S(2)}, u32[]{:S(2)}) async-start(bf16[64,128,512]{2,1,0:T(8,128)(2,1)} %shard_map.100), calls=%async_computation | async-start | bytes 16777216 | tf_op jit(solution)/shard_map/all_to_all | solution.py:183
  20.5 5.9 %collective-permute-start = (bf16[3072,512]{1,0:T(8,128)(2,1)S(1)}, bf16[3072,512]{1,0:T(8,128)(2,1)}, u32[]{:S(2)}, u32[]{:S(2)}) collective-permute-start(bf16[3072,512]{1,0:T(8,128)(2,1)S(1)} %copy-done), channel_id=1, source_target_pairs={{0,1},{1,0},{2,3},{3,2},{4,5},{5,4},{6,7},{7,6},{8,9},{9,8},{10,11... | collective-permute-start | bytes 9437192 | tf_op jit(solution)/shard_map/ppermute | solution.py:141
  45.9 103.2 %copy-start.2 = (s32[1,64,2]{1,2,0:T(2,128)S(1)}, s32[1,64,2]{1,2,0:T(2,128)}, u32[]{:S(2)}) copy-start(s32[1,64,2]{1,2,0:T(2,128)} %param.17) | copy-start | bytes 1540
  45.9 103.2 %copy-start.3 = (s32[1,64,2]{1,2,0:T(2,128)S(1)}, s32[1,64,2]{1,2,0:T(2,128)}, u32[]{:S(2)}) copy-start(s32[1,64,2]{1,2,0:T(2,128)} %param.16) | copy-start | bytes 1540
  46.0 103.4 %copy-start.1 = (s32[1,64,2]{1,2,0:T(2,128)S(1)}, s32[1,64,2]{1,2,0:T(2,128)}, u32[]{:S(2)}) copy-start(s32[1,64,2]{1,2,0:T(2,128)} %param.18) | copy-start | bytes 1540
  140.2 34.2 %collective-permute-start.1 = (bf16[64,128,512]{2,1,0:T(8,128)(2,1)}, bf16[64,128,512]{2,1,0:T(8,128)(2,1)}, u32[]{:S(2)}, u32[]{:S(2)}) collective-permute-start(bf16[64,128,512]{2,1,0:T(8,128)(2,1)} %all-to-all-done), channel_id=1, source_target_pairs={{0,1},{1,0},{2,3},{3,2},{4,5},{5,4},{6,7},{7,6},{8,9},{9,8},{10,11... | collective-permute-start | bytes 25165832 | tf_op jit(solution)/shard_map/ppermute | solution.py:141
  140.2 134.9 %all-to-all-start.1 = ((bf16[64,128,512]{2,1,0:T(8,128)(2,1)}), bf16[64,128,512]{2,1,0:T(8,128)(2,1)}, u32[]{:S(2)}, u32[]{:S(2)}) async-start(bf16[64,128,512]{2,1,0:T(8,128)(2,1)} %shard_map.101), calls=%async_computation.1 | async-start | bytes 16777216 | tf_op jit(solution)/shard_map/all_to_all | solution.py:189

commit v10 on v9

--- a/solution.py
+++ b/solution.py
@@ -66,7 +66,7 @@
         o_ref[j] = x_ref[rows, :]
 
 
-def _pick_blocks(x, src, block_rows, group=8):
+def _pick_blocks(x, src, block_rows, group=16):
     steps = src.shape[0]
     grid_spec = pltpu.PrefetchScalarGridSpec(
         num_scalar_prefetch=1,
@@ -105,7 +105,7 @@
         out_ref[...] = acc_ref[...].astype(out_ref.dtype)
 
 
-def _aggregate(acc, adj, msgs, inv, tb, k, final, group=16):
+def _aggregate(acc, adj, msgs, inv, tb, k, final, group=32):
     steps, block_rows, n_dim = msgs.shape
     rows = acc.shape[0]
     out_dtype = jnp.bfloat16 if final else jnp.float32

time: 288 us -> 286 us (level)
  no operation moved by 1% of the time
where the time goes in v10:
time: 286 us; the launch traced here: 284 us
  waiting for transfers between devices  166 us (58%)
  Pallas kernels  78.5 us (27%)
  starting transfers between devices  20.9 us (7%)
  other arithmetic  12 us (4%)
  local copies, waits for them, and re-layouts  5.29 us (2%)
    all_to_all x1, waiting for transfers between devices, on_device(): lax.all_to_all(raw, 'dom', split_axis=0, concat_axis=0, tiled=True)  94.2 us
    all_to_all x1, waiting for transfers between devices, on_device(): lax.all_to_all(msgs, 'dom', split_axis=0, concat_axis=0, tiled=True)  66.8 us
    pallas_call x3, Pallas kernels, _block_matmul(): pl.pallas_call(functools.partial(_bmm_kernel, group), grid_spec=grid_spec...  51.7 us
    pallas_call x2, Pallas kernels, _aggregate(): pl.pallas_call(functools.partial(_agg_kernel, group, final), grid_spec=gr...  20.6 us
    all_to_all x1, starting transfers between devices, on_device(): lax.all_to_all(raw, 'dom', split_axis=0, concat_axis=0, tiled=True)  11.9 us
    all_to_all x1, starting transfers between devices, on_device(): lax.all_to_all(msgs, 'dom', split_axis=0, concat_axis=0, tiled=True)  8.91 us
    convert_element_type x1, other arithmetic, on_device(): adjacency = (tiles4 * live2[:, :, None, None]).astype(jnp.bfloat16)  6.35 us
    pallas_call x1, Pallas kernels, _pick_blocks(): pl.pallas_call(functools.partial(_pick_kernel, group), grid_spec=grid_spe...  6.14 us
  transfers between devices with their start and end apart: 4, of which 3 were waited for; matrix products, arithmetic and copies ran while one was open for 6% of the time, Pallas kernels for 22%

profile of v10, /device:TPU:4, one launch (start us, length us, event | category | flops | bytes accessed | tf_op | source)
XLA Modules:
  0.0 283.8 jit_solution(7795167103978691179)
XLA Ops:
  0.0 1.3 slice_bitcast_fusion.5
  1.3 6.1 %shard_map.100 = bf16[64,128,512]{2,1,0:T(8,128)(2,1)} custom-call(s32[64]{0:T(128)} %get-tuple-element.14.src_ref, bf16[3072,512]{1,0:T(8,128)(2,1)} %mine_ref.3), custom_call_target="tpu_custom_call" | custom-call | bytes 11534336 | tf_op jit(solution)/shard_map/pallas_call | solution.py:77
  7.5 11.9 %all-to-all-start = ((bf16[64,128,512]{2,1,0:T(8,128)(2,1)}), bf16[64,128,512]{2,1,0:T(8,128)(2,1)}, u32[]{:S(2)}, u32[]{:S(2)}) async-start(bf16[64,128,512]{2,1,0:T(8,128)(2,1)} %shard_map.100), calls=%async_computation | async-start | bytes 16777216 | tf_op jit(solution)/shard_map/all_to_all | solution.py:183
  19.5 0.6 slice_bitcast_fusion.4.widx_ref
  20.1 5.2 %collective-permute-done.other_ref = bf16[3072,512]{1,0:T(8,128)(2,1)} collective-permute-done((bf16[3072,512]{1,0:T(8,128)(2,1)S(1)}, bf16[3072,512]{1,0:T(8,128)(2,1)}, u32[]{:S(2)}, u32[]{:S(2)}) %collective-permute-start) | collective-permute-done | bytes 3145760 | tf_op jit(solution)/shard_map/ppermute | solution.py:141
  25.3 19.6 %shard_map.101 = bf16[64,128,512]{2,1,0:T(8,128)(2,1)} custom-call(s32[64]{0:T(128)} %get-tuple-element.13.src_ref, s32[64]{0:T(128)} %slice_bitcast_fusion.4.widx_ref, s32[1]{0:T(128)} %bitcast.9.col_ref, bf16[3072,512]{1,0:T(8,128)(2,1)} %mine_ref.3, bf16[3072,512]{1,0:T(8,128)(2,1)} %collective-permute-done.other_ref, bf16[16,1024,512]{2,1,0:T(8,128)(2,1)} %w_ref.4), custom_call_target="tpu_custom_call" | custom-call | flops 8589934592 | bytes 31457280 | tf_op jit(solution)/shard_map/pallas_call | solution.py:50
  44.9 94.2 %all-to-all-done = bf16[64,128,512]{2,1,0:T(8,128)(2,1)} async-done(((bf16[64,128,512]{2,1,0:T(8,128)(2,1)}), bf16[64,128,512]{2,1,0:T(8,128)(2,1)}, u32[]{:S(2)}, u32[]{:S(2)}) %all-to-all-start) | async-done | bytes 8388640 | tf_op jit(solution)/shard_map/all_to_all | solution.py:183
  139.1 8.9 %all-to-all-start.1 = ((bf16[64,128,512]{2,1,0:T(8,128)(2,1)}), bf16[64,128,512]{2,1,0:T(8,128)(2,1)}, u32[]{:S(2)}, u32[]{:S(2)}) async-start(bf16[64,128,512]{2,1,0:T(8,128)(2,1)} %shard_map.101), calls=%async_computation.1 | async-start | bytes 16777216 | tf_op jit(solution)/shard_map/all_to_all | solution.py:189
  148.1 0.1 add.11
  148.4 0.1 mul.37
  148.6 5.7 %reduce_sum.11 = s32[64,2,128]{2,1,0:T(2,128)S(1)} reduce(s32[1,64,2,128,128]{4,3,2,1,0:T(8,128)} %param.19, s32[]{:T(128)} %constant.3.clone.1), dimensions={0,4}, to_apply=%region_0.0 | reduce | flops 2080768 | bytes 8454148 | tf_op jit(solution)/shard_map/reduce_sum | solution.py:168
  154.3 0.5 slice_bitcast_fusion.2.widx_ref
  154.8 0.6 slice_bitcast_fusion.3
  155.4 0.4 fusion.1
  155.8 0.3 fusion.2
  156.1 0.7 slice_bitcast_fusion
  156.8 6.4 %fusion.adj_ref = bf16[64,2,128,128]{3,2,1,0:T(8,128)(2,1)} fusion(s32[1,64,2,128,128]{4,3,2,1,0:T(8,128)} %param.19, s32[64,2]{1,0:T(8,128)S(1)} %copy.15), kind=kLoop, calls=%fused_computation.1 | loop fusion | flops 4194304 | bytes 12583424 | tf_op jit(solution)/shard_map/convert_element_type | solution.py:212
  163.1 0.5 iota.11.src_ref
  163.6 9.7 %shard_map.103 = f32[24,128,512]{2,1,0:T(8,128)} custom-call(s32[24]{0:T(128)} %iota.11.src_ref, s32[24]{0:T(128)} %widx_ref.1, s32[1]{0:T(128)} %bitcast.9.col_ref, bf16[3072,512]{1,0:T(8,128)(2,1)} %mine_ref.3, bf16[3072,512]{1,0:T(8,128)(2,1)} %collective-permute-done.other_ref, bf16[3,1024,512]{2,1,0:T(8,128)(2,1)} %w_ref.5), custom_call_target="tpu_custom_call" | custom-call | flops 3221225472 | bytes 15728640 | tf_op jit(solution)/shard_map/pallas_call | solution.py:50
  173.3 0.5 iota.10.src_ref
  173.8 22.5 %shard_map.102.msg_ref = bf16[64,128,512]{2,1,0:T(8,128)(2,1)} custom-call(s32[64]{0:T(128)} %iota.10.src_ref, s32[64]{0:T(128)} %slice_bitcast_fusion.2.widx_ref, s32[1]{0:T(128)} %bitcast.9.col_ref, bf16[8192,512]{1,0:T(8,128)(2,1)} %bitcast.16.mine_ref, bf16[8192,512]{1,0:T(8,128)(2,1)} %bitcast.17.other_ref, bf16[16,1024,512]{2,1,0:T(8,128)(2,1)} %w_ref.4), custom_call_target="tpu_custom_call" | custom-call | flops 8589934592 | bytes 41943040 | tf_op jit(solution)/shard_map/pallas_call | solution.py:50
  196.3 10.9 %shard_map.104.acc_ref = f32[3072,512]{1,0:T(8,128)} custom-call(s32[64]{0:T(128)} %get-tuple-element.11.tb_ref, bf16[64,2,128,128]{3,2,1,0:T(8,128)(2,1)} %fusion.adj_ref, bf16[64,128,512]{2,1,0:T(8,128)(2,1)} %shard_map.102.msg_ref, f32[64,1,128]{2,1,0:T(1,128)} %get-tuple-element.9.inv_ref, f32[3072,512]{1,0:T(8,128)} %bitcast.36), custom_call_target="tpu_custom_call" | custom-call | flops 1073741824 | bytes 23101440 | tf_op jit(solution)/shard_map/pallas_call | solution.py:129
  207.2 66.8 %all-to-all-done.1.msg_ref = bf16[64,128,512]{2,1,0:T(8,128)(2,1)} async-done(((bf16[64,128,512]{2,1,0:T(8,128)(2,1)}), bf16[64,128,512]{2,1,0:T(8,128)(2,1)}, u32[]{:S(2)}, u32[]{:S(2)}) %all-to-all-start.1) | async-done | bytes 8388640 | tf_op jit(solution)/shard_map/all_to_all | solution.py:189
  274.0 9.8 %shard_map.105 = bf16[3072,512]{1,0:T(8,128)(2,1)} custom-call(s32[64]{0:T(128)} %get-tuple-element.12.tb_ref, bf16[64,2,128,128]{3,2,1,0:T(8,128)(2,1)} %fusion.adj_ref, bf16[64,128,512]{2,1,0:T(8,128)(2,1)} %all-to-all-done.1.msg_ref, f32[64,1,128]{2,1,0:T(1,128)} %get-tuple-element.10.inv_ref, f32[3072,512]{1,0:T(8,128)} %shard_map.104.acc_ref), custom_call_target="tpu_custom_call" | custom-call | flops 1073741824 | bytes 19955712 | tf_op jit(solution)/shard_map/pallas_call | solution.py:129
  (17 shorter events, 0.4 us)
Async XLA Ops:
  7.5 11.9 %copy-start = (bf16[3072,512]{1,0:T(8,128)(2,1)S(1)}, bf16[3072,512]{1,0:T(8,128)(2,1)}, u32[]{:S(2)}) copy-start(bf16[3072,512]{1,0:T(8,128)(2,1)} %mine_ref.3) | copy-start | bytes 9437188
  7.5 12.0 %copy-start.4 = (s32[1,64,2]{1,2,0:T(2,128)S(1)}, s32[1,64,2]{1,2,0:T(2,128)}, u32[]{:S(2)}) copy-start(s32[1,64,2]{1,2,0:T(2,128)} %param.14) | copy-start | bytes 1540
  7.5 131.6 %all-to-all-start = ((bf16[64,128,512]{2,1,0:T(8,128)(2,1)}), bf16[64,128,512]{2,1,0:T(8,128)(2,1)}, u32[]{:S(2)}, u32[]{:S(2)}) async-start(bf16[64,128,512]{2,1,0:T(8,128)(2,1)} %shard_map.100), calls=%async_computation | async-start | bytes 16777216 | tf_op jit(solution)/shard_map/all_to_all | solution.py:183
  19.4 5.9 %collective-permute-start = (bf16[3072,512]{1,0:T(8,128)(2,1)S(1)}, bf16[3072,512]{1,0:T(8,128)(2,1)}, u32[]{:S(2)}, u32[]{:S(2)}) collective-permute-start(bf16[3072,512]{1,0:T(8,128)(2,1)S(1)} %copy-done), channel_id=1, source_target_pairs={{0,1},{1,0},{2,3},{3,2},{4,5},{5,4},{6,7},{7,6},{8,9},{9,8},{10,11... | collective-permute-start | bytes 9437192 | tf_op jit(solution)/shard_map/ppermute | solution.py:141
  44.9 103.2 %copy-start.2 = (s32[1,64,2]{1,2,0:T(2,128)S(1)}, s32[1,64,2]{1,2,0:T(2,128)}, u32[]{:S(2)}) copy-start(s32[1,64,2]{1,2,0:T(2,128)} %param.17) | copy-start | bytes 1540
  44.9 103.2 %copy-start.3 = (s32[1,64,2]{1,2,0:T(2,128)S(1)}, s32[1,64,2]{1,2,0:T(2,128)}, u32[]{:S(2)}) copy-start(s32[1,64,2]{1,2,0:T(2,128)} %param.16) | copy-start | bytes 1540
  44.9 103.4 %copy-start.1 = (s32[1,64,2]{1,2,0:T(2,128)S(1)}, s32[1,64,2]{1,2,0:T(2,128)}, u32[]{:S(2)}) copy-start(s32[1,64,2]{1,2,0:T(2,128)} %param.18) | copy-start | bytes 1540
  139.1 34.2 %collective-permute-start.1 = (bf16[64,128,512]{2,1,0:T(8,128)(2,1)}, bf16[64,128,512]{2,1,0:T(8,128)(2,1)}, u32[]{:S(2)}, u32[]{:S(2)}) collective-permute-start(bf16[64,128,512]{2,1,0:T(8,128)(2,1)} %all-to-all-done), channel_id=1, source_target_pairs={{0,1},{1,0},{2,3},{3,2},{4,5},{5,4},{6,7},{7,6},{8,9},{9,8},{10,11... | collective-permute-start | bytes 25165832 | tf_op jit(solution)/shard_map/ppermute | solution.py:141
  139.1 134.9 %all-to-all-start.1 = ((bf16[64,128,512]{2,1,0:T(8,128)(2,1)}), bf16[64,128,512]{2,1,0:T(8,128)(2,1)}, u32[]{:S(2)}, u32[]{:S(2)}) async-start(bf16[64,128,512]{2,1,0:T(8,128)(2,1)} %shard_map.101), calls=%async_computation.1 | async-start | bytes 16777216 | tf_op jit(solution)/shard_map/all_to_all | solution.py:189

commit v11 on v10

--- a/solution.py
+++ b/solution.py
@@ -66,8 +66,7 @@
         o_ref[j] = x_ref[rows, :]
 
 
-def _pick_blocks(x, src, block_rows, group=16):
-    steps = src.shape[0]
+def _pick_blocks(x, src, steps, block_rows, group=16):
     grid_spec = pltpu.PrefetchScalarGridSpec(
         num_scalar_prefetch=1,
         grid=(steps // group,),
@@ -179,7 +178,7 @@
     src_rels = source_relation.reshape(partitions, capacity)
     dst_blocks = target_block.reshape(partitions, capacity)
 
-    raw = _pick_blocks(features, src_blocks[:, 0], block_rows)
+    raw = _pick_blocks(features, jnp.transpose(src_blocks).reshape(slots), partitions, block_rows)
     arrived = [lax.all_to_all(raw, "dom", split_axis=0, concat_axis=0, tiled=True)]
     for k in range(1, capacity):
         msgs = _block_matmul(

time: 286 us -> 286 us (level)
  no operation moved by 1% of the time
where the time goes in v11:
time: 286 us; the launch traced here: 284 us
  waiting for transfers between devices  166 us (58%)
  Pallas kernels  78.5 us (27%)
  starting transfers between devices  20.9 us (7%)
  other arithmetic  12 us (4%)
  local copies, waits for them, and re-layouts  5.26 us (2%)
    all_to_all x1, waiting for transfers between devices, on_device(): lax.all_to_all(raw, 'dom', split_axis=0, concat_axis=0, tiled=True)  94.2 us
    all_to_all x1, waiting for transfers between devices, on_device(): lax.all_to_all(msgs, 'dom', split_axis=0, concat_axis=0, tiled=True)  66.7 us
    pallas_call x3, Pallas kernels, _block_matmul(): pl.pallas_call(functools.partial(_bmm_kernel, group), grid_spec=grid_spec...  51.7 us
    pallas_call x2, Pallas kernels, _aggregate(): pl.pallas_call(functools.partial(_agg_kernel, group, final), grid_spec=gr...  20.6 us
    all_to_all x1, starting transfers between devices, on_device(): lax.all_to_all(raw, 'dom', split_axis=0, concat_axis=0, tiled=True)  11.9 us
    all_to_all x1, starting transfers between devices, on_device(): lax.all_to_all(msgs, 'dom', split_axis=0, concat_axis=0, tiled=True)  8.91 us
    convert_element_type x1, other arithmetic, on_device(): adjacency = (tiles4 * live2[:, :, None, None]).astype(jnp.bfloat16)  6.35 us
    pallas_call x1, Pallas kernels, _pick_blocks(): pl.pallas_call(functools.partial(_pick_kernel, group), grid_spec=grid_spe...  6.13 us
  transfers between devices with their start and end apart: 4, of which 3 were waited for; matrix products, arithmetic and copies ran while one was open for 6% of the time, Pallas kernels for 22%

profile of v11, /device:TPU:4, one launch (start us, length us, event | category | flops | bytes accessed | tf_op | source)
XLA Modules:
  0.0 283.7 jit_solution(9410403477166599852)
XLA Ops:
  0.0 1.3 reshape.59.src_ref
  1.3 6.1 %shard_map.100 = bf16[64,128,512]{2,1,0:T(8,128)(2,1)} custom-call(s32[128]{0:T(128)} %reshape.59.src_ref, bf16[3072,512]{1,0:T(8,128)(2,1)} %mine_ref.3), custom_call_target="tpu_custom_call" | custom-call | bytes 11534336 | tf_op jit(solution)/shard_map/pallas_call | solution.py:76
  7.4 11.9 %all-to-all-start = ((bf16[64,128,512]{2,1,0:T(8,128)(2,1)}), bf16[64,128,512]{2,1,0:T(8,128)(2,1)}, u32[]{:S(2)}, u32[]{:S(2)}) async-start(bf16[64,128,512]{2,1,0:T(8,128)(2,1)} %shard_map.100), calls=%async_computation | async-start | bytes 16777216 | tf_op jit(solution)/shard_map/all_to_all | solution.py:182
  19.5 0.5 slice_bitcast_fusion.4
  20.0 5.2 %collective-permute-done.other_ref = bf16[3072,512]{1,0:T(8,128)(2,1)} collective-permute-done((bf16[3072,512]{1,0:T(8,128)(2,1)S(1)}, bf16[3072,512]{1,0:T(8,128)(2,1)}, u32[]{:S(2)}, u32[]{:S(2)}) %collective-permute-start) | collective-permute-done | bytes 3145760 | tf_op jit(solution)/shard_map/ppermute | solution.py:140
  25.2 19.6 %shard_map.101 = bf16[64,128,512]{2,1,0:T(8,128)(2,1)} custom-call(s32[64]{0:T(128)} %get-tuple-element.14.src_ref, s32[64]{0:T(128)} %get-tuple-element.13.widx_ref, s32[1]{0:T(128)} %bitcast.9.col_ref, bf16[3072,512]{1,0:T(8,128)(2,1)} %mine_ref.3, bf16[3072,512]{1,0:T(8,128)(2,1)} %collective-permute-done.other_ref, bf16[16,1024,512]{2,1,0:T(8,128)(2,1)} %w_ref.4), custom_call_target="tpu_custom_call" | custom-call | flops 8589934592 | bytes 31457280 | tf_op jit(solution)/shard_map/pallas_call | solution.py:50
  44.8 94.2 %all-to-all-done = bf16[64,128,512]{2,1,0:T(8,128)(2,1)} async-done(((bf16[64,128,512]{2,1,0:T(8,128)(2,1)}), bf16[64,128,512]{2,1,0:T(8,128)(2,1)}, u32[]{:S(2)}, u32[]{:S(2)}) %all-to-all-start) | async-done | bytes 8388640 | tf_op jit(solution)/shard_map/all_to_all | solution.py:182
  139.0 8.9 %all-to-all-start.1 = ((bf16[64,128,512]{2,1,0:T(8,128)(2,1)}), bf16[64,128,512]{2,1,0:T(8,128)(2,1)}, u32[]{:S(2)}, u32[]{:S(2)}) async-start(bf16[64,128,512]{2,1,0:T(8,128)(2,1)} %shard_map.101), calls=%async_computation.1 | async-start | bytes 16777216 | tf_op jit(solution)/shard_map/all_to_all | solution.py:188
  148.1 0.1 add.11
  148.3 0.1 mul.37
  148.6 5.7 %reduce_sum.11 = s32[64,2,128]{2,1,0:T(2,128)S(1)} reduce(s32[1,64,2,128,128]{4,3,2,1,0:T(8,128)} %param.19, s32[]{:T(128)} %constant.3.clone.1), dimensions={0,4}, to_apply=%region_0.0 | reduce | flops 2080768 | bytes 8454148 | tf_op jit(solution)/shard_map/reduce_sum | solution.py:167
  154.2 0.5 slice_bitcast_fusion.2.widx_ref
  154.7 0.6 slice_bitcast_fusion.3
  155.3 0.4 fusion.1
  155.8 0.3 fusion.2
  156.1 0.7 slice_bitcast_fusion
  156.7 6.3 %fusion.adj_ref = bf16[64,2,128,128]{3,2,1,0:T(8,128)(2,1)} fusion(s32[1,64,2,128,128]{4,3,2,1,0:T(8,128)} %param.19, s32[64,2]{1,0:T(8,128)S(1)} %copy.15), kind=kLoop, calls=%fused_computation.1 | loop fusion | flops 4194304 | bytes 12583424 | tf_op jit(solution)/shard_map/convert_element_type | solution.py:211
  163.1 0.5 iota.11.src_ref
  163.6 9.7 %shard_map.103 = f32[24,128,512]{2,1,0:T(8,128)} custom-call(s32[24]{0:T(128)} %iota.11.src_ref, s32[24]{0:T(128)} %widx_ref.1, s32[1]{0:T(128)} %bitcast.9.col_ref, bf16[3072,512]{1,0:T(8,128)(2,1)} %mine_ref.3, bf16[3072,512]{1,0:T(8,128)(2,1)} %collective-permute-done.other_ref, bf16[3,1024,512]{2,1,0:T(8,128)(2,1)} %w_ref.5), custom_call_target="tpu_custom_call" | custom-call | flops 3221225472 | bytes 15728640 | tf_op jit(solution)/shard_map/pallas_call | solution.py:50
  173.3 0.6 iota.10.src_ref
  173.9 22.5 %shard_map.102.msg_ref = bf16[64,128,512]{2,1,0:T(8,128)(2,1)} custom-call(s32[64]{0:T(128)} %iota.10.src_ref, s32[64]{0:T(128)} %slice_bitcast_fusion.2.widx_ref, s32[1]{0:T(128)} %bitcast.9.col_ref, bf16[8192,512]{1,0:T(8,128)(2,1)} %bitcast.16.mine_ref, bf16[8192,512]{1,0:T(8,128)(2,1)} %bitcast.17.other_ref, bf16[16,1024,512]{2,1,0:T(8,128)(2,1)} %w_ref.4), custom_call_target="tpu_custom_call" | custom-call | flops 8589934592 | bytes 41943040 | tf_op jit(solution)/shard_map/pallas_call | solution.py:50
  196.4 10.9 %shard_map.104.acc_ref = f32[3072,512]{1,0:T(8,128)} custom-call(s32[64]{0:T(128)} %get-tuple-element.11.tb_ref, bf16[64,2,128,128]{3,2,1,0:T(8,128)(2,1)} %fusion.adj_ref, bf16[64,128,512]{2,1,0:T(8,128)(2,1)} %shard_map.102.msg_ref, f32[64,1,128]{2,1,0:T(1,128)} %get-tuple-element.9.inv_ref, f32[3072,512]{1,0:T(8,128)} %bitcast.36), custom_call_target="tpu_custom_call" | custom-call | flops 1073741824 | bytes 23101440 | tf_op jit(solution)/shard_map/pallas_call | solution.py:128
  207.2 66.7 %all-to-all-done.1.msg_ref = bf16[64,128,512]{2,1,0:T(8,128)(2,1)} async-done(((bf16[64,128,512]{2,1,0:T(8,128)(2,1)}), bf16[64,128,512]{2,1,0:T(8,128)(2,1)}, u32[]{:S(2)}, u32[]{:S(2)}) %all-to-all-start.1) | async-done | bytes 8388640 | tf_op jit(solution)/shard_map/all_to_all | solution.py:188
  273.9 9.8 %shard_map.105 = bf16[3072,512]{1,0:T(8,128)(2,1)} custom-call(s32[64]{0:T(128)} %get-tuple-element.12.tb_ref, bf16[64,2,128,128]{3,2,1,0:T(8,128)(2,1)} %fusion.adj_ref, bf16[64,128,512]{2,1,0:T(8,128)(2,1)} %all-to-all-done.1.msg_ref, f32[64,1,128]{2,1,0:T(1,128)} %get-tuple-element.10.inv_ref, f32[3072,512]{1,0:T(8,128)} %shard_map.104.acc_ref), custom_call_target="tpu_custom_call" | custom-call | flops 1073741824 | bytes 19955712 | tf_op jit(solution)/shard_map/pallas_call | solution.py:128
  (19 shorter events, 0.4 us)
Async XLA Ops:
  7.4 11.9 %copy-start = (bf16[3072,512]{1,0:T(8,128)(2,1)S(1)}, bf16[3072,512]{1,0:T(8,128)(2,1)}, u32[]{:S(2)}) copy-start(bf16[3072,512]{1,0:T(8,128)(2,1)} %mine_ref.3) | copy-start | bytes 9437188
  7.4 12.0 %copy-start.4 = (s32[1,64,2]{1,2,0:T(2,128)S(1)}, s32[1,64,2]{1,2,0:T(2,128)}, u32[]{:S(2)}) copy-start(s32[1,64,2]{1,2,0:T(2,128)} %param.14) | copy-start | bytes 1540
  7.4 12.0 %copy-start.5 = (s32[1,64,2]{1,2,0:T(2,128)S(1)}, s32[1,64,2]{1,2,0:T(2,128)}, u32[]{:S(2)}) copy-start(s32[1,64,2]{1,2,0:T(2,128)} %param.15) | copy-start | bytes 1540
  7.4 131.6 %all-to-all-start = ((bf16[64,128,512]{2,1,0:T(8,128)(2,1)}), bf16[64,128,512]{2,1,0:T(8,128)(2,1)}, u32[]{:S(2)}, u32[]{:S(2)}) async-start(bf16[64,128,512]{2,1,0:T(8,128)(2,1)} %shard_map.100), calls=%async_computation | async-start | bytes 16777216 | tf_op jit(solution)/shard_map/all_to_all | solution.py:182
  19.3 5.9 %collective-permute-start = (bf16[3072,512]{1,0:T(8,128)(2,1)S(1)}, bf16[3072,512]{1,0:T(8,128)(2,1)}, u32[]{:S(2)}, u32[]{:S(2)}) collective-permute-start(bf16[3072,512]{1,0:T(8,128)(2,1)S(1)} %copy-done), channel_id=1, source_target_pairs={{0,1},{1,0},{2,3},{3,2},{4,5},{5,4},{6,7},{7,6},{8,9},{9,8},{10,11... | collective-permute-start | bytes 9437192 | tf_op jit(solution)/shard_map/ppermute | solution.py:140
  44.8 103.2 %copy-start.2 = (s32[1,64,2]{1,2,0:T(2,128)S(1)}, s32[1,64,2]{1,2,0:T(2,128)}, u32[]{:S(2)}) copy-start(s32[1,64,2]{1,2,0:T(2,128)} %param.17) | copy-start | bytes 1540
  44.8 103.2 %copy-start.3 = (s32[1,64,2]{1,2,0:T(2,128)S(1)}, s32[1,64,2]{1,2,0:T(2,128)}, u32[]{:S(2)}) copy-start(s32[1,64,2]{1,2,0:T(2,128)} %param.16) | copy-start | bytes 1540
  44.8 103.4 %copy-start.1 = (s32[1,64,2]{1,2,0:T(2,128)S(1)}, s32[1,64,2]{1,2,0:T(2,128)}, u32[]{:S(2)}) copy-start(s32[1,64,2]{1,2,0:T(2,128)} %param.18) | copy-start | bytes 1540
  139.0 34.3 %collective-permute-start.1 = (bf16[64,128,512]{2,1,0:T(8,128)(2,1)}, bf16[64,128,512]{2,1,0:T(8,128)(2,1)}, u32[]{:S(2)}, u32[]{:S(2)}) collective-permute-start(bf16[64,128,512]{2,1,0:T(8,128)(2,1)} %all-to-all-done), channel_id=1, source_target_pairs={{0,1},{1,0},{2,3},{3,2},{4,5},{5,4},{6,7},{7,6},{8,9},{9,8},{10,11... | collective-permute-start | bytes 25165832 | tf_op jit(solution)/shard_map/ppermute | solution.py:140
  139.0 134.9 %all-to-all-start.1 = ((bf16[64,128,512]{2,1,0:T(8,128)(2,1)}), bf16[64,128,512]{2,1,0:T(8,128)(2,1)}, u32[]{:S(2)}, u32[]{:S(2)}) async-start(bf16[64,128,512]{2,1,0:T(8,128)(2,1)} %shard_map.101), calls=%async_computation.1 | async-start | bytes 16777216 | tf_op jit(solution)/shard_map/all_to_all | solution.py:188
